TPU v7x, 32 devices: a whole 2x2x4 slice. The times are simulated.
32 devices in a mesh: pipe: 4 (over x, core), tensor: 8 (over z, y).
Axes of the slice: x: 2, y: 2, z: 4, core: 2. Of those that a mesh axis runs over, the one named last changes fastest.
Arguments:
- stretch: bfloat16 [768, 7168], P(('pipe', 'tensor')), may hold values from -6 to 6
- ln_gain: float32 [7168], replicated, may hold values from 0.5 to 1.5
- ln_bias: float32 [7168], replicated, may hold values from -1.75 to 1.75
- qkv_weight: bfloat16 [7168, 12288], P(None, 'tensor'), may hold values from -0.0625 to 0.0625
- qkv_bias: float32 [12288], P('tensor'), may hold values from -1.75 to 1.75
- out_weight: bfloat16 [4096, 7168], P('tensor'), may hold values from -0.09375 to 0.09375
- out_bias: float32 [7168], replicated, may hold values from -1.75 to 1.75
- segment_ids: int32 [768], P('pipe'), may hold values from 0 to 31, never falling along the last dimension, each value on 1 to 96 neighbouring positions
- prefill_cache: bfloat16 [1, 32, 2, 128, 4096], P(None, ('pipe', 'tensor')), may hold values from -6 to 6
- block_dest: int32 [1, 32, 1], P(None, 'pipe'), may hold values from 0 to 3; in each aligned block of 8 rows (0 to 7, 8 to 15, ..., all dimensions but the last counted through in order) at most 3 rows name the same one
Outputs:
- mixed: bfloat16 [768, 7168], P(('pipe', 'tensor'))
- decode_side_cache: bfloat16 [1, 48, 2, 128, 4096], P(None, 'pipe', None, None, 'tensor')
Inputs may be any that keep to these rules, and one draw needn't show every extreme that they name: `block_dest`: among the 8 blocks of one group and one layer no decode group is named more than 3 times, and some decode group exactly 3 times. `segment_ids`: never falling along the tokens; a request spans at most 96 tokens.
All inputs are finite; a program needn't handle non-finite values.
Results may differ from a plain program's by a relative error of at most 0.013.
Values may be sent and summed in bfloat16 or wider, within the bound.
No kernel may reach another device: no remote copies, remote signals or barrier semaphores. Data moves between devices by JAX's collectives and lax.ppermute only.
A program may use at most 128 MiB of HBM per device.

v0:
```python
import jax
import jax.numpy as jnp
from jax import lax
from jax.sharding import PartitionSpec as P

HD = 128


def normalize(x, gain, shift):
    mean = jnp.mean(x, axis=-1, keepdims=True)
    var = jnp.mean((x - mean) * (x - mean), axis=-1, keepdims=True)
    return ((x - mean) * lax.rsqrt(var + 1e-05) * gain + shift).astype(jnp.bfloat16)


def send_decode(per_head_rows, block_dest):
    layers = per_head_rows.shape[0]
    pipe_count = lax.axis_size("pipe")
    row_blocks = per_head_rows.shape[1]
    capacity = 3 * row_blocks // (2 * pipe_count)
    dest = block_dest[:, :, 0]
    onehot = (dest[:, :, None] == jnp.arange(pipe_count, dtype=jnp.int32)[None, None, :]).astype(
        jnp.int32
    )
    earlier_tokens = jnp.cumsum(onehot, axis=1) - onehot
    slot = jnp.sum(earlier_tokens * onehot, axis=-1)
    position = dest * capacity + slot
    targets = jnp.arange(pipe_count * capacity, dtype=jnp.int32)
    placement_index = (position[:, None, :] == targets[None, :, None]).astype(jnp.bfloat16)
    outgoing = jnp.einsum(
        "gud,gdoih->guoih", placement_index, per_head_rows, preferred_element_type=jnp.float32
    ).astype(jnp.bfloat16)
    outgoing = outgoing.reshape((layers, pipe_count, capacity) + per_head_rows.shape[2:])
    arrived = lax.all_to_all(outgoing, "pipe", split_axis=1, concat_axis=1, tiled=True)
    return arrived.reshape((layers, pipe_count * capacity) + per_head_rows.shape[2:])


def local(
    stretch,
    ln_gain,
    ln_bias,
    qkv_weight,
    qkv_bias,
    out_weight,
    out_bias,
    segment_ids,
    prefill_cache,
    block_dest,
):
    per_head_rows = lax.all_to_all(prefill_cache, "tensor", split_axis=4, concat_axis=1, tiled=True)
    hidden = stretch.astype(jnp.float32)
    head_count = qkv_weight.shape[1] // (3 * HD)
    normed = normalize(hidden, ln_gain, ln_bias)
    qkv = (
        jnp.dot(
            lax.all_gather(normed, "tensor", axis=0, tiled=True),
            qkv_weight,
            preferred_element_type=jnp.float32,
        )
        + qkv_bias
    ).astype(jnp.bfloat16)
    group_tokens = qkv.shape[0]
    heads = qkv.reshape(group_tokens, head_count, 3, HD)
    query = heads[:, :, 0]
    keys = heads[:, :, 1]
    value_rows = heads[:, :, 2]
    finished = per_head_rows[0]
    prefix_length = finished.shape[0] * finished.shape[2]
    cached_keys = finished[:, 0].reshape(prefix_length, head_count, HD)
    old_values = finished[:, 1].reshape(prefix_length, head_count, HD)
    scale = HD ** (-0.5)
    own_scores = jnp.einsum("qhd,khd->hqk", query, keys, preferred_element_type=jnp.float32) * scale
    old_scores = (
        jnp.einsum("qhd,khd->hqk", query, cached_keys, preferred_element_type=jnp.float32) * scale
    )
    place = jnp.arange(group_tokens)
    own_visible = (segment_ids[:, None] == segment_ids[None, :]) & (
        place[None, :] <= place[:, None]
    )
    old_visible = (segment_ids == segment_ids[0])[:, None]
    own_scores = jnp.where(own_visible[None], own_scores, -jnp.inf)
    old_scores = jnp.where(old_visible[None], old_scores, -jnp.inf)
    scores = jnp.concatenate([old_scores, own_scores], axis=2)
    weights = jax.nn.softmax(scores, axis=-1).astype(jnp.bfloat16)
    context = jnp.einsum(
        "hqk,khd->qhd",
        weights[:, :, :prefix_length],
        old_values,
        preferred_element_type=jnp.float32,
    )
    context = context + jnp.einsum(
        "hqk,khd->qhd",
        weights[:, :, prefix_length:],
        value_rows,
        preferred_element_type=jnp.float32,
    )
    context = context.astype(jnp.bfloat16).reshape(group_tokens, head_count * HD)
    summed = lax.psum_scatter(
        jnp.dot(context, out_weight, preferred_element_type=jnp.float32).astype(jnp.bfloat16),
        "tensor",
        scatter_dimension=0,
        tiled=True,
    ).astype(jnp.float32)
    mixed = (hidden + summed + out_bias).astype(jnp.bfloat16)
    decode_side_cache = send_decode(per_head_rows, block_dest)
    return (mixed, decode_side_cache)


def solution(mesh):
    return jax.shard_map(
        local,
        mesh=mesh,
        in_specs=(
            P(("pipe", "tensor"), None),
            P(),
            P(),
            P(None, "tensor"),
            P("tensor"),
            P("tensor", None),
            P(),
            P("pipe"),
            P(None, ("pipe", "tensor"), None, None, None),
            P(None, "pipe", None),
        ),
        out_specs=(P(("pipe", "tensor"), None), P(None, "pipe", None, None, "tensor")),
        check_vma=False,
    )
```

profile of v0, /device:TPU:0, one launch (start us, length us, event | category | flops | bytes accessed | tf_op | source)
XLA Modules:
  0.0 220.1 jit_solution(4760761331875960938)
XLA Ops:
  7.2 0.0 all-gather.2.cloned.1.call-start
  7.2 1.1 convert_reduce_fusion
  8.4 1.2 fusion.14
  9.6 1.9 fusion.17
  11.6 0.0 all-gather.2.cloned.1.call-update
  11.6 0.0 copy-start.5
  11.6 6.2 %copy.38 = bf16[1,1,2,128,4096]{3,2,1,0,4:T(2,128)(2,1)} copy(bf16[1,1,2,128,4096]{4,3,2,1,0:T(8,128)(2,1)} %param.18) | data formatting | bytes 4194304 | tf_op args[8]
  17.8 7.3 %all-to-all-start = ((bf16[1,1,2,128,4096]{3,2,1,0,4:T(2,128)(2,1)}), bf16[1,1,2,128,4096]{3,2,1,0,4:T(2,128)(2,1)S(1)}, u32[]{:S(2)}, u32[]{:S(2)}) async-start(bf16[1,1,2,128,4096]{3,2,1,0,4:T(2,128)(2,1)} %copy.38), calls=%async_computation | async-start | bytes 4194304 | tf_op jit(solution)/shard_map/all_to_all | solution.py:49
  25.0 0.0 reduce-scatter.2.cloned.1.call-start
  25.1 0.0 copy-done.5
  25.1 0.5 slice.24
  25.6 0.6 broadcast_compare_fusion
  26.2 0.1 fusion.23
  26.3 77.7 %all-to-all-done = bf16[1,1,2,128,4096]{3,2,1,0,4:T(2,128)(2,1)S(1)} async-done(((bf16[1,1,2,128,4096]{3,2,1,0,4:T(2,128)(2,1)}), bf16[1,1,2,128,4096]{3,2,1,0,4:T(2,128)(2,1)S(1)}, u32[]{:S(2)}, u32[]{:S(2)}) %all-to-all-start) | async-done | bytes 2097184 | tf_op jit(solution)/shard_map/all_to_all | solution.py:49
  104.0 1.3 copy-done
  105.3 3.6 %copy.52 = bf16[1,1,2,128,8,512]{5,4,3,2,1,0:T(8,128)(2,1)S(1)} copy(bf16[1,1,2,128,8,512]{3,2,5,4,1,0:T(2,128)(2,1)} %bitcast.65) | data formatting | bytes 4194304 | tf_op jit(solution)/shard_map/all_to_all | solution.py:49
  108.9 1.5 fusion.29
  110.3 2.2 %copy.43 = bf16[8,1,128,512]{2,0,3,1:T(8,128)(2,1)S(1)} copy(bf16[8,1,128,512]{3,0,2,1:T(8,128)(2,1)} %get-tuple-element.3) | data formatting | bytes 2097152 | tf_op jit(solution)/shard_map/slice | solution.py:69
  112.6 0.0 copy-start.7
  112.6 1.3 reshape_squeeze.7
  113.9 2.2 %copy.40 = bf16[8,1,128,512]{2,0,3,1:T(8,128)(2,1)S(1)} copy(bf16[8,1,128,512]{3,0,2,1:T(8,128)(2,1)} %get-tuple-element.2) | data formatting | bytes 2097152 | tf_op jit(solution)/shard_map/slice | solution.py:68
  116.1 1.3 reshape_squeeze.6
  117.4 0.0 copy-done.7
  117.4 12.5 %fusion.2 = bf16[192,1536]{1,0:T(8,128)(2,1)S(1)} fusion(bf16[192,7168]{1,0:T(8,128)(2,1)} %all-gather.2.cloned.1.call-done, bf16[7168,1536]{1,0:T(8,128)(2,1)} %param.13, f32[1536]{0:T(1024)S(1)} %copy-done.7), kind=kOutput, calls=%fused_computation.8 | convolution fusion | flops 4228448256 | bytes 25368576 | tf_op jit(solution)/shard_map/dot_general | solution.py:54
  129.9 0.4 reshape.210
  130.4 0.0 copy-start.2
  130.4 0.8 fusion.30
  131.2 0.4 fusion.32
  131.7 0.7 fusion.31
  132.4 0.0 slice-start
  132.4 0.7 fusion.1
  133.1 0.0 slice-start.1
  133.1 0.8 divide_convert_fusion
  134.0 0.7 copy-done.3
  134.7 0.6 fusion.6
  135.3 0.3 fusion.11
  135.5 0.4 slice-done.1
  136.0 3.1 %convolution_convert_fusion = bf16[192,7168]{1,0:T(8,128)(2,1)} fusion(bf16[512,7168]{1,0:T(8,128)(2,1)S(1)} %bitcast.67, bf16[4,24,8,128]{3,2,1,0:T(8,128)(2,1)S(1)} %fusion.11), kind=kOutput, calls=%fused_computation | convolution fusion | flops 1410662400 | bytes 10289152 | tf_op jit(solution)/shard_map/dot_general | solution.py:98
  139.1 0.0 reduce-scatter.2.cloned.1.call-update
  139.2 0.2 reduce_window_sum.11
  139.4 1.7 convolution_convert_fusion.1
  141.1 1.8 copy.47
  142.8 0.0 copy-start.1
  142.8 0.0 copy-start.4
  142.8 39.6 %all_to_all.20 = bf16[1,4,3,2,128,512]{5,4,3,2,0,1:T(8,128)(2,1)S(1)} all-to-all(bf16[1,4,3,2,128,512]{5,4,3,2,0,1:T(8,128)(2,1)S(1)} %bitcast.63), channel_id=1, replica_groups=mesh['pipe'=4,'tensor'=8] {'pipe'}, dimensions={1} | all-to-all | bytes 6291456 | tf_op jit(solution)/shard_map/all_to_all | solution.py:33
  182.4 27.3 %reduce-scatter.2.cloned.1.call-done = bf16[24,7168]{1,0:T(8,128)(2,1)} async-done(((bf16[192,7168]{1,0:T(8,128)(2,1)}), bf16[24,7168]{1,0:T(8,128)(2,1)}) %reduce-scatter.2.cloned.1.call-update) | async-done | bytes 344080 | tf_op jit(solution)/shard_map/reduce_scatter | solution.py:97
  209.8 1.8 fusion.19
  211.6 1.7 copy.75
  (16 shorter events, 0.1 us)
Async XLA Ops:
  7.2 110.2 %all-gather.2.cloned.1.call-start = ((), (), s32[]{:S(2)}) async-start(), calls=%async_computation.3 | async-start | bytes 3096576 | tf_op jit(solution)/shard_map/all_gather | solution.py:55
  11.6 13.5 %copy-start.5 = (s32[192]{0:T(256)S(1)}, s32[192]{0:T(256)}, u32[]{:S(2)}) copy-start(s32[192]{0:T(256)} %param.17) | copy-start | bytes 2308
  17.8 86.2 %all-to-all-start = ((bf16[1,1,2,128,4096]{3,2,1,0,4:T(2,128)(2,1)}), bf16[1,1,2,128,4096]{3,2,1,0,4:T(2,128)(2,1)S(1)}, u32[]{:S(2)}, u32[]{:S(2)}) async-start(bf16[1,1,2,128,4096]{3,2,1,0,4:T(2,128)(2,1)} %copy.38), calls=%async_computation | async-start | bytes 4194304 | tf_op jit(solution)/shard_map/all_to_all | solution.py:49
  25.0 184.8 %reduce-scatter.2.cloned.1.call-start = ((), (), s32[]{:S(2)}) async-start(), calls=%async_computation.4 | async-start | bytes 3096576 | tf_op jit(solution)/shard_map/reduce_scatter | solution.py:97
  104.0 1.3 copy-start
  112.6 4.8 %copy-start.7 = (f32[1536]{0:T(1024)S(1)}, f32[1536]{0:T(1024)}, u32[]{:S(2)}) copy-start(f32[1536]{0:T(1024)} %param.14) | copy-start | bytes 18436
  130.4 1.3 copy-start.2
  132.4 3.1 %slice-start = ((s8[7340032]{0:T(1024)(128)(4,1)}), s8[4194304]{0:T(1024)(128)(4,1)S(1)}, s32[]{:S(2)}) async-start(s8[7340032]{0:T(1024)(128)(4,1)} %bitcast.66), calls=%async_computation.5 | async-start | bytes 8388608
  133.1 1.6 copy-start.3
  133.1 2.9 %slice-start.1 = ((s8[7340032]{0:T(1024)(128)(4,1)}), s8[3145728]{0:T(1024)(128)(4,1)S(1)}, s32[]{:S(2)}) async-start(s8[7340032]{0:T(1024)(128)(4,1)} %bitcast.66), calls=%async_computation.6 | async-start | bytes 6291456
  136.0 3.2 %copy-start.6 = (s32[1,8,1]{1,2,0:T(1,128)S(1)}, s32[1,8,1]{1,2,0:T(1,128)}, u32[]{:S(2)}) copy-start(s32[1,8,1]{1,2,0:T(1,128)} %param.19) | copy-start | bytes 100
  142.8 67.0 %copy-start.1 = (bf16[24,7168]{1,0:T(8,128)(2,1)S(1)}, bf16[24,7168]{1,0:T(8,128)(2,1)}, u32[]{:S(2)}) copy-start(bf16[24,7168]{1,0:T(8,128)(2,1)} %param.10) | copy-start | bytes 1032196
  142.8 67.0 %copy-start.4 = (f32[7168]{0:T(1024)S(1)}, f32[7168]{0:T(1024)}, u32[]{:S(2)}) copy-start(f32[7168]{0:T(1024)} %param.16) | copy-start | bytes 86020
Sparse Core Ops, SparseCore 0:
  11.7 93.3 all-gather.1
  139.3 70.4 reduce-scatter.1
where the time goes:
time: 221 us; the launch traced here: 220 us
  waiting for transfers between devices  105 us (48%)
  blocking collectives  39.6 us (18%)
  local copies, waits for them, and re-layouts  26 us (12%)
  matrix products  19.3 us (9%)
  between operations  14.2 us (6%)
  other arithmetic  8.6 us (4%)
  starting transfers between devices  7.36 us (3%)
    all_to_all x1, waiting for transfers between devices, local(): lax.all_to_all(prefill_cache, 'tensor', split_axis=4, concat_axis=1, tile...  77.7 us
    all_to_all x1, blocking collectives, send_decode(): lax.all_to_all(outgoing, 'pipe', split_axis=1, concat_axis=1, tiled=True)  39.6 us
    reduce_scatter x1, waiting for transfers between devices, local(): lax.psum_scatter(jnp.dot(context, out_weight, preferred_element_type=jnp....  27.3 us
    dot_general x1, matrix products, local(): jnp.dot(lax.all_gather(normed, 'tensor', axis=0, tiled=True), qkv_weight,...  12.5 us
    unnamed x22, local copies, waits for them, and re-layouts  10.3 us
    all_to_all x1, starting transfers between devices, local(): lax.all_to_all(prefill_cache, 'tensor', split_axis=4, concat_axis=1, tile...  7.28 us
  transfers between devices with their start and end apart: 3, of which 2 were waited for; matrix products, arithmetic and copies ran while one was open for 10% of the time, Pallas kernels for 0%

commit v1 on v0

--- a/solution.py
+++ b/solution.py
@@ -4,6 +4,9 @@
 from jax.sharding import PartitionSpec as P
 
 HD = 128
+PIPE_PERMUTE = True
+A2A_PERMUTE = True
+RELAY_BARRIER = True
 
 
 def normalize(x, gain, shift):
@@ -12,7 +15,27 @@
     return ((x - mean) * lax.rsqrt(var + 1e-05) * gain + shift).astype(jnp.bfloat16)
 
 
-def send_decode(per_head_rows, block_dest):
+def shifted(x, axis, k, n):
+    return lax.ppermute(x, axis, [(j, (j + k) % n) for j in range(n)])
+
+
+def gather_heads(prefill_cache):
+    tensor_count = lax.axis_size("tensor")
+    if not A2A_PERMUTE:
+        rows = lax.all_to_all(prefill_cache, "tensor", split_axis=4, concat_axis=1, tiled=True)
+        return rows, jnp.arange(tensor_count)
+    i = lax.axis_index("tensor")
+    layers, _, two, blk, width = prefill_cache.shape
+    chunks = prefill_cache.reshape(layers, two, blk, tensor_count, width // tensor_count)
+    arrived = []
+    for k in range(tensor_count):
+        piece = lax.dynamic_index_in_dim(chunks, (i + k) % tensor_count, 3, keepdims=False)
+        arrived.append(piece if k == 0 else shifted(piece, "tensor", k, tensor_count))
+    rows = jnp.stack(arrived, axis=1)
+    return rows, (i - jnp.arange(tensor_count)) % tensor_count
+
+
+def send_decode(per_head_rows, block_of, block_dest):
     layers = per_head_rows.shape[0]
     pipe_count = lax.axis_size("pipe")
     row_blocks = per_head_rows.shape[1]
@@ -23,15 +46,68 @@
     )
     earlier_tokens = jnp.cumsum(onehot, axis=1) - onehot
     slot = jnp.sum(earlier_tokens * onehot, axis=-1)
-    position = dest * capacity + slot
+    position = (dest * capacity + slot)[:, block_of]
     targets = jnp.arange(pipe_count * capacity, dtype=jnp.int32)
     placement_index = (position[:, None, :] == targets[None, :, None]).astype(jnp.bfloat16)
     outgoing = jnp.einsum(
         "gud,gdoih->guoih", placement_index, per_head_rows, preferred_element_type=jnp.float32
     ).astype(jnp.bfloat16)
     outgoing = outgoing.reshape((layers, pipe_count, capacity) + per_head_rows.shape[2:])
-    arrived = lax.all_to_all(outgoing, "pipe", split_axis=1, concat_axis=1, tiled=True)
+    if not PIPE_PERMUTE:
+        arrived = lax.all_to_all(outgoing, "pipe", split_axis=1, concat_axis=1, tiled=True)
+        return arrived.reshape((layers, pipe_count * capacity) + per_head_rows.shape[2:])
+    i = lax.axis_index("pipe")
+    arrived = []
+    for k in range(pipe_count):
+        piece = lax.dynamic_index_in_dim(outgoing, (i + k) % pipe_count, 1, keepdims=False)
+        arrived.append(piece if k == 0 else shifted(piece, "pipe", k, pipe_count))
+    arrived = jnp.stack(arrived, axis=1)
+    arrived = jnp.take(arrived, (i - jnp.arange(pipe_count)) % pipe_count, axis=1)
     return arrived.reshape((layers, pipe_count * capacity) + per_head_rows.shape[2:])
+
+
+def partner(x):
+    tensor_count = lax.axis_size("tensor")
+    return lax.ppermute(x, "tensor", [(j, j ^ 1) for j in range(tensor_count)])
+
+
+def ring(x):
+    tensor_count = lax.axis_size("tensor")
+    rows = tensor_count // 2
+    return lax.ppermute(
+        x, "tensor", [(j, ((j // 2 + 1) % rows) * 2 + j % 2) for j in range(tensor_count)]
+    )
+
+
+def gather_tokens(x):
+    tensor_count = lax.axis_size("tensor")
+    rows = tensor_count // 2
+    i = lax.axis_index("tensor")
+    outer, inner = i // 2, i % 2
+    own = [x]
+    for _ in range(1, rows):
+        own.append(ring(own[-1]))
+    other = [partner(piece) for piece in own]
+    steps = jnp.arange(rows)
+    source = jnp.concatenate(
+        [((outer - steps) % rows) * 2 + inner, ((outer - steps) % rows) * 2 + (1 - inner)]
+    )
+    return jnp.concatenate(own + other, axis=0), source
+
+
+def scatter_tokens(partial):
+    tensor_count = lax.axis_size("tensor")
+    rows = tensor_count // 2
+    blocks = partial.reshape((2, rows, -1) + partial.shape[1:])
+    mine = [
+        blocks[0, s] + partner(blocks[1, s].astype(jnp.bfloat16)).astype(jnp.float32)
+        for s in range(rows)
+    ]
+    carried = mine[1 % rows]
+    for k in range(1, rows):
+        arrived = ring(carried.astype(jnp.bfloat16)).astype(jnp.float32)
+        carried = arrived + mine[(k + 1) % rows]
+    return carried
 
 
 def local(
@@ -46,19 +122,19 @@
     prefill_cache,
     block_dest,
 ):
-    per_head_rows = lax.all_to_all(prefill_cache, "tensor", split_axis=4, concat_axis=1, tiled=True)
+    per_head_rows, block_of = gather_heads(prefill_cache)
+    decode_side_cache = send_decode(per_head_rows, block_of, block_dest)
     hidden = stretch.astype(jnp.float32)
     head_count = qkv_weight.shape[1] // (3 * HD)
     normed = normalize(hidden, ln_gain, ln_bias)
+    gathered, source = gather_tokens(normed)
     qkv = (
-        jnp.dot(
-            lax.all_gather(normed, "tensor", axis=0, tiled=True),
-            qkv_weight,
-            preferred_element_type=jnp.float32,
-        )
-        + qkv_bias
+        jnp.dot(gathered, qkv_weight, preferred_element_type=jnp.float32) + qkv_bias
     ).astype(jnp.bfloat16)
     group_tokens = qkv.shape[0]
+    place = (source[:, None] * normed.shape[0] + jnp.arange(normed.shape[0])[None, :]).reshape(-1)
+    first_segment = segment_ids[0]
+    segment_ids = segment_ids[place]
     heads = qkv.reshape(group_tokens, head_count, 3, HD)
     query = heads[:, :, 0]
     keys = heads[:, :, 1]
@@ -72,11 +148,10 @@
     old_scores = (
         jnp.einsum("qhd,khd->hqk", query, cached_keys, preferred_element_type=jnp.float32) * scale
     )
-    place = jnp.arange(group_tokens)
     own_visible = (segment_ids[:, None] == segment_ids[None, :]) & (
         place[None, :] <= place[:, None]
     )
-    old_visible = (segment_ids == segment_ids[0])[:, None]
+    old_visible = (segment_ids == first_segment)[:, None]
     own_scores = jnp.where(own_visible[None], own_scores, -jnp.inf)
     old_scores = jnp.where(old_visible[None], old_scores, -jnp.inf)
     scores = jnp.concatenate([old_scores, own_scores], axis=2)
@@ -94,14 +169,10 @@
         preferred_element_type=jnp.float32,
     )
     context = context.astype(jnp.bfloat16).reshape(group_tokens, head_count * HD)
-    summed = lax.psum_scatter(
-        jnp.dot(context, out_weight, preferred_element_type=jnp.float32).astype(jnp.bfloat16),
-        "tensor",
-        scatter_dimension=0,
-        tiled=True,
-    ).astype(jnp.float32)
+    if RELAY_BARRIER:
+        decode_side_cache, context = lax.optimization_barrier((decode_side_cache, context))
+    summed = scatter_tokens(jnp.dot(context, out_weight, preferred_element_type=jnp.float32))
     mixed = (hidden + summed + out_bias).astype(jnp.bfloat16)
-    decode_side_cache = send_decode(per_head_rows, block_dest)
     return (mixed, decode_side_cache)
 
 

time: 221 us -> 205 us (0.928)
  starting transfers between devices: 7.36 us -> 49.7 us
  blocking collectives: 39.6 us -> 0 us
  waiting for transfers between devices: 105 us -> 66.2 us
  local copies, waits for them, and re-layouts: 26 us -> 59.7 us
  between operations: 14.2 us -> 1.34 us
  matrix products: 19.3 us -> 14.9 us
    all_to_all x1 -> x0, waiting for transfers between devices: 77.7 us -> none  [local(): lax.all_to_all(prefill_cache, 'tensor', split_axis=4, concat_axis=1, tile...]
    ppermute x0 -> x24, waiting for transfers between devices: none -> 66.2 us  [the longest x6 36.6 us: ring(): lax.ppermute(x, 'tensor', [(j, (j // 2 + 1) % rows * 2 + j % 2) for j in...]
    ppermute x0 -> x24, starting transfers between devices: none -> 49.7 us  [the longest x6 19.7 us: ring(): lax.ppermute(x, 'tensor', [(j, (j // 2 + 1) % rows * 2 + j % 2) for j in...]
    all_to_all x1 -> x0, blocking collectives: 39.6 us -> none  [send_decode(): lax.all_to_all(outgoing, 'pipe', split_axis=1, concat_axis=1, tiled=True)]
    reduce_scatter x1 -> x0, waiting for transfers between devices: 27.3 us -> none  [local(): lax.psum_scatter(jnp.dot(context, out_weight, preferred_element_type=jnp....]
    another operation x0 -> x9, local copies, waits for them, and re-layouts: none -> 20.2 us  [gather_heads(): rows = jnp.stack(arrived, axis=1)]
    dynamic_slice x0 -> x9, local copies, waits for them, and re-layouts: none -> 8.99 us  [the longest x8 8.66 us: gather_heads(): lax.dynamic_index_in_dim(chunks, (i + k) % tensor_count, 3, keepdims=False)]
    all_to_all x1 -> x0, starting transfers between devices: 7.28 us -> none  [local(): lax.all_to_all(prefill_cache, 'tensor', split_axis=4, concat_axis=1, tile...]
  transfers between devices with their start and end apart: 3 -> 24, of which waited for: 2 -> 11; matrix products, arithmetic and copies ran while one was open for 10% -> 30% of each run, Pallas kernels for 0% -> 0%
where the time goes in v1:
time: 205 us; the launch traced here: 202 us
  waiting for transfers between devices  66.2 us (32%)
  local copies, waits for them, and re-layouts  59.7 us (29%)
  starting transfers between devices  49.7 us (24%)
  matrix products  14.9 us (7%)
  other arithmetic  10.4 us (5%)
    ppermute x6, waiting for transfers between devices, ring(): lax.ppermute(x, 'tensor', [(j, (j // 2 + 1) % rows * 2 + j % 2) for j in...  36.6 us
    ppermute x8, waiting for transfers between devices, partner(): return lax.ppermute(x, 'tensor', [(j, j ^ 1) for j in range(tensor_count)])  24.4 us
    another operation x9, local copies, waits for them, and re-layouts, gather_heads(): rows = jnp.stack(arrived, axis=1)  20.2 us
    ppermute x6, starting transfers between devices, ring(): lax.ppermute(x, 'tensor', [(j, (j // 2 + 1) % rows * 2 + j % 2) for j in...  19.7 us
    ppermute x10, starting transfers between devices, shifted(): return lax.ppermute(x, axis, [(j, (j + k) % n) for j in range(n)])  15.8 us
    ppermute x8, starting transfers between devices, partner(): return lax.ppermute(x, 'tensor', [(j, j ^ 1) for j in range(tensor_count)])  14.2 us
    unnamed x35, local copies, waits for them, and re-layouts  11.8 us
    dot_general x1, matrix products, local(): jnp.dot(gathered, qkv_weight, preferred_element_type=jnp.float32) + qkv_bias  9.7 us
  transfers between devices with their start and end apart: 24, of which 11 were waited for; matrix products, arithmetic and copies ran while one was open for 30% of the time, Pallas kernels for 0%

profile of v1, /device:TPU:0, one launch (start us, length us, event | category | flops | bytes accessed | tf_op | source)
XLA Modules:
  0.0 202.3 jit_solution(12361387776895563461)
XLA Ops:
  0.7 3.1 %copy.86 = bf16[1,1,2,128,4096]{3,4,2,1,0:T(8,128)(2,1)S(1)} copy(bf16[1,1,2,128,4096]{4,3,2,1,0:T(8,128)(2,1)} %param.18) | data formatting | bytes 4194304 | tf_op args[8]
  6.1 3.0 %collective-permute-start = (bf16[1,2,128,512]{3,2,1,0:T(8,128)(2,1)S(1)}, bf16[1,2,128,512]{3,2,1,0:T(8,128)(2,1)S(1)}, u32[]{:S(2)}, u32[]{:S(2)}) collective-permute-start(bf16[1,2,128,512]{3,2,1,0:T(8,128)(2,1)S(1)} %bitcast.153), channel_id=1, source_target_pairs={{0,1},{1,2},{2,3},{3,4},{4,5},{5,6},{6,7},{7,0},{8,9},{9,10},{10,1... | collective-permute-start | bytes 786440 | tf_op jit(solution)/shard_map/ppermute | solution.py:19
  10.2 1.6 collective-permute-start.1
  11.9 1.8 copy.90
  13.7 2.5 %collective-permute-start.2 = (bf16[1,2,128,512]{3,2,1,0:T(8,128)(2,1)}, bf16[1,2,128,512]{3,2,1,0:T(8,128)(2,1)}, u32[]{:S(2)}, u32[]{:S(2)}) collective-permute-start(bf16[1,2,128,512]{3,2,1,0:T(8,128)(2,1)} %bitcast.13), channel_id=1, source_target_pairs={{0,3},{1,4},{2,5},{3,6},{4,7},{5,0},{6,1},{7,2},{8,11},{9,12},{10,... | collective-permute-start | bytes 786440 | tf_op jit(solution)/shard_map/ppermute | solution.py:19
  16.2 1.8 copy.91
  18.0 1.2 collective-permute-start.3
  20.1 2.6 %collective-permute-start.4 = (bf16[1,2,128,512]{3,2,1,0:T(8,128)(2,1)}, bf16[1,2,128,512]{3,2,1,0:T(8,128)(2,1)S(1)}, u32[]{:S(2)}, u32[]{:S(2)}) collective-permute-start(bf16[1,2,128,512]{3,2,1,0:T(8,128)(2,1)} %bitcast.17), channel_id=1, source_target_pairs={{0,5},{1,6},{2,7},{3,0},{4,1},{5,2},{6,3},{7,4},{8,13},{9,14},{10,... | collective-permute-start | bytes 786440 | tf_op jit(solution)/shard_map/ppermute | solution.py:19
  25.4 1.6 gather_fusion.2
  28.7 1.4 collective-permute-start.5
  30.1 1.4 collective-permute-start.6
  33.9 2.1 %copy.97 = bf16[1,1,2,128,512]{4,1,3,2,0:T(2,128)(2,1)} copy(bf16[1,1,2,128,512]{4,3,2,1,0:T(8,128)(2,1)} %bitcast.148) | data formatting | bytes 524288 | tf_op jit(solution)/shard_map/stack | solution.py:34
  36.1 5.1 %collective-permute-done.2 = bf16[1,2,128,512]{3,2,1,0:T(8,128)(2,1)} collective-permute-done((bf16[1,2,128,512]{3,2,1,0:T(8,128)(2,1)}, bf16[1,2,128,512]{3,2,1,0:T(8,128)(2,1)}, u32[]{:S(2)}, u32[]{:S(2)}) %collective-permute-start.2) | collective-permute-done | bytes 262176 | tf_op jit(solution)/shard_map/ppermute | solution.py:19
  41.2 2.1 %copy.98 = bf16[1,1,2,128,512]{4,1,3,2,0:T(2,128)(2,1)} copy(bf16[1,1,2,128,512]{4,3,2,1,0:T(8,128)(2,1)} %bitcast.14) | data formatting | bytes 524288 | tf_op jit(solution)/shard_map/stack | solution.py:34
  43.4 11.6 %collective-permute-start.10 = (bf16[24,7168]{1,0:T(8,128)(2,1)}, bf16[24,7168]{1,0:T(8,128)(2,1)}, u32[]{:S(2)}, u32[]{:S(2)}) collective-permute-start(bf16[24,7168]{1,0:T(8,128)(2,1)} %get-tuple-element.7), channel_id=1, source_target_pairs={{0,2},{1,3},{2,4},{3,5},{4,6},{5,7},{6,0},{7,1},{8,10},{9,11},{10,... | collective-permute-start | bytes 1032200 | tf_op jit(solution)/shard_map/ppermute | solution.py:77
  56.1 1.2 copy.100
  59.8 10.2 %stack.48 = bf16[1,8,2,128,512]{4,1,3,2,0:T(8,128)(2,1)S(1)} concatenate(bf16[1,1,2,128,512]{4,1,3,2,0:T(2,128)(2,1)S(1)} %copy.95, bf16[1,1,2,128,512]{4,1,3,2,0:T(2,128)(2,1)S(1)} %copy.96, bf16[1,1,2,128,512]{4,1,3,2,0:T(2,128)(2,1)} %copy.97, bf16[1,1,2,128,512]{4,1,3,2,0:T(2,128)(2,1)} %copy.98, bf16[1,1,2,128,512]{4,1,3,2,0:T(2,128)(2,1)} %copy.99, ...), dimensions={1} | concatenate | bytes 4194304 | tf_op jit(solution)/shard_map/stack | solution.py:34
  70.0 1.5 fusion.49
  71.5 2.2 %copy.104 = bf16[8,1,128,512]{2,0,3,1:T(8,128)(2,1)S(1)} copy(bf16[8,1,128,512]{3,0,2,1:T(8,128)(2,1)} %get-tuple-element.16) | data formatting | bytes 2097152 | tf_op jit(solution)/shard_map/slice | solution.py:145
  73.7 1.3 reshape_squeeze.6
  75.0 2.2 %copy.106 = bf16[8,1,128,512]{2,0,3,1:T(8,128)(2,1)S(1)} copy(bf16[8,1,128,512]{3,0,2,1:T(8,128)(2,1)} %get-tuple-element.17) | data formatting | bytes 2097152 | tf_op jit(solution)/shard_map/slice | solution.py:144
  77.3 1.3 reshape_squeeze.7
  78.5 1.7 convolution_convert_fusion
  80.2 1.8 copy.103
  82.5 1.6 collective-permute-start.8
  84.3 3.6 %collective-permute-start.11 = (bf16[24,7168]{1,0:T(8,128)(2,1)}, bf16[24,7168]{1,0:T(8,128)(2,1)S(1)}, u32[]{:S(2)}, u32[]{:S(2)}) collective-permute-start(bf16[24,7168]{1,0:T(8,128)(2,1)} %collective-permute-done.10), channel_id=1, source_target_pairs={{0,2},{1,3},{2,4},{3,5},{4,6},{5,7},{6,0},{7,1},{8,10},{9,11},{10,... | collective-permute-start | bytes 1032200 | tf_op jit(solution)/shard_map/ppermute | solution.py:77
  87.9 1.8 constant_dynamic-update-slice_fusion.6
  89.6 7.1 %collective-permute-done.11 = bf16[24,7168]{1,0:T(8,128)(2,1)S(1)} collective-permute-done((bf16[24,7168]{1,0:T(8,128)(2,1)}, bf16[24,7168]{1,0:T(8,128)(2,1)S(1)}, u32[]{:S(2)}, u32[]{:S(2)}) %collective-permute-start.11) | collective-permute-done | bytes 344096 | tf_op jit(solution)/shard_map/ppermute | solution.py:77
  96.7 4.1 %collective-permute-start.12 = (bf16[24,7168]{1,0:T(8,128)(2,1)S(1)}, bf16[24,7168]{1,0:T(8,128)(2,1)}, u32[]{:S(2)}, u32[]{:S(2)}) collective-permute-start(bf16[24,7168]{1,0:T(8,128)(2,1)S(1)} %collective-permute-done.11), channel_id=1, source_target_pairs={{0,2},{1,3},{2,4},{3,5},{4,6},{5,7},{6,0},{7,1},{8,10},{9,11},{10,... | collective-permute-start | bytes 1032200 | tf_op jit(solution)/shard_map/ppermute | solution.py:77
  101.6 9.1 %collective-permute-done.12 = bf16[24,7168]{1,0:T(8,128)(2,1)} collective-permute-done((bf16[24,7168]{1,0:T(8,128)(2,1)S(1)}, bf16[24,7168]{1,0:T(8,128)(2,1)}, u32[]{:S(2)}, u32[]{:S(2)}) %collective-permute-start.12) | collective-permute-done | bytes 344096 | tf_op jit(solution)/shard_map/ppermute | solution.py:77
  110.7 4.5 %collective-permute-start.14 = (bf16[24,7168]{1,0:T(8,128)(2,1)}, bf16[24,7168]{1,0:T(8,128)(2,1)S(1)}, u32[]{:S(2)}, u32[]{:S(2)}) collective-permute-start(bf16[24,7168]{1,0:T(8,128)(2,1)} %collective-permute-done.10), channel_id=1, source_target_pairs={{0,1},{1,0},{2,3},{3,2},{4,5},{5,4},{6,7},{7,6},{8,9},{9,8},{10,11... | collective-permute-start | bytes 1032200 | tf_op jit(solution)/shard_map/ppermute | solution.py:71
  115.2 1.7 constant_dynamic-update-slice_fusion.4
  117.0 1.7 constant_dynamic-update-slice_fusion.3
  118.7 5.6 %collective-permute-done.14 = bf16[24,7168]{1,0:T(8,128)(2,1)S(1)} collective-permute-done((bf16[24,7168]{1,0:T(8,128)(2,1)}, bf16[24,7168]{1,0:T(8,128)(2,1)S(1)}, u32[]{:S(2)}, u32[]{:S(2)}) %collective-permute-start.14) | collective-permute-done | bytes 344096 | tf_op jit(solution)/shard_map/ppermute | solution.py:71
  124.3 2.1 %collective-permute-start.16 = (bf16[24,7168]{1,0:T(8,128)(2,1)}, bf16[24,7168]{1,0:T(8,128)(2,1)}, u32[]{:S(2)}, u32[]{:S(2)}) collective-permute-start(bf16[24,7168]{1,0:T(8,128)(2,1)} %collective-permute-done.12), channel_id=1, source_target_pairs={{0,1},{1,0},{2,3},{3,2},{4,5},{5,4},{6,7},{7,6},{8,9},{9,8},{10,11... | collective-permute-start | bytes 1032200 | tf_op jit(solution)/shard_map/ppermute | solution.py:71
  127.2 4.6 %collective-permute-done.15 = bf16[24,7168]{1,0:T(8,128)(2,1)S(1)} collective-permute-done((bf16[24,7168]{1,0:T(8,128)(2,1)S(1)}, bf16[24,7168]{1,0:T(8,128)(2,1)S(1)}, u32[]{:S(2)}, u32[]{:S(2)}) %collective-permute-start.15) | collective-permute-done | bytes 344096 | tf_op jit(solution)/shard_map/ppermute | solution.py:71
  132.9 2.4 %gather_fusion.1 = bf16[4,3,2,128,512]{4,3,2,1,0:T(8,128)(2,1)} fusion(bf16[4,3,2,128,512]{4,3,2,1,0:T(8,128)(2,1)S(1)} %maximum_bitcast_fusion, s32[1024]{0:T(1024)S(1)} %pad_clamp_fusion.1), kind=kCustom, calls=%fused_computation.1 | custom fusion | bytes 6291472 | tf_op jit(solution)/shard_map/jit(_take)/gather | solution.py:65
  135.3 4.1 %bitcast_select_fusion = bf16[1,12,2,128,512]{4,3,2,1,0:T(8,128)(2,1)} fusion(pred[12]{0:T(512)(128)(4,1)S(1)} %copy-done.10, bf16[1,12,2,128,512]{4,3,2,1,0:T(8,128)(2,1)} %bitcast.137), kind=kLoop, calls=%fused_computation.7 | loop fusion | flops 1572864 | bytes 6291468 | tf_op jit(solution)/shard_map/jit(_take)/select_n | solution.py:65
  140.4 9.7 %fusion.2 = bf16[192,1536]{1,0:T(8,128)(2,1)S(1)} fusion(bf16[192,7168]{1,0:T(8,128)(2,1)S(1)} %constant_dynamic-update-slice_fusion, bf16[7168,1536]{1,0:T(8,128)(2,1)} %param.13, f32[1536]{0:T(1024)S(1)} %copy-done.11), kind=kOutput, calls=%fused_computation.12 | convolution fusion | flops 4228448256 | bytes 25368576 | tf_op jit(solution)/shard_map/dot_general | solution.py:132
  156.2 1.6 fusion.53
  158.3 2.1 %collective-permute-start.17 = (bf16[24,7168]{1,0:T(8,128)(2,1)S(1)}, bf16[24,7168]{1,0:T(8,128)(2,1)S(1)}, u32[]{:S(2)}, u32[]{:S(2)}) collective-permute-start(bf16[24,7168]{1,0:T(8,128)(2,1)S(1)} %get-tuple-element.12), channel_id=1, source_target_pairs={{0,1},{1,0},{2,3},{3,2},{4,5},{5,4},{6,7},{7,6},{8,9},{9,8},{10,11... | collective-permute-start | bytes 1032200 | tf_op jit(solution)/shard_map/ppermute | solution.py:71
  160.5 8.9 %collective-permute-done.17 = bf16[24,7168]{1,0:T(8,128)(2,1)S(1)} collective-permute-done((bf16[24,7168]{1,0:T(8,128)(2,1)S(1)}, bf16[24,7168]{1,0:T(8,128)(2,1)S(1)}, u32[]{:S(2)}, u32[]{:S(2)}) %collective-permute-start.17) | collective-permute-done | bytes 344096 | tf_op jit(solution)/shard_map/ppermute | solution.py:71
  169.9 2.0 collective-permute-start.21
  171.9 4.9 %collective-permute-done.19 = bf16[24,7168]{1,0:T(8,128)(2,1)S(1)} collective-permute-done((bf16[24,7168]{1,0:T(8,128)(2,1)S(1)}, bf16[24,7168]{1,0:T(8,128)(2,1)S(1)}, u32[]{:S(2)}, u32[]{:S(2)}) %collective-permute-start.19) | collective-permute-done | bytes 344096 | tf_op jit(solution)/shard_map/ppermute | solution.py:71
  176.8 3.4 %collective-permute-done.18 = bf16[24,7168]{1,0:T(8,128)(2,1)S(1)} collective-permute-done((bf16[24,7168]{1,0:T(8,128)(2,1)S(1)}, bf16[24,7168]{1,0:T(8,128)(2,1)S(1)}, u32[]{:S(2)}, u32[]{:S(2)}) %collective-permute-start.18) | collective-permute-done | bytes 344096 | tf_op jit(solution)/shard_map/ppermute | solution.py:77
  180.3 3.4 %collective-permute-start.23 = (bf16[24,7168]{1,0:T(8,128)(2,1)S(1)}, bf16[24,7168]{1,0:T(8,128)(2,1)S(1)}, u32[]{:S(2)}, u32[]{:S(2)}) collective-permute-start(bf16[24,7168]{1,0:T(8,128)(2,1)S(1)} %get-tuple-element.13), channel_id=1, source_target_pairs={{0,1},{1,0},{2,3},{3,2},{4,5},{5,4},{6,7},{7,6},{8,9},{9,8},{10,11... | collective-permute-start | bytes 1032200 | tf_op jit(solution)/shard_map/ppermute | solution.py:71
  184.1 8.0 %collective-permute-done.20 = bf16[24,7168]{1,0:T(8,128)(2,1)S(1)} collective-permute-done((bf16[24,7168]{1,0:T(8,128)(2,1)S(1)}, bf16[24,7168]{1,0:T(8,128)(2,1)S(1)}, u32[]{:S(2)}, u32[]{:S(2)}) %collective-permute-start.20) | collective-permute-done | bytes 344096 | tf_op jit(solution)/shard_map/ppermute | solution.py:77
  192.3 9.0 %collective-permute-done.22 = bf16[24,7168]{1,0:T(8,128)(2,1)S(1)} collective-permute-done((bf16[24,7168]{1,0:T(8,128)(2,1)S(1)}, bf16[24,7168]{1,0:T(8,128)(2,1)S(1)}, u32[]{:S(2)}, u32[]{:S(2)}) %collective-permute-start.22) | collective-permute-done | bytes 344096 | tf_op jit(solution)/shard_map/ppermute | solution.py:77
  (111 shorter events, 27.5 us)
Async XLA Ops:
  3.9 18.8 %copy-start.1 = (bf16[24,7168]{1,0:T(8,128)(2,1)S(1)}, bf16[24,7168]{1,0:T(8,128)(2,1)}, u32[]{:S(2)}) copy-start(bf16[24,7168]{1,0:T(8,128)(2,1)} %param.10) | copy-start | bytes 1032196
  3.9 19.3 %copy-start.9 = (s32[1,8,1]{1,2,0:T(1,128)S(1)}, s32[1,8,1]{1,2,0:T(1,128)}, u32[]{:S(2)}) copy-start(s32[1,8,1]{1,2,0:T(1,128)} %param.19) | copy-start | bytes 100
  3.9 19.8 %copy-start.7 = (f32[7168]{0:T(1024)S(1)}, f32[7168]{0:T(1024)}, u32[]{:S(2)}) copy-start(f32[7168]{0:T(1024)} %param.12) | copy-start | bytes 86020
  4.0 19.8 %copy-start.8 = (f32[7168]{0:T(1024)S(1)}, f32[7168]{0:T(1024)}, u32[]{:S(2)}) copy-start(f32[7168]{0:T(1024)} %param.11) | copy-start | bytes 86020
  5.0 19.8 %copy-start = (s32[192]{0:T(256)S(1)}, s32[192]{0:T(256)}, u32[]{:S(2)}) copy-start(s32[192]{0:T(256)} %param.17) | copy-start | bytes 2308
  6.1 22.5 %collective-permute-start = (bf16[1,2,128,512]{3,2,1,0:T(8,128)(2,1)S(1)}, bf16[1,2,128,512]{3,2,1,0:T(8,128)(2,1)S(1)}, u32[]{:S(2)}, u32[]{:S(2)}) collective-permute-start(bf16[1,2,128,512]{3,2,1,0:T(8,128)(2,1)S(1)} %bitcast.153), channel_id=1, source_target_pairs={{0,1},{1,2},{2,3},{3,4},{4,5},{5,6},{6,7},{7,0},{8,9},{9,10},{10,1... | collective-permute-start | bytes 786440 | tf_op jit(solution)/shard_map/ppermute | solution.py:19
  10.2 19.8 %collective-permute-start.1 = (bf16[1,2,128,512]{3,2,1,0:T(8,128)(2,1)S(1)}, bf16[1,2,128,512]{3,2,1,0:T(8,128)(2,1)S(1)}, u32[]{:S(2)}, u32[]{:S(2)}) collective-permute-start(bf16[1,2,128,512]{3,2,1,0:T(8,128)(2,1)S(1)} %bitcast.152), channel_id=1, source_target_pairs={{0,2},{1,3},{2,4},{3,5},{4,6},{5,7},{6,0},{7,1},{8,10},{9,11},{10,... | collective-permute-start | bytes 786440 | tf_op jit(solution)/shard_map/ppermute | solution.py:19
  13.7 27.6 %collective-permute-start.2 = (bf16[1,2,128,512]{3,2,1,0:T(8,128)(2,1)}, bf16[1,2,128,512]{3,2,1,0:T(8,128)(2,1)}, u32[]{:S(2)}, u32[]{:S(2)}) collective-permute-start(bf16[1,2,128,512]{3,2,1,0:T(8,128)(2,1)} %bitcast.13), channel_id=1, source_target_pairs={{0,3},{1,4},{2,5},{3,6},{4,7},{5,0},{6,1},{7,2},{8,11},{9,12},{10,... | collective-permute-start | bytes 786440 | tf_op jit(solution)/shard_map/ppermute | solution.py:19
  18.0 25.4 %collective-permute-start.3 = (bf16[1,2,128,512]{3,2,1,0:T(8,128)(2,1)}, bf16[1,2,128,512]{3,2,1,0:T(8,128)(2,1)S(1)}, u32[]{:S(2)}, u32[]{:S(2)}) collective-permute-start(bf16[1,2,128,512]{3,2,1,0:T(8,128)(2,1)} %bitcast.15), channel_id=1, source_target_pairs={{0,4},{1,5},{2,6},{3,7},{4,0},{5,1},{6,2},{7,3},{8,12},{9,13},{10,... | collective-permute-start | bytes 786440 | tf_op jit(solution)/shard_map/ppermute | solution.py:19
  20.1 36.0 %collective-permute-start.4 = (bf16[1,2,128,512]{3,2,1,0:T(8,128)(2,1)}, bf16[1,2,128,512]{3,2,1,0:T(8,128)(2,1)S(1)}, u32[]{:S(2)}, u32[]{:S(2)}) collective-permute-start(bf16[1,2,128,512]{3,2,1,0:T(8,128)(2,1)} %bitcast.17), channel_id=1, source_target_pairs={{0,5},{1,6},{2,7},{3,0},{4,1},{5,2},{6,3},{7,4},{8,13},{9,14},{10,... | collective-permute-start | bytes 786440 | tf_op jit(solution)/shard_map/ppermute | solution.py:19
  28.7 28.7 %collective-permute-start.5 = (bf16[1,2,128,512]{3,2,1,0:T(8,128)(2,1)}, bf16[1,2,128,512]{3,2,1,0:T(8,128)(2,1)S(1)}, u32[]{:S(2)}, u32[]{:S(2)}) collective-permute-start(bf16[1,2,128,512]{3,2,1,0:T(8,128)(2,1)} %bitcast.19), channel_id=1, source_target_pairs={{0,6},{1,7},{2,0},{3,1},{4,2},{5,3},{6,4},{7,5},{8,14},{9,15},{10,... | collective-permute-start | bytes 786440 | tf_op jit(solution)/shard_map/ppermute | solution.py:19
  30.1 2.2 %copy-start.4 = (bf16[1,2,128,512]{3,2,1,0:T(8,128)(2,1)}, bf16[1,2,128,512]{3,2,1,0:T(8,128)(2,1)S(1)}, u32[]{:S(2)}) copy-start(bf16[1,2,128,512]{3,2,1,0:T(8,128)(2,1)S(1)} %collective-permute-done.1) | copy-start | bytes 786436
  30.1 28.5 %collective-permute-start.6 = (bf16[1,2,128,512]{3,2,1,0:T(8,128)(2,1)S(1)}, bf16[1,2,128,512]{3,2,1,0:T(8,128)(2,1)S(1)}, u32[]{:S(2)}, u32[]{:S(2)}) collective-permute-start(bf16[1,2,128,512]{3,2,1,0:T(8,128)(2,1)S(1)} %bitcast.151), channel_id=1, source_target_pairs={{0,7},{1,0},{2,1},{3,2},{4,3},{5,4},{6,5},{7,6},{8,15},{9,8},{10,9... | collective-permute-start | bytes 786440 | tf_op jit(solution)/shard_map/ppermute | solution.py:19
  41.2 75.8 %collective-permute-start.13 = (bf16[24,7168]{1,0:T(8,128)(2,1)}, bf16[24,7168]{1,0:T(8,128)(2,1)}, u32[]{:S(2)}, u32[]{:S(2)}) collective-permute-start(bf16[24,7168]{1,0:T(8,128)(2,1)} %get-tuple-element.7), channel_id=1, source_target_pairs={{0,1},{1,0},{2,3},{3,2},{4,5},{5,4},{6,7},{7,6},{8,9},{9,8},{10,11... | collective-permute-start | bytes 1032200 | tf_op jit(solution)/shard_map/ppermute | solution.py:71
  43.4 40.9 %collective-permute-start.10 = (bf16[24,7168]{1,0:T(8,128)(2,1)}, bf16[24,7168]{1,0:T(8,128)(2,1)}, u32[]{:S(2)}, u32[]{:S(2)}) collective-permute-start(bf16[24,7168]{1,0:T(8,128)(2,1)} %get-tuple-element.7), channel_id=1, source_target_pairs={{0,2},{1,3},{2,4},{3,5},{4,6},{5,7},{6,0},{7,1},{8,10},{9,11},{10,... | collective-permute-start | bytes 1032200 | tf_op jit(solution)/shard_map/ppermute | solution.py:77
  82.3 50.2 %collective-permute-start.9 = (bf16[1,3,2,128,512]{4,3,2,1,0:T(8,128)(2,1)S(1)}, bf16[1,3,2,128,512]{4,3,2,1,0:T(8,128)(2,1)S(1)}, u32[]{:S(2)}, u32[]{:S(2)}) collective-permute-start(bf16[1,3,2,128,512]{4,3,2,1,0:T(8,128)(2,1)S(1)} %get-tuple-element.9), channel_id=1, source_target_pairs={{0,24},{8,0},{16,8},{24,16},{1,25},{9,1},{17,9},{25,17},{2,26},{10... | collective-permute-start | bytes 2359304 | tf_op jit(solution)/shard_map/ppermute | solution.py:19
  82.5 49.9 %collective-permute-start.8 = (bf16[1,3,2,128,512]{4,3,2,1,0:T(8,128)(2,1)S(1)}, bf16[1,3,2,128,512]{4,3,2,1,0:T(8,128)(2,1)S(1)}, u32[]{:S(2)}, u32[]{:S(2)}) collective-permute-start(bf16[1,3,2,128,512]{4,3,2,1,0:T(8,128)(2,1)S(1)} %get-tuple-element.10), channel_id=1, source_target_pairs={{0,16},{8,24},{16,0},{24,8},{1,17},{9,25},{17,1},{25,9},{2,18},{10... | collective-permute-start | bytes 2359304 | tf_op jit(solution)/shard_map/ppermute | solution.py:19
  84.1 48.4 %collective-permute-start.7 = (bf16[1,3,2,128,512]{4,3,2,1,0:T(8,128)(2,1)S(1)}, bf16[1,3,2,128,512]{4,3,2,1,0:T(8,128)(2,1)S(1)}, u32[]{:S(2)}, u32[]{:S(2)}) collective-permute-start(bf16[1,3,2,128,512]{4,3,2,1,0:T(8,128)(2,1)S(1)} %get-tuple-element.11), channel_id=1, source_target_pairs={{0,8},{8,16},{16,24},{24,0},{1,9},{9,17},{17,25},{25,1},{2,10},{10... | collective-permute-start | bytes 2359304 | tf_op jit(solution)/shard_map/ppermute | solution.py:19
  84.3 12.5 %collective-permute-start.11 = (bf16[24,7168]{1,0:T(8,128)(2,1)}, bf16[24,7168]{1,0:T(8,128)(2,1)S(1)}, u32[]{:S(2)}, u32[]{:S(2)}) collective-permute-start(bf16[24,7168]{1,0:T(8,128)(2,1)} %collective-permute-done.10), channel_id=1, source_target_pairs={{0,2},{1,3},{2,4},{3,5},{4,6},{5,7},{6,0},{7,1},{8,10},{9,11},{10,... | collective-permute-start | bytes 1032200 | tf_op jit(solution)/shard_map/ppermute | solution.py:77
  96.7 14.0 %collective-permute-start.12 = (bf16[24,7168]{1,0:T(8,128)(2,1)S(1)}, bf16[24,7168]{1,0:T(8,128)(2,1)}, u32[]{:S(2)}, u32[]{:S(2)}) collective-permute-start(bf16[24,7168]{1,0:T(8,128)(2,1)S(1)} %collective-permute-done.11), channel_id=1, source_target_pairs={{0,2},{1,3},{2,4},{3,5},{4,6},{5,7},{6,0},{7,1},{8,10},{9,11},{10,... | collective-permute-start | bytes 1032200 | tf_op jit(solution)/shard_map/ppermute | solution.py:77
  110.7 13.6 %collective-permute-start.14 = (bf16[24,7168]{1,0:T(8,128)(2,1)}, bf16[24,7168]{1,0:T(8,128)(2,1)S(1)}, u32[]{:S(2)}, u32[]{:S(2)}) collective-permute-start(bf16[24,7168]{1,0:T(8,128)(2,1)} %collective-permute-done.10), channel_id=1, source_target_pairs={{0,1},{1,0},{2,3},{3,2},{4,5},{5,4},{6,7},{7,6},{8,9},{9,8},{10,11... | collective-permute-start | bytes 1032200 | tf_op jit(solution)/shard_map/ppermute | solution.py:71
  117.0 14.7 %collective-permute-start.15 = (bf16[24,7168]{1,0:T(8,128)(2,1)S(1)}, bf16[24,7168]{1,0:T(8,128)(2,1)S(1)}, u32[]{:S(2)}, u32[]{:S(2)}) collective-permute-start(bf16[24,7168]{1,0:T(8,128)(2,1)S(1)} %collective-permute-done.11), channel_id=1, source_target_pairs={{0,1},{1,0},{2,3},{3,2},{4,5},{5,4},{6,7},{7,6},{8,9},{9,8},{10,11... | collective-permute-start | bytes 1032200 | tf_op jit(solution)/shard_map/ppermute | solution.py:71
  124.3 15.1 %collective-permute-start.16 = (bf16[24,7168]{1,0:T(8,128)(2,1)}, bf16[24,7168]{1,0:T(8,128)(2,1)}, u32[]{:S(2)}, u32[]{:S(2)}) collective-permute-start(bf16[24,7168]{1,0:T(8,128)(2,1)} %collective-permute-done.12), channel_id=1, source_target_pairs={{0,1},{1,0},{2,3},{3,2},{4,5},{5,4},{6,7},{7,6},{8,9},{9,8},{10,11... | collective-permute-start | bytes 1032200 | tf_op jit(solution)/shard_map/ppermute | solution.py:71
  132.9 2.4 %copy-start.10 = (pred[12]{0:T(512)(128)(4,1)S(1)}, pred[12]{0:T(512)(128)(4,1)}, u32[]{:S(2)}) copy-start(pred[12]{0:T(512)(128)(4,1)} %broadcast_in_dim.39) | copy-start | bytes 40
  135.3 4.1 %copy-start.5 = (bf16[192,7168]{1,0:T(8,128)(2,1)S(1)}, bf16[192,7168]{1,0:T(8,128)(2,1)}, u32[]{:S(2)}) copy-start(bf16[192,7168]{1,0:T(8,128)(2,1)} %constant_dynamic-update-slice_fusion.1) | copy-start | bytes 8257540
  135.3 5.1 %copy-start.11 = (f32[1536]{0:T(1024)S(1)}, f32[1536]{0:T(1024)}, u32[]{:S(2)}) copy-start(f32[1536]{0:T(1024)} %param.14) | copy-start | bytes 18436
  150.1 1.7 copy-start.2
  152.6 2.9 %slice-start = ((s8[7340032]{0:T(1024)(128)(4,1)}), s8[4194304]{0:T(1024)(128)(4,1)S(1)}, s32[]{:S(2)}) async-start(s8[7340032]{0:T(1024)(128)(4,1)} %bitcast.139), calls=%async_computation | async-start | bytes 8388608
  153.3 1.6 copy-start.3
  153.3 2.9 %slice-start.1 = ((s8[7340032]{0:T(1024)(128)(4,1)}), s8[3145728]{0:T(1024)(128)(4,1)S(1)}, s32[]{:S(2)}) async-start(s8[7340032]{0:T(1024)(128)(4,1)} %bitcast.139), calls=%async_computation.1 | async-start | bytes 6291456
  158.2 43.2 %copy-start.6 = (f32[7168]{0:T(1024)S(1)}, f32[7168]{0:T(1024)}, u32[]{:S(2)}) copy-start(f32[7168]{0:T(1024)} %param.16) | copy-start | bytes 86020
  158.3 11.1 %collective-permute-start.17 = (bf16[24,7168]{1,0:T(8,128)(2,1)S(1)}, bf16[24,7168]{1,0:T(8,128)(2,1)S(1)}, u32[]{:S(2)}, u32[]{:S(2)}) collective-permute-start(bf16[24,7168]{1,0:T(8,128)(2,1)S(1)} %get-tuple-element.12), channel_id=1, source_target_pairs={{0,1},{1,0},{2,3},{3,2},{4,5},{5,4},{6,7},{7,6},{8,9},{9,8},{10,11... | collective-permute-start | bytes 1032200 | tf_op jit(solution)/shard_map/ppermute | solution.py:71
  160.4 16.4 %collective-permute-start.19 = (bf16[24,7168]{1,0:T(8,128)(2,1)S(1)}, bf16[24,7168]{1,0:T(8,128)(2,1)S(1)}, u32[]{:S(2)}, u32[]{:S(2)}) collective-permute-start(bf16[24,7168]{1,0:T(8,128)(2,1)S(1)} %get-tuple-element.15), channel_id=1, source_target_pairs={{0,1},{1,0},{2,3},{3,2},{4,5},{5,4},{6,7},{7,6},{8,9},{9,8},{10,11... | collective-permute-start | bytes 1032200 | tf_op jit(solution)/shard_map/ppermute | solution.py:71
  169.5 10.7 %collective-permute-start.18 = (bf16[24,7168]{1,0:T(8,128)(2,1)S(1)}, bf16[24,7168]{1,0:T(8,128)(2,1)S(1)}, u32[]{:S(2)}, u32[]{:S(2)}) collective-permute-start(bf16[24,7168]{1,0:T(8,128)(2,1)S(1)} %fusion.32), channel_id=1, source_target_pairs={{0,2},{1,3},{2,4},{3,5},{4,6},{5,7},{6,0},{7,1},{8,10},{9,11},{10,... | collective-permute-start | bytes 1032200 | tf_op jit(solution)/shard_map/ppermute | solution.py:77
  169.9 14.3 %collective-permute-start.21 = (bf16[24,7168]{1,0:T(8,128)(2,1)S(1)}, bf16[24,7168]{1,0:T(8,128)(2,1)S(1)}, u32[]{:S(2)}, u32[]{:S(2)}) collective-permute-start(bf16[24,7168]{1,0:T(8,128)(2,1)S(1)} %get-tuple-element.14), channel_id=1, source_target_pairs={{0,1},{1,0},{2,3},{3,2},{4,5},{5,4},{6,7},{7,6},{8,9},{9,8},{10,11... | collective-permute-start | bytes 1032200 | tf_op jit(solution)/shard_map/ppermute | solution.py:71
  180.3 11.8 %collective-permute-start.20 = (bf16[24,7168]{1,0:T(8,128)(2,1)S(1)}, bf16[24,7168]{1,0:T(8,128)(2,1)S(1)}, u32[]{:S(2)}, u32[]{:S(2)}) collective-permute-start(bf16[24,7168]{1,0:T(8,128)(2,1)S(1)} %fusion.30), channel_id=1, source_target_pairs={{0,2},{1,3},{2,4},{3,5},{4,6},{5,7},{6,0},{7,1},{8,10},{9,11},{10,... | collective-permute-start | bytes 1032200 | tf_op jit(solution)/shard_map/ppermute | solution.py:77
  180.3 12.0 %collective-permute-start.23 = (bf16[24,7168]{1,0:T(8,128)(2,1)S(1)}, bf16[24,7168]{1,0:T(8,128)(2,1)S(1)}, u32[]{:S(2)}, u32[]{:S(2)}) collective-permute-start(bf16[24,7168]{1,0:T(8,128)(2,1)S(1)} %get-tuple-element.13), channel_id=1, source_target_pairs={{0,1},{1,0},{2,3},{3,2},{4,5},{5,4},{6,7},{7,6},{8,9},{9,8},{10,11... | collective-permute-start | bytes 1032200 | tf_op jit(solution)/shard_map/ppermute | solution.py:71
  192.2 9.1 %collective-permute-start.22 = (bf16[24,7168]{1,0:T(8,128)(2,1)S(1)}, bf16[24,7168]{1,0:T(8,128)(2,1)S(1)}, u32[]{:S(2)}, u32[]{:S(2)}) collective-permute-start(bf16[24,7168]{1,0:T(8,128)(2,1)S(1)} %fusion.27), channel_id=1, source_target_pairs={{0,2},{1,3},{2,4},{3,5},{4,6},{5,7},{6,0},{7,1},{8,10},{9,11},{10,... | collective-permute-start | bytes 1032200 | tf_op jit(solution)/shard_map/ppermute | solution.py:77

commit v2 on v1

v2 whole, which is shorter than its diff:
```python
import jax
import jax.numpy as jnp
from jax import lax
from jax.sharding import PartitionSpec as P

HD = 128
RELAY_STEP = 3


def normalize(x, gain, shift):
    mean = jnp.mean(x, axis=-1, keepdims=True)
    var = jnp.mean((x - mean) * (x - mean), axis=-1, keepdims=True)
    return ((x - mean) * lax.rsqrt(var + 1e-05) * gain + shift).astype(jnp.bfloat16)


def shifted(x, axis, k, n):
    return lax.ppermute(x, axis, [(j, (j + k) % n) for j in range(n)])


def split_heads(prefill_cache):
    tensor_count = lax.axis_size("tensor")
    layers, _, two, blk, width = prefill_cache.shape
    local_heads = width // tensor_count // HD
    split = prefill_cache.reshape(layers, two, blk, tensor_count, local_heads, HD)
    return jnp.transpose(split, (0, 1, 4, 3, 2, 5))


def send_decode(per_head_rows, block_dest):
    layers, two, local_heads, row_blocks, blk, _ = per_head_rows.shape
    pipe_count = lax.axis_size("pipe")
    capacity = 3 * row_blocks // (2 * pipe_count)
    dest = block_dest[:, :, 0]
    onehot = (dest[:, :, None] == jnp.arange(pipe_count, dtype=jnp.int32)[None, None, :]).astype(
        jnp.int32
    )
    earlier_tokens = jnp.cumsum(onehot, axis=1) - onehot
    slot = jnp.sum(earlier_tokens * onehot, axis=-1)
    position = dest * capacity + slot
    i = lax.axis_index("pipe")
    outgoing = []
    for k in range(pipe_count):
        targets = ((i + k) % pipe_count) * capacity + jnp.arange(capacity, dtype=jnp.int32)
        placement_index = (position[:, None, :] == targets[None, :, None]).astype(jnp.bfloat16)
        piece = jnp.einsum(
            "gud,gohdtc->guothc", placement_index, per_head_rows, preferred_element_type=jnp.float32
        ).astype(jnp.bfloat16)
        outgoing.append(piece.reshape((layers, capacity, two, blk, local_heads * HD)))
    return outgoing


def receive_decode(outgoing):
    pipe_count = lax.axis_size("pipe")
    i = lax.axis_index("pipe")
    layers, capacity = outgoing[0].shape[:2]
    arrived = jnp.zeros((layers, pipe_count * capacity) + outgoing[0].shape[2:], outgoing[0].dtype)
    for k in range(pipe_count):
        piece = outgoing[k] if k == 0 else shifted(outgoing[k], "pipe", k, pipe_count)
        arrived = lax.dynamic_update_slice_in_dim(
            arrived, piece, ((i - k) % pipe_count) * capacity, axis=1
        )
    return arrived

def partner(x):
    tensor_count = lax.axis_size("tensor")
    return lax.ppermute(x, "tensor", [(j, j ^ 1) for j in range(tensor_count)])


def ring(x):
    tensor_count = lax.axis_size("tensor")
    rows = tensor_count // 2
    return lax.ppermute(
        x, "tensor", [(j, ((j // 2 + 1) % rows) * 2 + j % 2) for j in range(tensor_count)]
    )


def gather_tokens(x):
    tensor_count = lax.axis_size("tensor")
    rows = tensor_count // 2
    i = lax.axis_index("tensor")
    outer, inner = i // 2, i % 2
    own = [x]
    for _ in range(1, rows):
        own.append(ring(own[-1]))
    other = [partner(piece) for piece in own]
    steps = jnp.arange(rows)
    source = jnp.concatenate(
        [((outer - steps) % rows) * 2 + inner, ((outer - steps) % rows) * 2 + (1 - inner)]
    )
    return jnp.concatenate(own + other, axis=0), source


def scatter_tokens(partial, rider):
    tensor_count = lax.axis_size("tensor")
    rows = tensor_count // 2
    blocks = partial.reshape((2, rows, -1) + partial.shape[1:])
    mine = [
        blocks[0, s] + partner(blocks[1, s].astype(jnp.bfloat16)).astype(jnp.float32)
        for s in range(rows)
    ]
    carried = mine[1 % rows]
    for k in range(1, rows):
        if k == RELAY_STEP:
            carried, rider = lax.optimization_barrier((carried, rider))
        arrived = ring(carried.astype(jnp.bfloat16)).astype(jnp.float32)
        carried = arrived + mine[(k + 1) % rows]
    return carried, rider


def local(
    stretch,
    ln_gain,
    ln_bias,
    qkv_weight,
    qkv_bias,
    out_weight,
    out_bias,
    segment_ids,
    prefill_cache,
    block_dest,
):
    hidden = stretch.astype(jnp.float32)
    head_count = qkv_weight.shape[1] // (3 * HD)
    normed = normalize(hidden, ln_gain, ln_bias)
    gathered, source = gather_tokens(normed)
    split = split_heads(prefill_cache)
    gathered, split = lax.optimization_barrier((gathered, split))
    per_head_rows = lax.all_to_all(split, "tensor", split_axis=3, concat_axis=3, tiled=True)
    outgoing = send_decode(per_head_rows, block_dest)
    qkv = (
        jnp.dot(gathered, qkv_weight, preferred_element_type=jnp.float32) + qkv_bias
    ).astype(jnp.bfloat16)
    group_tokens = qkv.shape[0]
    place = (source[:, None] * normed.shape[0] + jnp.arange(normed.shape[0])[None, :]).reshape(-1)
    first_segment = segment_ids[0]
    segment_ids = segment_ids[place]
    heads = qkv.reshape(group_tokens, head_count, 3, HD)
    query = heads[:, :, 0]
    keys = heads[:, :, 1]
    value_rows = heads[:, :, 2]
    finished = per_head_rows[0]
    prefix_length = finished.shape[2] * finished.shape[3]
    cached_keys = finished[0].reshape(head_count, prefix_length, HD)
    old_values = finished[1].reshape(head_count, prefix_length, HD)
    scale = HD ** (-0.5)
    own_scores = jnp.einsum("qhd,khd->hqk", query, keys, preferred_element_type=jnp.float32) * scale
    old_scores = (
        jnp.einsum("qhd,hkd->hqk", query, cached_keys, preferred_element_type=jnp.float32) * scale
    )
    own_visible = (segment_ids[:, None] == segment_ids[None, :]) & (
        place[None, :] <= place[:, None]
    )
    old_visible = (segment_ids == first_segment)[:, None]
    own_scores = jnp.where(own_visible[None], own_scores, -jnp.inf)
    old_scores = jnp.where(old_visible[None], old_scores, -jnp.inf)
    scores = jnp.concatenate([old_scores, own_scores], axis=2)
    weights = jax.nn.softmax(scores, axis=-1).astype(jnp.bfloat16)
    context = jnp.einsum(
        "hqk,hkd->qhd",
        weights[:, :, :prefix_length],
        old_values,
        preferred_element_type=jnp.float32,
    )
    context = context + jnp.einsum(
        "hqk,khd->qhd",
        weights[:, :, prefix_length:],
        value_rows,
        preferred_element_type=jnp.float32,
    )
    context = context.astype(jnp.bfloat16).reshape(group_tokens, head_count * HD)
    decode_side_cache = receive_decode(outgoing)
    summed, decode_side_cache = scatter_tokens(
        jnp.dot(context, out_weight, preferred_element_type=jnp.float32), decode_side_cache
    )
    mixed = (hidden + summed + out_bias).astype(jnp.bfloat16)
    return (mixed, decode_side_cache)


def solution(mesh):
    return jax.shard_map(
        local,
        mesh=mesh,
        in_specs=(
            P(("pipe", "tensor"), None),
            P(),
            P(),
            P(None, "tensor"),
            P("tensor"),
            P("tensor", None),
            P(),
            P("pipe"),
            P(None, ("pipe", "tensor"), None, None, None),
            P(None, "pipe", None),
        ),
        out_specs=(P(("pipe", "tensor"), None), P(None, "pipe", None, None, "tensor")),
        check_vma=False,
    )
```

time: 205 us -> 170 us (0.83)
  starting transfers between devices: 49.7 us -> 18.1 us
  local copies, waits for them, and re-layouts: 59.7 us -> 31.2 us
  matrix products: 14.9 us -> 29.5 us
  other arithmetic: 10.4 us -> 17.1 us
  waiting for transfers between devices: 66.2 us -> 72.3 us
    another operation x11 -> x0, local copies, waits for them, and re-layouts: 22.8 us -> none  [the longest x9 20.2 us: gather_heads(): rows = jnp.stack(arrived, axis=1)]
    all_to_all x0 -> x1, waiting for transfers between devices: none -> 22.7 us  [local(): lax.all_to_all(split, 'tensor', split_axis=3, concat_axis=3, tiled=True)]
    ppermute x6, starting transfers between devices: 19.7 us -> 1.65 us  [ring(): lax.ppermute(x, 'tensor', [(j, (j // 2 + 1) % rows * 2 + j % 2) for j in...]
    ppermute x8, waiting for transfers between devices: 24.4 us -> 10.9 us  [partner(): return lax.ppermute(x, 'tensor', [(j, j ^ 1) for j in range(tensor_count)])]
    ppermute x10 -> x3, starting transfers between devices: 15.8 us -> 3.01 us  [shifted(): return lax.ppermute(x, axis, [(j, (j + k) % n) for j in range(n)])]
    dynamic_slice x9 -> x0, local copies, waits for them, and re-layouts: 8.99 us -> none  [the longest x8 8.66 us: gather_heads(): lax.dynamic_index_in_dim(chunks, (i + k) % tensor_count, 3, keepdims=False)]
    slice x3, local copies, waits for them, and re-layouts: 5.95 us -> 0.31 us  [the longest x2 0.21 us: local(): old_values = finished[1].reshape(head_count, prefix_length, HD)]
    dot_general x1, matrix products: 1.6 us -> 7.12 us  [local(): jnp.dot(context, out_weight, preferred_element_type=jnp.float32)]
  transfers between devices with their start and end apart: 24 -> 18, of which waited for: 11 -> 10; matrix products, arithmetic and copies ran while one was open for 30% -> 37% of each run, Pallas kernels for 0% -> 0%
where the time goes in v2:
time: 170 us; the launch traced here: 169 us
  waiting for transfers between devices  72.3 us (43%)
  local copies, waits for them, and re-layouts  31.2 us (18%)
  matrix products  29.5 us (17%)
  starting transfers between devices  18.1 us (11%)
  other arithmetic  17.1 us (10%)
    ppermute x6, waiting for transfers between devices, ring(): lax.ppermute(x, 'tensor', [(j, (j // 2 + 1) % rows * 2 + j % 2) for j in...  38.7 us
    all_to_all x1, waiting for transfers between devices, local(): lax.all_to_all(split, 'tensor', split_axis=3, concat_axis=3, tiled=True)  22.7 us
    dot_general x1, matrix products, local(): jnp.dot(gathered, qkv_weight, preferred_element_type=jnp.float32) + qkv_bias  12.5 us
    ppermute x8, waiting for transfers between devices, partner(): return lax.ppermute(x, 'tensor', [(j, j ^ 1) for j in range(tensor_count)])  10.9 us
    ppermute x8, starting transfers between devices, partner(): return lax.ppermute(x, 'tensor', [(j, j ^ 1) for j in range(tensor_count)])  9.75 us
    unnamed x33, local copies, waits for them, and re-layouts  9.22 us
    dot_general x1, matrix products, local(): jnp.dot(context, out_weight, preferred_element_type=jnp.float32)  7.12 us
    dot_general x4, matrix products, send_decode(): jnp.einsum('gud,gohdtc->guothc', placement_index, per_head_rows, preferre...  6.4 us
  transfers between devices with their start and end apart: 18, of which 10 were waited for; matrix products, arithmetic and copies ran while one was open for 37% of the time, Pallas kernels for 0%

profile of v2, /device:TPU:0, one launch (start us, length us, event | category | flops | bytes accessed | tf_op | source)
XLA Modules:
  0.0 169.3 jit_solution(12857148127494631812)
XLA Ops:
  0.6 1.1 convert_reduce_fusion
  1.8 1.2 fusion.55
  3.1 1.9 %constant_dynamic-update-slice_fusion.7 = (bf16[192,7168]{1,0:T(8,128)(2,1)}, bf16[24,7168]{1,0:T(8,128)(2,1)S(1)}) fusion(f32[7168]{0:T(1024)} %param.12, f32[7168]{0:T(1024)} %param.11, f32[24]{0:T(128)S(1)} %add_rsqrt_fusion, f32[24]{0:T(128)S(1)} %broadcast_multiply_fusion, bf16[24,7168]{1,0:T(8,128)(2,1)} %param.10), kind=kLoop, calls=%fused_computation.78 | loop fusion | flops 1032191 | bytes 1089728
  5.0 3.0 %collective-permute-start.3 = (bf16[24,7168]{1,0:T(8,128)(2,1)S(1)}, bf16[24,7168]{1,0:T(8,128)(2,1)S(1)}, u32[]{:S(2)}, u32[]{:S(2)}) collective-permute-start(bf16[24,7168]{1,0:T(8,128)(2,1)S(1)} %get-tuple-element.11), channel_id=1, source_target_pairs={{0,1},{1,0},{2,3},{3,2},{4,5},{5,4},{6,7},{7,6},{8,9},{9,8},{10,11... | collective-permute-start | bytes 1032200 | tf_op jit(solution)/shard_map/ppermute | solution.py:65
  8.0 1.6 collective-permute-start
  10.9 3.1 %copy.50 = bf16[1,1,2,128,4096]{3,4,2,1,0:T(8,128)(2,1)S(1)} copy(bf16[1,1,2,128,4096]{4,3,2,1,0:T(8,128)(2,1)} %param.18) | data formatting | bytes 4194304 | tf_op args[8]
  14.1 5.3 %collective-permute-done = bf16[24,7168]{1,0:T(8,128)(2,1)S(1)} collective-permute-done((bf16[24,7168]{1,0:T(8,128)(2,1)S(1)}, bf16[24,7168]{1,0:T(8,128)(2,1)S(1)}, u32[]{:S(2)}, u32[]{:S(2)}) %collective-permute-start) | collective-permute-done | bytes 344096 | tf_op jit(solution)/shard_map/ppermute | solution.py:71
  20.6 9.7 %collective-permute-done.1 = bf16[24,7168]{1,0:T(8,128)(2,1)S(1)} collective-permute-done((bf16[24,7168]{1,0:T(8,128)(2,1)S(1)}, bf16[24,7168]{1,0:T(8,128)(2,1)S(1)}, u32[]{:S(2)}, u32[]{:S(2)}) %collective-permute-start.1) | collective-permute-done | bytes 344096 | tf_op jit(solution)/shard_map/ppermute | solution.py:71
  30.3 1.3 collective-permute-start.5
  32.3 8.3 %collective-permute-done.2 = bf16[24,7168]{1,0:T(8,128)(2,1)S(1)} collective-permute-done((bf16[24,7168]{1,0:T(8,128)(2,1)S(1)}, bf16[24,7168]{1,0:T(8,128)(2,1)S(1)}, u32[]{:S(2)}, u32[]{:S(2)}) %collective-permute-start.2) | collective-permute-done | bytes 344096 | tf_op jit(solution)/shard_map/ppermute | solution.py:71
  40.6 1.0 collective-permute-start.6
  44.6 3.3 %collective-permute-done.6 = bf16[24,7168]{1,0:T(8,128)(2,1)S(1)} collective-permute-done((bf16[24,7168]{1,0:T(8,128)(2,1)S(1)}, bf16[24,7168]{1,0:T(8,128)(2,1)S(1)}, u32[]{:S(2)}, u32[]{:S(2)}) %collective-permute-start.6) | collective-permute-done | bytes 344096 | tf_op jit(solution)/shard_map/ppermute | solution.py:65
  48.6 2.6 %copy.51 = bf16[1,2,4,8,128,128]{5,4,2,1,0,3:T(8,128)(2,1)} copy(bf16[1,2,4,8,128,128]{4,5,2,3,1,0:T(8,128)(2,1)S(1)} %bitcast.140) | data formatting | bytes 4194304 | tf_op jit(solution)/shard_map/optimization_barrier | solution.py:126
  51.2 3.7 %all-to-all-start = ((bf16[1,2,4,8,128,128]{5,4,2,1,0,3:T(8,128)(2,1)}), bf16[1,2,4,8,128,128]{5,4,2,1,0,3:T(8,128)(2,1)S(1)}, u32[]{:S(2)}, u32[]{:S(2)}) async-start(bf16[1,2,4,8,128,128]{5,4,2,1,0,3:T(8,128)(2,1)} %copy.51), calls=%async_computation | async-start | bytes 4194304 | tf_op jit(solution)/shard_map/all_to_all | solution.py:127
  56.4 1.6 gather_fusion
  59.4 12.5 %fusion.4 = bf16[192,1536]{1,0:T(8,128)(2,1)S(1)} fusion(bf16[192,7168]{1,0:T(8,128)(2,1)} %constant_dynamic-update-slice_fusion, bf16[7168,1536]{1,0:T(8,128)(2,1)} %param.13, f32[1536]{0:T(1024)S(1)} %copy-done.12), kind=kOutput, calls=%fused_computation.9 | convolution fusion | flops 4228448256 | bytes 25368576 | tf_op jit(solution)/shard_map/dot_general | solution.py:130
  72.4 0.8 fusion.93
  74.0 2.0 %fusion.95 = (f32[4,192]{1,0:T(4,128)S(1)}, f32[4,192,192]{2,1,0:T(8,128)}) fusion(bf16[192,4,1,128]{3,2,1,0:T(2,128)(2,1)S(1)} %get-tuple-element.19, bf16[192,4,1,128]{3,2,1,0:T(2,128)(2,1)S(1)} %get-tuple-element.20, pred[192,192]{1,0:T(8,128)(4,1)} %compare_and_fusion), kind=kOutput, calls=%fused_computation.124 | convolution fusion | flops 38190336 | bytes 1022976 | tf_op jit(solution)/shard_map/qhd,khd->hqk/dot_general | solution.py:145
  76.0 22.7 %all-to-all-done = bf16[1,2,4,8,128,128]{5,4,2,1,0,3:T(8,128)(2,1)S(1)} async-done(((bf16[1,2,4,8,128,128]{5,4,2,1,0,3:T(8,128)(2,1)}), bf16[1,2,4,8,128,128]{5,4,2,1,0,3:T(8,128)(2,1)S(1)}, u32[]{:S(2)}, u32[]{:S(2)}) %all-to-all-start) | async-done | bytes 2097184 | tf_op jit(solution)/shard_map/all_to_all | solution.py:127
  98.7 2.0 %fusion.30 = bf16[1,3,2,128,4,128]{5,1,3,4,2,0:T(4,128)(2,1)S(1)} fusion(bf16[1,2,4,8,128,128]{5,4,2,1,0,3:T(8,128)(2,1)S(1)} %all-to-all-done, s32[8]{0:T(128)S(1)} %multiply_add_fusion, s32[3]{0:T(128)} %iota_add_fusion.2), kind=kOutput, calls=%fused_computation.25 | convolution fusion | flops 6684696 | bytes 2883628 | tf_op jit(solution)/shard_map/gud,gohdtc->guothc/dot_general | solution.py:44
  100.8 1.4 copy.63
  102.1 1.5 collective-permute-start.13
  106.2 1.0 divide_convert_fusion
  108.3 7.1 %fusion.96 = (bf16[2,4,24,7168]{3,2,1,0:T(8,128)(2,1)S(1)}, f32[2,4,24,7168]{3,2,1,0:T(8,128)}) fusion(bf16[2,4,24,512]{3,2,1,0:T(8,128)(2,1)S(1)} %dot_general.37, bf16[512,7168]{1,0:T(8,128)(2,1)} %param.15), kind=kOutput, calls=%fused_computation.125 | convolution fusion | flops 1410662400 | bytes 15794176 | tf_op jit(solution)/shard_map/dot_general | solution.py:172
  115.4 1.1 slice_bitcast_fusion.7
  116.5 1.3 collective-permute-start.7
  117.8 1.4 fusion.33
  119.3 1.3 copy.61
  120.6 1.4 fusion.36
  122.1 1.3 copy.59
  123.4 2.3 %copy.60 = bf16[1,3,2,128,512]{4,3,2,1,0:T(8,128)(2,1)} copy(bf16[1,3,2,128,512]{3,4,2,1,0:T(8,128)(2,1)} %bitcast.142) | data formatting | bytes 1572864 | tf_op jit(solution)/shard_map/reshape | solution.py:47
  126.5 2.0 %fusion.69 = bf16[24,7168]{1,0:T(8,128)(2,1)} fusion(f32[2,4,24,7168]{3,2,1,0:T(8,128)} %get-tuple-element.26, bf16[24,7168]{1,0:T(8,128)(2,1)} %collective-permute-done.7), kind=kLoop, calls=%fused_computation.60 | loop fusion | flops 516096 | bytes 1376256 | tf_op jit(solution)/shard_map/convert_element_type | solution.py:104
  128.5 1.4 fusion.27
  130.7 1.5 collective-permute-start.14
  132.6 3.9 %collective-permute-done.9 = bf16[24,7168]{1,0:T(8,128)(2,1)S(1)} collective-permute-done((bf16[24,7168]{1,0:T(8,128)(2,1)}, bf16[24,7168]{1,0:T(8,128)(2,1)S(1)}, u32[]{:S(2)}, u32[]{:S(2)}) %collective-permute-start.9) | collective-permute-done | bytes 344096 | tf_op jit(solution)/shard_map/ppermute | solution.py:65
  137.3 3.6 %collective-permute-done.8 = bf16[24,7168]{1,0:T(8,128)(2,1)} collective-permute-done((bf16[24,7168]{1,0:T(8,128)(2,1)}, bf16[24,7168]{1,0:T(8,128)(2,1)}, u32[]{:S(2)}, u32[]{:S(2)}) %collective-permute-start.8) | collective-permute-done | bytes 344096 | tf_op jit(solution)/shard_map/ppermute | solution.py:71
  140.9 1.3 collective-permute-start.11
  142.2 2.1 %fusion.67 = bf16[24,7168]{1,0:T(8,128)(2,1)} fusion(f32[2,4,24,7168]{3,2,1,0:T(8,128)} %get-tuple-element.26, bf16[24,7168]{1,0:T(8,128)(2,1)} %copy-done.7, bf16[24,7168]{1,0:T(8,128)(2,1)} %collective-permute-done.8), kind=kLoop, calls=%fused_computation.57 | loop fusion | flops 860160 | bytes 1720320 | tf_op jit(solution)/shard_map/convert_element_type | solution.py:104
  144.4 1.4 copy.64
  145.8 1.4 copy.62
  147.5 0.9 constant_dynamic-update-slice_fusion.10
  148.5 0.9 constant_dynamic-update-slice_fusion.9
  149.4 0.9 constant_dynamic-update-slice_fusion.8
  150.3 3.7 %collective-permute-done.11 = bf16[24,7168]{1,0:T(8,128)(2,1)S(1)} collective-permute-done((bf16[24,7168]{1,0:T(8,128)(2,1)}, bf16[24,7168]{1,0:T(8,128)(2,1)S(1)}, u32[]{:S(2)}, u32[]{:S(2)}) %collective-permute-start.11) | collective-permute-done | bytes 344096 | tf_op jit(solution)/shard_map/ppermute | solution.py:65
  154.0 1.7 collective-permute-done.10
  155.7 1.3 fusion.64
  157.1 10.1 %collective-permute-done.15 = bf16[24,7168]{1,0:T(8,128)(2,1)S(1)} collective-permute-done((bf16[24,7168]{1,0:T(8,128)(2,1)S(1)}, bf16[24,7168]{1,0:T(8,128)(2,1)S(1)}, u32[]{:S(2)}, u32[]{:S(2)}) %collective-permute-start.15) | collective-permute-done | bytes 344096 | tf_op jit(solution)/shard_map/ppermute | solution.py:71
  167.2 2.1 %fusion.60 = bf16[24,7168]{1,0:T(8,128)(2,1)} fusion(bf16[24,7168]{1,0:T(8,128)(2,1)S(1)} %copy-done.1, f32[2,4,24,7168]{3,2,1,0:T(8,128)} %get-tuple-element.26, bf16[24,7168]{1,0:T(8,128)(2,1)} %collective-permute-done.16, bf16[24,7168]{1,0:T(8,128)(2,1)S(1)} %collective-permute-done.15, f32[7168]{0:T(1024)S(1)} %copy-done.8), kind=kLoop, calls=%fused_computation.47 | loop fusion | flops 1376256 | bytes 2093056 | tf_op jit(solution)/shard_map/convert_element_type | solution.py:174
  (85 shorter events, 17.7 us)
Async XLA Ops:
  3.0 11.0 %copy-start.9 = (s32[1,8,1]{1,2,0:T(1,128)S(1)}, s32[1,8,1]{1,2,0:T(1,128)}, u32[]{:S(2)}) copy-start(s32[1,8,1]{1,2,0:T(1,128)} %param.19) | copy-start | bytes 100
  5.0 37.3 %collective-permute-start.3 = (bf16[24,7168]{1,0:T(8,128)(2,1)S(1)}, bf16[24,7168]{1,0:T(8,128)(2,1)S(1)}, u32[]{:S(2)}, u32[]{:S(2)}) collective-permute-start(bf16[24,7168]{1,0:T(8,128)(2,1)S(1)} %get-tuple-element.11), channel_id=1, source_target_pairs={{0,1},{1,0},{2,3},{3,2},{4,5},{5,4},{6,7},{7,6},{8,9},{9,8},{10,11... | collective-permute-start | bytes 1032200 | tf_op jit(solution)/shard_map/ppermute | solution.py:65
  8.0 11.4 %collective-permute-start = (bf16[24,7168]{1,0:T(8,128)(2,1)S(1)}, bf16[24,7168]{1,0:T(8,128)(2,1)S(1)}, u32[]{:S(2)}, u32[]{:S(2)}) collective-permute-start(bf16[24,7168]{1,0:T(8,128)(2,1)S(1)} %get-tuple-element.11), channel_id=1, source_target_pairs={{0,2},{1,3},{2,4},{3,5},{4,6},{5,7},{6,0},{7,1},{8,10},{9,11},{10,... | collective-permute-start | bytes 1032200 | tf_op jit(solution)/shard_map/ppermute | solution.py:71
  19.3 23.7 %collective-permute-start.4 = (bf16[24,7168]{1,0:T(8,128)(2,1)S(1)}, bf16[24,7168]{1,0:T(8,128)(2,1)S(1)}, u32[]{:S(2)}, u32[]{:S(2)}) collective-permute-start(bf16[24,7168]{1,0:T(8,128)(2,1)S(1)} %collective-permute-done), channel_id=1, source_target_pairs={{0,1},{1,0},{2,3},{3,2},{4,5},{5,4},{6,7},{7,6},{8,9},{9,8},{10,11... | collective-permute-start | bytes 1032200 | tf_op jit(solution)/shard_map/ppermute | solution.py:65
  19.8 10.4 %collective-permute-start.1 = (bf16[24,7168]{1,0:T(8,128)(2,1)S(1)}, bf16[24,7168]{1,0:T(8,128)(2,1)S(1)}, u32[]{:S(2)}, u32[]{:S(2)}) collective-permute-start(bf16[24,7168]{1,0:T(8,128)(2,1)S(1)} %collective-permute-done), channel_id=1, source_target_pairs={{0,2},{1,3},{2,4},{3,5},{4,6},{5,7},{6,0},{7,1},{8,10},{9,11},{10,... | collective-permute-start | bytes 1032200 | tf_op jit(solution)/shard_map/ppermute | solution.py:71
  30.3 13.5 %collective-permute-start.5 = (bf16[24,7168]{1,0:T(8,128)(2,1)S(1)}, bf16[24,7168]{1,0:T(8,128)(2,1)S(1)}, u32[]{:S(2)}, u32[]{:S(2)}) collective-permute-start(bf16[24,7168]{1,0:T(8,128)(2,1)S(1)} %collective-permute-done.1), channel_id=1, source_target_pairs={{0,1},{1,0},{2,3},{3,2},{4,5},{5,4},{6,7},{7,6},{8,9},{9,8},{10,11... | collective-permute-start | bytes 1032200 | tf_op jit(solution)/shard_map/ppermute | solution.py:65
  31.6 9.0 %collective-permute-start.2 = (bf16[24,7168]{1,0:T(8,128)(2,1)S(1)}, bf16[24,7168]{1,0:T(8,128)(2,1)S(1)}, u32[]{:S(2)}, u32[]{:S(2)}) collective-permute-start(bf16[24,7168]{1,0:T(8,128)(2,1)S(1)} %collective-permute-done.1), channel_id=1, source_target_pairs={{0,2},{1,3},{2,4},{3,5},{4,6},{5,7},{6,0},{7,1},{8,10},{9,11},{10,... | collective-permute-start | bytes 1032200 | tf_op jit(solution)/shard_map/ppermute | solution.py:71
  40.6 7.2 %collective-permute-start.6 = (bf16[24,7168]{1,0:T(8,128)(2,1)S(1)}, bf16[24,7168]{1,0:T(8,128)(2,1)S(1)}, u32[]{:S(2)}, u32[]{:S(2)}) collective-permute-start(bf16[24,7168]{1,0:T(8,128)(2,1)S(1)} %collective-permute-done.2), channel_id=1, source_target_pairs={{0,1},{1,0},{2,3},{3,2},{4,5},{5,4},{6,7},{7,6},{8,9},{9,8},{10,11... | collective-permute-start | bytes 1032200 | tf_op jit(solution)/shard_map/ppermute | solution.py:65
  51.2 4.4 %copy-start = (s32[192]{0:T(256)S(1)}, s32[192]{0:T(256)}, u32[]{:S(2)}) copy-start(s32[192]{0:T(256)} %param.17) | copy-start | bytes 2308
  51.2 8.2 %copy-start.12 = (f32[1536]{0:T(1024)S(1)}, f32[1536]{0:T(1024)}, u32[]{:S(2)}) copy-start(f32[1536]{0:T(1024)} %param.14) | copy-start | bytes 18436
  51.2 47.5 %all-to-all-start = ((bf16[1,2,4,8,128,128]{5,4,2,1,0,3:T(8,128)(2,1)}), bf16[1,2,4,8,128,128]{5,4,2,1,0,3:T(8,128)(2,1)S(1)}, u32[]{:S(2)}, u32[]{:S(2)}) async-start(bf16[1,2,4,8,128,128]{5,4,2,1,0,3:T(8,128)(2,1)} %copy.51), calls=%async_computation | async-start | bytes 4194304 | tf_op jit(solution)/shard_map/all_to_all | solution.py:127
  73.3 0.7 copy-start.5
  102.1 42.2 %collective-permute-start.13 = (bf16[1,3,2,128,512]{3,4,2,1,0:T(8,128)(2,1)}, bf16[1,3,2,128,512]{3,4,2,1,0:T(8,128)(2,1)}, u32[]{:S(2)}, u32[]{:S(2)}) collective-permute-start(bf16[1,3,2,128,512]{3,4,2,1,0:T(8,128)(2,1)} %bitcast.144), channel_id=1, source_target_pairs={{0,16},{8,24},{16,0},{24,8},{1,17},{9,25},{17,1},{25,9},{2,18},{10... | collective-permute-start | bytes 2359304 | tf_op jit(solution)/shard_map/ppermute | solution.py:17
  103.7 1.0 copy-start.6
  103.8 1.6 copy-start.4
  115.4 2.4 %copy-start.10 = (s32[3]{0:T(128)S(1)}, s32[3]{0:T(128)}, u32[]{:S(2)}) copy-start(s32[3]{0:T(128)} %iota_add_fusion.3) | copy-start | bytes 40
  116.5 10.0 %collective-permute-start.7 = (bf16[24,7168]{1,0:T(8,128)(2,1)}, bf16[24,7168]{1,0:T(8,128)(2,1)}, u32[]{:S(2)}, u32[]{:S(2)}) collective-permute-start(bf16[24,7168]{1,0:T(8,128)(2,1)} %get-tuple-element.12), channel_id=1, source_target_pairs={{0,1},{1,0},{2,3},{3,2},{4,5},{5,4},{6,7},{7,6},{8,9},{9,8},{10,11... | collective-permute-start | bytes 1032200 | tf_op jit(solution)/shard_map/ppermute | solution.py:65
  120.6 25.2 %collective-permute-start.12 = (bf16[1,3,2,128,512]{3,4,2,1,0:T(8,128)(2,1)}, bf16[1,3,2,128,512]{3,4,2,1,0:T(8,128)(2,1)}, u32[]{:S(2)}, u32[]{:S(2)}) collective-permute-start(bf16[1,3,2,128,512]{3,4,2,1,0:T(8,128)(2,1)} %bitcast.145), channel_id=1, source_target_pairs={{0,8},{8,16},{16,24},{24,0},{1,9},{9,17},{17,25},{25,1},{2,10},{10... | collective-permute-start | bytes 2359304 | tf_op jit(solution)/shard_map/ppermute | solution.py:17
  122.1 6.4 %copy-start.11 = (s32[3]{0:T(128)S(1)}, s32[3]{0:T(128)}, u32[]{:S(2)}) copy-start(s32[3]{0:T(128)} %iota_add_fusion.1) | copy-start | bytes 40
  125.8 10.8 %collective-permute-start.9 = (bf16[24,7168]{1,0:T(8,128)(2,1)}, bf16[24,7168]{1,0:T(8,128)(2,1)S(1)}, u32[]{:S(2)}, u32[]{:S(2)}) collective-permute-start(bf16[24,7168]{1,0:T(8,128)(2,1)} %get-tuple-element.15), channel_id=1, source_target_pairs={{0,1},{1,0},{2,3},{3,2},{4,5},{5,4},{6,7},{7,6},{8,9},{9,8},{10,11... | collective-permute-start | bytes 1032200 | tf_op jit(solution)/shard_map/ppermute | solution.py:65
  128.5 12.4 %collective-permute-start.8 = (bf16[24,7168]{1,0:T(8,128)(2,1)}, bf16[24,7168]{1,0:T(8,128)(2,1)}, u32[]{:S(2)}, u32[]{:S(2)}) collective-permute-start(bf16[24,7168]{1,0:T(8,128)(2,1)} %fusion.69), channel_id=1, source_target_pairs={{0,2},{1,3},{2,4},{3,5},{4,6},{5,7},{6,0},{7,1},{8,10},{9,11},{10,... | collective-permute-start | bytes 1032200 | tf_op jit(solution)/shard_map/ppermute | solution.py:71
  130.0 2.6 %copy-start.2 = (bf16[1,3,2,128,512]{4,3,2,1,0:T(8,128)(2,1)S(1)}, bf16[1,3,2,128,512]{4,3,2,1,0:T(8,128)(2,1)}, u32[]{:S(2)}) copy-start(bf16[1,3,2,128,512]{4,3,2,1,0:T(8,128)(2,1)} %copy.60) | copy-start | bytes 2359300
  130.7 16.5 %collective-permute-start.14 = (bf16[1,3,2,128,512]{3,4,2,1,0:T(8,128)(2,1)S(1)}, bf16[1,3,2,128,512]{3,4,2,1,0:T(8,128)(2,1)S(1)}, u32[]{:S(2)}, u32[]{:S(2)}) collective-permute-start(bf16[1,3,2,128,512]{3,4,2,1,0:T(8,128)(2,1)S(1)} %bitcast.146), channel_id=1, source_target_pairs={{0,24},{8,0},{16,8},{24,16},{1,25},{9,1},{17,9},{25,17},{2,26},{10... | collective-permute-start | bytes 2359304 | tf_op jit(solution)/shard_map/ppermute | solution.py:17
  132.6 11.7 %copy-start.3 = (bf16[1,12,2,128,512]{4,3,2,1,0:T(8,128)(2,1)}, bf16[1,12,2,128,512]{4,3,2,1,0:T(8,128)(2,1)S(1)}, u32[]{:S(2)}) copy-start(bf16[1,12,2,128,512]{4,3,2,1,0:T(8,128)(2,1)S(1)} %constant_dynamic-update-slice_fusion.11) | copy-start | bytes 9437188
  136.6 4.3 %copy-start.7 = (bf16[24,7168]{1,0:T(8,128)(2,1)}, bf16[24,7168]{1,0:T(8,128)(2,1)S(1)}, u32[]{:S(2)}) copy-start(bf16[24,7168]{1,0:T(8,128)(2,1)S(1)} %collective-permute-done.9) | copy-start | bytes 1032196
  136.6 20.5 %collective-permute-start.16 = (bf16[24,7168]{1,0:T(8,128)(2,1)}, bf16[24,7168]{1,0:T(8,128)(2,1)}, u32[]{:S(2)}, u32[]{:S(2)}) collective-permute-start(bf16[24,7168]{1,0:T(8,128)(2,1)} %get-tuple-element.13), channel_id=1, source_target_pairs={{0,1},{1,0},{2,3},{3,2},{4,5},{5,4},{6,7},{7,6},{8,9},{9,8},{10,11... | collective-permute-start | bytes 1032200 | tf_op jit(solution)/shard_map/ppermute | solution.py:65
  140.9 13.1 %collective-permute-start.11 = (bf16[24,7168]{1,0:T(8,128)(2,1)}, bf16[24,7168]{1,0:T(8,128)(2,1)S(1)}, u32[]{:S(2)}, u32[]{:S(2)}) collective-permute-start(bf16[24,7168]{1,0:T(8,128)(2,1)} %get-tuple-element.14), channel_id=1, source_target_pairs={{0,1},{1,0},{2,3},{3,2},{4,5},{5,4},{6,7},{7,6},{8,9},{9,8},{10,11... | collective-permute-start | bytes 1032200 | tf_op jit(solution)/shard_map/ppermute | solution.py:65
  144.4 11.3 %collective-permute-start.10 = (bf16[24,7168]{1,0:T(8,128)(2,1)}, bf16[24,7168]{1,0:T(8,128)(2,1)}, u32[]{:S(2)}, u32[]{:S(2)}) collective-permute-start(bf16[24,7168]{1,0:T(8,128)(2,1)} %fusion.67), channel_id=1, source_target_pairs={{0,2},{1,3},{2,4},{3,5},{4,6},{5,7},{6,0},{7,1},{8,10},{9,11},{10,... | collective-permute-start | bytes 1032200 | tf_op jit(solution)/shard_map/ppermute | solution.py:71
  148.4 18.7 %copy-start.1 = (bf16[24,7168]{1,0:T(8,128)(2,1)S(1)}, bf16[24,7168]{1,0:T(8,128)(2,1)}, u32[]{:S(2)}) copy-start(bf16[24,7168]{1,0:T(8,128)(2,1)} %param.10) | copy-start | bytes 1032196
  148.4 18.7 %copy-start.8 = (f32[7168]{0:T(1024)S(1)}, f32[7168]{0:T(1024)}, u32[]{:S(2)}) copy-start(f32[7168]{0:T(1024)} %param.16) | copy-start | bytes 86020
  157.0 10.2 %collective-permute-start.15 = (bf16[24,7168]{1,0:T(8,128)(2,1)S(1)}, bf16[24,7168]{1,0:T(8,128)(2,1)S(1)}, u32[]{:S(2)}, u32[]{:S(2)}) collective-permute-start(bf16[24,7168]{1,0:T(8,128)(2,1)S(1)} %fusion.64), channel_id=1, source_target_pairs={{0,2},{1,3},{2,4},{3,5},{4,6},{5,7},{6,0},{7,1},{8,10},{9,11},{10,... | collective-permute-start | bytes 1032200 | tf_op jit(solution)/shard_map/ppermute | solution.py:71

commit v3 on v2

--- a/solution.py
+++ b/solution.py
@@ -5,6 +5,7 @@
 
 HD = 128
 RELAY_STEP = 3
+CACHE_STEP = 2
 
 
 def normalize(x, gain, shift):
@@ -73,20 +74,22 @@
     )
 
 
-def gather_tokens(x):
+def gather_tokens(x, rider):
     tensor_count = lax.axis_size("tensor")
     rows = tensor_count // 2
     i = lax.axis_index("tensor")
     outer, inner = i // 2, i % 2
     own = [x]
-    for _ in range(1, rows):
+    for k in range(1, rows):
         own.append(ring(own[-1]))
+        if k == CACHE_STEP:
+            own[-1], rider = lax.optimization_barrier((own[-1], rider))
     other = [partner(piece) for piece in own]
     steps = jnp.arange(rows)
     source = jnp.concatenate(
         [((outer - steps) % rows) * 2 + inner, ((outer - steps) % rows) * 2 + (1 - inner)]
     )
-    return jnp.concatenate(own + other, axis=0), source
+    return jnp.concatenate(own + other, axis=0), source, rider
 
 
 def scatter_tokens(partial, rider):
@@ -121,9 +124,10 @@
     hidden = stretch.astype(jnp.float32)
     head_count = qkv_weight.shape[1] // (3 * HD)
     normed = normalize(hidden, ln_gain, ln_bias)
-    gathered, source = gather_tokens(normed)
     split = split_heads(prefill_cache)
-    gathered, split = lax.optimization_barrier((gathered, split))
+    gathered, source, split = gather_tokens(normed, split)
+    if CACHE_STEP == 0:
+        gathered, split = lax.optimization_barrier((gathered, split))
     per_head_rows = lax.all_to_all(split, "tensor", split_axis=3, concat_axis=3, tiled=True)
     outgoing = send_decode(per_head_rows, block_dest)
     qkv = (

time: 170 us -> 162 us (0.953)
  waiting for transfers between devices: 72.3 us -> 54.6 us
  local copies, waits for them, and re-layouts: 31.2 us -> 35.3 us
  starting transfers between devices: 18.1 us -> 21.3 us
  other arithmetic: 17.1 us -> 19 us
    all_to_all x1, waiting for transfers between devices: 22.7 us -> 1.92 us  [local(): lax.all_to_all(split, 'tensor', split_axis=3, concat_axis=3, tiled=True)]
    ppermute x8, waiting for transfers between devices: 10.9 us -> 27.5 us  [partner(): return lax.ppermute(x, 'tensor', [(j, j ^ 1) for j in range(tensor_count)])]
    ppermute x6, waiting for transfers between devices: 38.7 us -> 25.2 us  [ring(): lax.ppermute(x, 'tensor', [(j, (j // 2 + 1) % rows * 2 + j % 2) for j in...]
    unnamed x33 -> x29, local copies, waits for them, and re-layouts: 9.22 us -> 12.2 us
  transfers between devices with their start and end apart: 18 -> 18, of which waited for: 10 -> 9; matrix products, arithmetic and copies ran while one was open for 37% -> 45% of each run, Pallas kernels for 0% -> 0%
where the time goes in v3:
time: 162 us; the launch traced here: 161 us
  waiting for transfers between devices  54.6 us (34%)
  local copies, waits for them, and re-layouts  35.3 us (22%)
  matrix products  29.5 us (18%)
  starting transfers between devices  21.3 us (13%)
  other arithmetic  19 us (12%)
    ppermute x8, waiting for transfers between devices, partner(): return lax.ppermute(x, 'tensor', [(j, j ^ 1) for j in range(tensor_count)])  27.5 us
    ppermute x6, waiting for transfers between devices, ring(): lax.ppermute(x, 'tensor', [(j, (j // 2 + 1) % rows * 2 + j % 2) for j in...  25.2 us
    dot_general x1, matrix products, local(): jnp.dot(gathered, qkv_weight, preferred_element_type=jnp.float32) + qkv_bias  12.5 us
    unnamed x29, local copies, waits for them, and re-layouts  12.2 us
    ppermute x8, starting transfers between devices, partner(): return lax.ppermute(x, 'tensor', [(j, j ^ 1) for j in range(tensor_count)])  9.99 us
    dot_general x1, matrix products, local(): jnp.dot(context, out_weight, preferred_element_type=jnp.float32)  7.1 us
    dot_general x4, matrix products, send_decode(): jnp.einsum('gud,gohdtc->guothc', placement_index, per_head_rows, preferre...  6.41 us
    all_to_all x1, starting transfers between devices, local(): lax.all_to_all(split, 'tensor', split_axis=3, concat_axis=3, tiled=True)  5.07 us
  transfers between devices with their start and end apart: 18, of which 9 were waited for; matrix products, arithmetic and copies ran while one was open for 45% of the time, Pallas kernels for 0%

profile of v3, /device:TPU:0, one launch (start us, length us, event | category | flops | bytes accessed | tf_op | source)
XLA Modules:
  0.0 160.7 jit_solution(3797015064309666616)
XLA Ops:
  0.6 1.1 convert_reduce_fusion
  1.8 1.2 fusion.55
  3.0 1.9 %constant_dynamic-update-slice_fusion.7 = (bf16[192,7168]{1,0:T(8,128)(2,1)}, bf16[24,7168]{1,0:T(8,128)(2,1)S(1)}) fusion(f32[7168]{0:T(1024)} %param.12, f32[7168]{0:T(1024)} %param.11, f32[24]{0:T(128)S(1)} %add_rsqrt_fusion, f32[24]{0:T(128)S(1)} %broadcast_multiply_fusion, bf16[24,7168]{1,0:T(8,128)(2,1)} %param.10), kind=kLoop, calls=%fused_computation.78 | loop fusion | flops 1032191 | bytes 1089728
  5.0 3.0 %collective-permute-start.3 = (bf16[24,7168]{1,0:T(8,128)(2,1)S(1)}, bf16[24,7168]{1,0:T(8,128)(2,1)S(1)}, u32[]{:S(2)}, u32[]{:S(2)}) collective-permute-start(bf16[24,7168]{1,0:T(8,128)(2,1)S(1)} %get-tuple-element.11), channel_id=1, source_target_pairs={{0,1},{1,0},{2,3},{3,2},{4,5},{5,4},{6,7},{7,6},{8,9},{9,8},{10,11... | collective-permute-start | bytes 1032200 | tf_op jit(solution)/shard_map/ppermute | solution.py:66
  8.0 1.6 collective-permute-start
  9.5 1.2 slice.55
  13.8 2.0 %gather_fusion = s32[192]{0:T(256)S(1)} fusion(s32[192]{0:T(256)} %param.17, s32[1024]{0:T(1024)S(1)} %pad_clamp_fusion), kind=kCustom, calls=%fused_computation | custom fusion | bytes 2304 | tf_op jit(solution)/shard_map/gather | solution.py:139
  17.0 3.1 %copy.50 = bf16[1,1,2,128,4096]{3,4,2,1,0:T(8,128)(2,1)S(1)} copy(bf16[1,1,2,128,4096]{4,3,2,1,0:T(8,128)(2,1)} %param.18) | data formatting | bytes 4194304 | tf_op args[8]
  22.0 1.6 collective-permute-start.1
  24.3 8.5 %collective-permute-done.1 = bf16[24,7168]{1,0:T(8,128)(2,1)} collective-permute-done((bf16[24,7168]{1,0:T(8,128)(2,1)S(1)}, bf16[24,7168]{1,0:T(8,128)(2,1)}, u32[]{:S(2)}, u32[]{:S(2)}) %collective-permute-start.1) | collective-permute-done | bytes 344096 | tf_op jit(solution)/shard_map/ppermute | solution.py:72
  32.9 1.5 collective-permute-start.5
  34.4 1.8 %constant_dynamic-update-slice_fusion.5 = bf16[192,7168]{1,0:T(8,128)(2,1)} fusion(bf16[192,7168]{1,0:T(8,128)(2,1)} %constant_dynamic-update-slice_fusion.6, bf16[24,7168]{1,0:T(8,128)(2,1)} %collective-permute-done.1), kind=kLoop, calls=%fused_computation.76 | loop fusion | bytes 688128
  36.2 2.6 %copy.51 = bf16[1,2,4,8,128,128]{5,4,2,1,0,3:T(8,128)(2,1)} copy(bf16[1,2,4,8,128,128]{4,5,2,3,1,0:T(8,128)(2,1)S(1)} %bitcast.140) | data formatting | bytes 4194304 | tf_op jit(solution)/shard_map/optimization_barrier | solution.py:86
  38.8 5.1 %all-to-all-start = ((bf16[1,2,4,8,128,128]{5,4,2,1,0,3:T(8,128)(2,1)}), bf16[1,2,4,8,128,128]{5,4,2,1,0,3:T(8,128)(2,1)S(1)}, u32[]{:S(2)}, u32[]{:S(2)}) async-start(bf16[1,2,4,8,128,128]{5,4,2,1,0,3:T(8,128)(2,1)} %copy.51), calls=%async_computation | async-start | bytes 4194304 | tf_op jit(solution)/shard_map/all_to_all | solution.py:131
  44.3 1.7 %collective-permute-start.6 = (bf16[24,7168]{1,0:T(8,128)(2,1)}, bf16[24,7168]{1,0:T(8,128)(2,1)S(1)}, u32[]{:S(2)}, u32[]{:S(2)}) collective-permute-start(bf16[24,7168]{1,0:T(8,128)(2,1)} %collective-permute-done.2), channel_id=1, source_target_pairs={{0,1},{1,0},{2,3},{3,2},{4,5},{5,4},{6,7},{7,6},{8,9},{9,8},{10,11... | collective-permute-start | bytes 1032200 | tf_op jit(solution)/shard_map/ppermute | solution.py:66
  46.0 1.8 %constant_dynamic-update-slice_fusion.4 = bf16[192,7168]{1,0:T(8,128)(2,1)} fusion(bf16[192,7168]{1,0:T(8,128)(2,1)} %constant_dynamic-update-slice_fusion.5, bf16[24,7168]{1,0:T(8,128)(2,1)} %collective-permute-done.2), kind=kLoop, calls=%fused_computation.75 | loop fusion | bytes 688128
  49.2 1.7 %constant_dynamic-update-slice_fusion.1 = bf16[192,7168]{1,0:T(8,128)(2,1)} fusion(bf16[192,7168]{1,0:T(8,128)(2,1)} %constant_dynamic-update-slice_fusion.2, bf16[24,7168]{1,0:T(8,128)(2,1)} %collective-permute-done.5), kind=kLoop, calls=%fused_computation.72 | loop fusion | bytes 688128
  51.0 19.8 %collective-permute-done.6 = bf16[24,7168]{1,0:T(8,128)(2,1)S(1)} collective-permute-done((bf16[24,7168]{1,0:T(8,128)(2,1)}, bf16[24,7168]{1,0:T(8,128)(2,1)S(1)}, u32[]{:S(2)}, u32[]{:S(2)}) %collective-permute-start.6) | collective-permute-done | bytes 344096 | tf_op jit(solution)/shard_map/ppermute | solution.py:66
  71.5 12.5 %fusion.4 = bf16[192,1536]{1,0:T(8,128)(2,1)S(1)} fusion(bf16[192,7168]{1,0:T(8,128)(2,1)} %constant_dynamic-update-slice_fusion, bf16[7168,1536]{1,0:T(8,128)(2,1)} %param.13, f32[1536]{0:T(1024)S(1)} %copy-done.10), kind=kOutput, calls=%fused_computation.9 | convolution fusion | flops 4228448256 | bytes 25368576 | tf_op jit(solution)/shard_map/dot_general | solution.py:134
  86.1 2.0 %fusion.95 = (f32[4,192]{1,0:T(4,128)S(1)}, f32[4,192,192]{2,1,0:T(8,128)}) fusion(bf16[192,4,1,128]{3,2,1,0:T(2,128)(2,1)S(1)} %get-tuple-element.19, bf16[192,4,1,128]{3,2,1,0:T(2,128)(2,1)S(1)} %get-tuple-element.20, pred[192,192]{1,0:T(8,128)(4,1)} %compare_and_fusion), kind=kOutput, calls=%fused_computation.124 | convolution fusion | flops 38190336 | bytes 1022976 | tf_op jit(solution)/shard_map/qhd,khd->hqk/dot_general | solution.py:149
  88.1 1.9 %all-to-all-done = bf16[1,2,4,8,128,128]{5,4,2,1,0,3:T(8,128)(2,1)S(1)} async-done(((bf16[1,2,4,8,128,128]{5,4,2,1,0,3:T(8,128)(2,1)}), bf16[1,2,4,8,128,128]{5,4,2,1,0,3:T(8,128)(2,1)S(1)}, u32[]{:S(2)}, u32[]{:S(2)}) %all-to-all-start) | async-done | bytes 2097184 | tf_op jit(solution)/shard_map/all_to_all | solution.py:131
  90.0 2.1 %fusion.30 = bf16[1,3,2,128,4,128]{5,1,3,4,2,0:T(4,128)(2,1)S(1)} fusion(bf16[1,2,4,8,128,128]{5,4,2,1,0,3:T(8,128)(2,1)S(1)} %all-to-all-done, s32[8]{0:T(128)S(1)} %multiply_add_fusion, s32[3]{0:T(128)} %iota_add_fusion.2), kind=kOutput, calls=%fused_computation.25 | convolution fusion | flops 6684696 | bytes 2883628 | tf_op jit(solution)/shard_map/gud,gohdtc->guothc/dot_general | solution.py:45
  92.1 1.4 copy.63
  93.4 1.5 collective-permute-start.13
  97.5 1.0 divide_convert_fusion
  99.6 7.1 %fusion.96 = (bf16[2,4,24,7168]{3,2,1,0:T(8,128)(2,1)S(1)}, f32[2,4,24,7168]{3,2,1,0:T(8,128)}) fusion(bf16[2,4,24,512]{3,2,1,0:T(8,128)(2,1)S(1)} %dot_general.37, bf16[512,7168]{1,0:T(8,128)(2,1)} %param.15), kind=kOutput, calls=%fused_computation.125 | convolution fusion | flops 1410662400 | bytes 15794176 | tf_op jit(solution)/shard_map/dot_general | solution.py:176
  106.7 1.1 slice_bitcast_fusion.7
  107.8 1.2 collective-permute-start.7
  109.0 1.4 fusion.33
  110.5 1.3 copy.61
  111.8 1.4 fusion.36
  113.3 1.3 copy.59
  114.6 2.3 %copy.60 = bf16[1,3,2,128,512]{4,3,2,1,0:T(8,128)(2,1)} copy(bf16[1,3,2,128,512]{3,4,2,1,0:T(8,128)(2,1)} %bitcast.142) | data formatting | bytes 1572864 | tf_op jit(solution)/shard_map/reshape | solution.py:48
  117.8 2.0 %fusion.69 = bf16[24,7168]{1,0:T(8,128)(2,1)} fusion(f32[2,4,24,7168]{3,2,1,0:T(8,128)} %get-tuple-element.26, bf16[24,7168]{1,0:T(8,128)(2,1)} %collective-permute-done.7), kind=kLoop, calls=%fused_computation.60 | loop fusion | flops 516096 | bytes 1376256 | tf_op jit(solution)/shard_map/convert_element_type | solution.py:107
  119.8 1.4 fusion.27
  122.0 1.5 collective-permute-start.14
  123.9 3.9 %collective-permute-done.9 = bf16[24,7168]{1,0:T(8,128)(2,1)S(1)} collective-permute-done((bf16[24,7168]{1,0:T(8,128)(2,1)}, bf16[24,7168]{1,0:T(8,128)(2,1)S(1)}, u32[]{:S(2)}, u32[]{:S(2)}) %collective-permute-start.9) | collective-permute-done | bytes 344096 | tf_op jit(solution)/shard_map/ppermute | solution.py:66
  128.6 4.4 %collective-permute-done.8 = bf16[24,7168]{1,0:T(8,128)(2,1)} collective-permute-done((bf16[24,7168]{1,0:T(8,128)(2,1)}, bf16[24,7168]{1,0:T(8,128)(2,1)}, u32[]{:S(2)}, u32[]{:S(2)}) %collective-permute-start.8) | collective-permute-done | bytes 344096 | tf_op jit(solution)/shard_map/ppermute | solution.py:72
  133.4 2.1 %fusion.67 = bf16[24,7168]{1,0:T(8,128)(2,1)} fusion(f32[2,4,24,7168]{3,2,1,0:T(8,128)} %get-tuple-element.26, bf16[24,7168]{1,0:T(8,128)(2,1)} %copy-done.6, bf16[24,7168]{1,0:T(8,128)(2,1)} %collective-permute-done.8), kind=kLoop, calls=%fused_computation.57 | loop fusion | flops 860160 | bytes 1720320 | tf_op jit(solution)/shard_map/convert_element_type | solution.py:107
  135.6 1.4 copy.64
  137.0 1.4 copy.62
  138.7 0.9 constant_dynamic-update-slice_fusion.10
  139.7 0.9 constant_dynamic-update-slice_fusion.9
  141.5 3.8 %collective-permute-done.11 = bf16[24,7168]{1,0:T(8,128)(2,1)S(1)} collective-permute-done((bf16[24,7168]{1,0:T(8,128)(2,1)}, bf16[24,7168]{1,0:T(8,128)(2,1)S(1)}, u32[]{:S(2)}, u32[]{:S(2)}) %collective-permute-start.11) | collective-permute-done | bytes 344096 | tf_op jit(solution)/shard_map/ppermute | solution.py:66
  145.3 1.7 %collective-permute-done.10 = bf16[24,7168]{1,0:T(8,128)(2,1)} collective-permute-done((bf16[24,7168]{1,0:T(8,128)(2,1)}, bf16[24,7168]{1,0:T(8,128)(2,1)}, u32[]{:S(2)}, u32[]{:S(2)}) %collective-permute-start.10) | collective-permute-done | bytes 344096 | tf_op jit(solution)/shard_map/ppermute | solution.py:72
  147.0 1.3 fusion.64
  148.4 10.2 %collective-permute-done.15 = bf16[24,7168]{1,0:T(8,128)(2,1)S(1)} collective-permute-done((bf16[24,7168]{1,0:T(8,128)(2,1)S(1)}, bf16[24,7168]{1,0:T(8,128)(2,1)S(1)}, u32[]{:S(2)}, u32[]{:S(2)}) %collective-permute-start.15) | collective-permute-done | bytes 344096 | tf_op jit(solution)/shard_map/ppermute | solution.py:72
  158.6 2.1 %fusion.60 = bf16[24,7168]{1,0:T(8,128)(2,1)} fusion(bf16[24,7168]{1,0:T(8,128)(2,1)S(1)} %copy-done, f32[2,4,24,7168]{3,2,1,0:T(8,128)} %get-tuple-element.26, bf16[24,7168]{1,0:T(8,128)(2,1)} %collective-permute-done.16, bf16[24,7168]{1,0:T(8,128)(2,1)S(1)} %collective-permute-done.15, f32[7168]{0:T(1024)S(1)} %copy-done.7), kind=kLoop, calls=%fused_computation.47 | loop fusion | flops 1376256 | bytes 2093056 | tf_op jit(solution)/shard_map/convert_element_type | solution.py:178
  (81 shorter events, 19.6 us)
Async XLA Ops:
  5.0 42.7 %collective-permute-start.3 = (bf16[24,7168]{1,0:T(8,128)(2,1)S(1)}, bf16[24,7168]{1,0:T(8,128)(2,1)S(1)}, u32[]{:S(2)}, u32[]{:S(2)}) collective-permute-start(bf16[24,7168]{1,0:T(8,128)(2,1)S(1)} %get-tuple-element.11), channel_id=1, source_target_pairs={{0,1},{1,0},{2,3},{3,2},{4,5},{5,4},{6,7},{7,6},{8,9},{9,8},{10,11... | collective-permute-start | bytes 1032200 | tf_op jit(solution)/shard_map/ppermute | solution.py:66
  8.0 13.5 %collective-permute-start = (bf16[24,7168]{1,0:T(8,128)(2,1)S(1)}, bf16[24,7168]{1,0:T(8,128)(2,1)S(1)}, u32[]{:S(2)}, u32[]{:S(2)}) collective-permute-start(bf16[24,7168]{1,0:T(8,128)(2,1)S(1)} %get-tuple-element.11), channel_id=1, source_target_pairs={{0,2},{1,3},{2,4},{3,5},{4,6},{5,7},{6,0},{7,1},{8,10},{9,11},{10,... | collective-permute-start | bytes 1032200 | tf_op jit(solution)/shard_map/ppermute | solution.py:72
  21.5 27.0 %collective-permute-start.4 = (bf16[24,7168]{1,0:T(8,128)(2,1)S(1)}, bf16[24,7168]{1,0:T(8,128)(2,1)S(1)}, u32[]{:S(2)}, u32[]{:S(2)}) collective-permute-start(bf16[24,7168]{1,0:T(8,128)(2,1)S(1)} %collective-permute-done), channel_id=1, source_target_pairs={{0,1},{1,0},{2,3},{3,2},{4,5},{5,4},{6,7},{7,6},{8,9},{9,8},{10,11... | collective-permute-start | bytes 1032200 | tf_op jit(solution)/shard_map/ppermute | solution.py:66
  22.0 10.9 %collective-permute-start.1 = (bf16[24,7168]{1,0:T(8,128)(2,1)S(1)}, bf16[24,7168]{1,0:T(8,128)(2,1)}, u32[]{:S(2)}, u32[]{:S(2)}) collective-permute-start(bf16[24,7168]{1,0:T(8,128)(2,1)S(1)} %collective-permute-done), channel_id=1, source_target_pairs={{0,2},{1,3},{2,4},{3,5},{4,6},{5,7},{6,0},{7,1},{8,10},{9,11},{10,... | collective-permute-start | bytes 1032200 | tf_op jit(solution)/shard_map/ppermute | solution.py:72
  32.9 16.4 %collective-permute-start.5 = (bf16[24,7168]{1,0:T(8,128)(2,1)}, bf16[24,7168]{1,0:T(8,128)(2,1)}, u32[]{:S(2)}, u32[]{:S(2)}) collective-permute-start(bf16[24,7168]{1,0:T(8,128)(2,1)} %collective-permute-done.1), channel_id=1, source_target_pairs={{0,1},{1,0},{2,3},{3,2},{4,5},{5,4},{6,7},{7,6},{8,9},{9,8},{10,11... | collective-permute-start | bytes 1032200 | tf_op jit(solution)/shard_map/ppermute | solution.py:66
  34.4 9.9 %collective-permute-start.2 = (bf16[24,7168]{1,0:T(8,128)(2,1)}, bf16[24,7168]{1,0:T(8,128)(2,1)}, u32[]{:S(2)}, u32[]{:S(2)}) collective-permute-start(bf16[24,7168]{1,0:T(8,128)(2,1)} %collective-permute-done.1), channel_id=1, source_target_pairs={{0,2},{1,3},{2,4},{3,5},{4,6},{5,7},{6,0},{7,1},{8,10},{9,11},{10,... | collective-permute-start | bytes 1032200 | tf_op jit(solution)/shard_map/ppermute | solution.py:72
  38.8 51.2 %all-to-all-start = ((bf16[1,2,4,8,128,128]{5,4,2,1,0,3:T(8,128)(2,1)}), bf16[1,2,4,8,128,128]{5,4,2,1,0,3:T(8,128)(2,1)S(1)}, u32[]{:S(2)}, u32[]{:S(2)}) async-start(bf16[1,2,4,8,128,128]{5,4,2,1,0,3:T(8,128)(2,1)} %copy.51), calls=%async_computation | async-start | bytes 4194304 | tf_op jit(solution)/shard_map/all_to_all | solution.py:131
  43.9 27.7 %copy-start.10 = (f32[1536]{0:T(1024)S(1)}, f32[1536]{0:T(1024)}, u32[]{:S(2)}) copy-start(f32[1536]{0:T(1024)} %param.14) | copy-start | bytes 18436
  44.3 26.5 %collective-permute-start.6 = (bf16[24,7168]{1,0:T(8,128)(2,1)}, bf16[24,7168]{1,0:T(8,128)(2,1)S(1)}, u32[]{:S(2)}, u32[]{:S(2)}) collective-permute-start(bf16[24,7168]{1,0:T(8,128)(2,1)} %collective-permute-done.2), channel_id=1, source_target_pairs={{0,1},{1,0},{2,3},{3,2},{4,5},{5,4},{6,7},{7,6},{8,9},{9,8},{10,11... | collective-permute-start | bytes 1032200 | tf_op jit(solution)/shard_map/ppermute | solution.py:66
  85.4 0.7 copy-start.4
  93.4 42.1 %collective-permute-start.13 = (bf16[1,3,2,128,512]{3,4,2,1,0:T(8,128)(2,1)}, bf16[1,3,2,128,512]{3,4,2,1,0:T(8,128)(2,1)}, u32[]{:S(2)}, u32[]{:S(2)}) collective-permute-start(bf16[1,3,2,128,512]{3,4,2,1,0:T(8,128)(2,1)} %bitcast.144), channel_id=1, source_target_pairs={{0,16},{8,24},{16,0},{24,8},{1,17},{9,25},{17,1},{25,9},{2,18},{10... | collective-permute-start | bytes 2359304 | tf_op jit(solution)/shard_map/ppermute | solution.py:18
  95.1 1.0 copy-start.5
  95.2 1.6 copy-start.3
  106.7 2.4 %copy-start.8 = (s32[3]{0:T(128)S(1)}, s32[3]{0:T(128)}, u32[]{:S(2)}) copy-start(s32[3]{0:T(128)} %iota_add_fusion.3) | copy-start | bytes 40
  107.8 10.0 %collective-permute-start.7 = (bf16[24,7168]{1,0:T(8,128)(2,1)}, bf16[24,7168]{1,0:T(8,128)(2,1)}, u32[]{:S(2)}, u32[]{:S(2)}) collective-permute-start(bf16[24,7168]{1,0:T(8,128)(2,1)} %get-tuple-element.12), channel_id=1, source_target_pairs={{0,1},{1,0},{2,3},{3,2},{4,5},{5,4},{6,7},{7,6},{8,9},{9,8},{10,11... | collective-permute-start | bytes 1032200 | tf_op jit(solution)/shard_map/ppermute | solution.py:66
  111.8 25.2 %collective-permute-start.12 = (bf16[1,3,2,128,512]{3,4,2,1,0:T(8,128)(2,1)}, bf16[1,3,2,128,512]{3,4,2,1,0:T(8,128)(2,1)}, u32[]{:S(2)}, u32[]{:S(2)}) collective-permute-start(bf16[1,3,2,128,512]{3,4,2,1,0:T(8,128)(2,1)} %bitcast.145), channel_id=1, source_target_pairs={{0,8},{8,16},{16,24},{24,0},{1,9},{9,17},{17,25},{25,1},{2,10},{10... | collective-permute-start | bytes 2359304 | tf_op jit(solution)/shard_map/ppermute | solution.py:18
  113.3 6.5 %copy-start.9 = (s32[3]{0:T(128)S(1)}, s32[3]{0:T(128)}, u32[]{:S(2)}) copy-start(s32[3]{0:T(128)} %iota_add_fusion.1) | copy-start | bytes 40
  117.0 10.8 %collective-permute-start.9 = (bf16[24,7168]{1,0:T(8,128)(2,1)}, bf16[24,7168]{1,0:T(8,128)(2,1)S(1)}, u32[]{:S(2)}, u32[]{:S(2)}) collective-permute-start(bf16[24,7168]{1,0:T(8,128)(2,1)} %get-tuple-element.15), channel_id=1, source_target_pairs={{0,1},{1,0},{2,3},{3,2},{4,5},{5,4},{6,7},{7,6},{8,9},{9,8},{10,11... | collective-permute-start | bytes 1032200 | tf_op jit(solution)/shard_map/ppermute | solution.py:66
  119.8 13.2 %collective-permute-start.8 = (bf16[24,7168]{1,0:T(8,128)(2,1)}, bf16[24,7168]{1,0:T(8,128)(2,1)}, u32[]{:S(2)}, u32[]{:S(2)}) collective-permute-start(bf16[24,7168]{1,0:T(8,128)(2,1)} %fusion.69), channel_id=1, source_target_pairs={{0,2},{1,3},{2,4},{3,5},{4,6},{5,7},{6,0},{7,1},{8,10},{9,11},{10,... | collective-permute-start | bytes 1032200 | tf_op jit(solution)/shard_map/ppermute | solution.py:72
  121.3 2.6 %copy-start.1 = (bf16[1,3,2,128,512]{4,3,2,1,0:T(8,128)(2,1)S(1)}, bf16[1,3,2,128,512]{4,3,2,1,0:T(8,128)(2,1)}, u32[]{:S(2)}) copy-start(bf16[1,3,2,128,512]{4,3,2,1,0:T(8,128)(2,1)} %copy.60) | copy-start | bytes 2359300
  122.0 16.4 %collective-permute-start.14 = (bf16[1,3,2,128,512]{3,4,2,1,0:T(8,128)(2,1)S(1)}, bf16[1,3,2,128,512]{3,4,2,1,0:T(8,128)(2,1)S(1)}, u32[]{:S(2)}, u32[]{:S(2)}) collective-permute-start(bf16[1,3,2,128,512]{3,4,2,1,0:T(8,128)(2,1)S(1)} %bitcast.146), channel_id=1, source_target_pairs={{0,24},{8,0},{16,8},{24,16},{1,25},{9,1},{17,9},{25,17},{2,26},{10... | collective-permute-start | bytes 2359304 | tf_op jit(solution)/shard_map/ppermute | solution.py:18
  123.9 11.7 %copy-start.2 = (bf16[1,12,2,128,512]{4,3,2,1,0:T(8,128)(2,1)}, bf16[1,12,2,128,512]{4,3,2,1,0:T(8,128)(2,1)S(1)}, u32[]{:S(2)}) copy-start(bf16[1,12,2,128,512]{4,3,2,1,0:T(8,128)(2,1)S(1)} %constant_dynamic-update-slice_fusion.11) | copy-start | bytes 9437188
  127.8 5.2 %copy-start.6 = (bf16[24,7168]{1,0:T(8,128)(2,1)}, bf16[24,7168]{1,0:T(8,128)(2,1)S(1)}, u32[]{:S(2)}) copy-start(bf16[24,7168]{1,0:T(8,128)(2,1)S(1)} %collective-permute-done.9) | copy-start | bytes 1032196
  127.8 20.6 %collective-permute-start.16 = (bf16[24,7168]{1,0:T(8,128)(2,1)}, bf16[24,7168]{1,0:T(8,128)(2,1)}, u32[]{:S(2)}, u32[]{:S(2)}) collective-permute-start(bf16[24,7168]{1,0:T(8,128)(2,1)} %get-tuple-element.13), channel_id=1, source_target_pairs={{0,1},{1,0},{2,3},{3,2},{4,5},{5,4},{6,7},{7,6},{8,9},{9,8},{10,11... | collective-permute-start | bytes 1032200 | tf_op jit(solution)/shard_map/ppermute | solution.py:66
  133.0 12.3 %collective-permute-start.11 = (bf16[24,7168]{1,0:T(8,128)(2,1)}, bf16[24,7168]{1,0:T(8,128)(2,1)S(1)}, u32[]{:S(2)}, u32[]{:S(2)}) collective-permute-start(bf16[24,7168]{1,0:T(8,128)(2,1)} %get-tuple-element.14), channel_id=1, source_target_pairs={{0,1},{1,0},{2,3},{3,2},{4,5},{5,4},{6,7},{7,6},{8,9},{9,8},{10,11... | collective-permute-start | bytes 1032200 | tf_op jit(solution)/shard_map/ppermute | solution.py:66
  135.6 11.4 %collective-permute-start.10 = (bf16[24,7168]{1,0:T(8,128)(2,1)}, bf16[24,7168]{1,0:T(8,128)(2,1)}, u32[]{:S(2)}, u32[]{:S(2)}) collective-permute-start(bf16[24,7168]{1,0:T(8,128)(2,1)} %fusion.67), channel_id=1, source_target_pairs={{0,2},{1,3},{2,4},{3,5},{4,6},{5,7},{6,0},{7,1},{8,10},{9,11},{10,... | collective-permute-start | bytes 1032200 | tf_op jit(solution)/shard_map/ppermute | solution.py:72
  139.7 18.9 %copy-start = (bf16[24,7168]{1,0:T(8,128)(2,1)S(1)}, bf16[24,7168]{1,0:T(8,128)(2,1)}, u32[]{:S(2)}) copy-start(bf16[24,7168]{1,0:T(8,128)(2,1)} %param.10) | copy-start | bytes 1032196
  139.7 18.9 %copy-start.7 = (f32[7168]{0:T(1024)S(1)}, f32[7168]{0:T(1024)}, u32[]{:S(2)}) copy-start(f32[7168]{0:T(1024)} %param.16) | copy-start | bytes 86020
  148.3 10.3 %collective-permute-start.15 = (bf16[24,7168]{1,0:T(8,128)(2,1)S(1)}, bf16[24,7168]{1,0:T(8,128)(2,1)S(1)}, u32[]{:S(2)}, u32[]{:S(2)}) collective-permute-start(bf16[24,7168]{1,0:T(8,128)(2,1)S(1)} %fusion.64), channel_id=1, source_target_pairs={{0,2},{1,3},{2,4},{3,5},{4,6},{5,7},{6,0},{7,1},{8,10},{9,11},{10,... | collective-permute-start | bytes 1032200 | tf_op jit(solution)/shard_map/ppermute | solution.py:72

commit v4 on v3

--- a/solution.py
+++ b/solution.py
@@ -4,8 +4,9 @@
 from jax.sharding import PartitionSpec as P
 
 HD = 128
-RELAY_STEP = 3
+RELAY_STEP = 0
 CACHE_STEP = 2
+CHAIN_PARTNER = True
 
 
 def normalize(x, gain, shift):
@@ -96,10 +97,15 @@
     tensor_count = lax.axis_size("tensor")
     rows = tensor_count // 2
     blocks = partial.reshape((2, rows, -1) + partial.shape[1:])
-    mine = [
-        blocks[0, s] + partner(blocks[1, s].astype(jnp.bfloat16)).astype(jnp.float32)
-        for s in range(rows)
-    ]
+    sent = blocks[1].astype(jnp.bfloat16)
+    mine = [None] * rows
+    previous = None
+    for s in [(s + 1) % rows for s in range(rows)]:
+        piece = sent[s]
+        if previous is not None and CHAIN_PARTNER:
+            piece, previous = lax.optimization_barrier((piece, previous))
+        previous = partner(piece)
+        mine[s] = blocks[0, s] + previous.astype(jnp.float32)
     carried = mine[1 % rows]
     for k in range(1, rows):
         if k == RELAY_STEP:

time: 162 us -> 155 us (0.957)
  matrix products: 29.5 us -> 24.3 us
  other arithmetic: 19 us -> 14.4 us
  waiting for transfers between devices: 54.6 us -> 58.3 us
  starting transfers between devices: 21.3 us -> 19.4 us
    ppermute x6, waiting for transfers between devices: 25.2 us -> 16.7 us  [ring(): lax.ppermute(x, 'tensor', [(j, (j // 2 + 1) % rows * 2 + j % 2) for j in...]
    ppermute x3, waiting for transfers between devices: 0.01 us -> 8.42 us  [shifted(): return lax.ppermute(x, axis, [(j, (j + k) % n) for j in range(n)])]
    dot_general x1, matrix products: 7.1 us -> 4.03 us  [local(): jnp.dot(context, out_weight, preferred_element_type=jnp.float32)]
    unnamed x29 -> x27, local copies, waits for them, and re-layouts: 12.2 us -> 14.7 us
    reshape x1, local copies, waits for them, and re-layouts: 2.34 us -> 0.28 us  [send_decode(): piece.reshape((layers, capacity, two, blk, local_heads * HD))]
    ppermute x8, waiting for transfers between devices: 27.5 us -> 29.4 us  [partner(): return lax.ppermute(x, 'tensor', [(j, j ^ 1) for j in range(tensor_count)])]
    ppermute x3, starting transfers between devices: 3.01 us -> 1.05 us  [shifted(): return lax.ppermute(x, axis, [(j, (j + k) % n) for j in range(n)])]
    all_to_all x1, waiting for transfers between devices: 1.92 us -> 3.75 us  [local(): lax.all_to_all(split, 'tensor', split_axis=3, concat_axis=3, tiled=True)]
  transfers between devices with their start and end apart: 18 -> 18, of which waited for: 9 -> 11; matrix products, arithmetic and copies ran while one was open for 45% -> 37% of each run, Pallas kernels for 0% -> 0%
where the time goes in v4:
time: 155 us; the launch traced here: 154 us
  waiting for transfers between devices  58.3 us (38%)
  local copies, waits for them, and re-layouts  36.5 us (24%)
  matrix products  24.3 us (16%)
  starting transfers between devices  19.4 us (13%)
  other arithmetic  14.4 us (9%)
    ppermute x8, waiting for transfers between devices, partner(): return lax.ppermute(x, 'tensor', [(j, j ^ 1) for j in range(tensor_count)])  29.4 us
    ppermute x6, waiting for transfers between devices, ring(): lax.ppermute(x, 'tensor', [(j, (j // 2 + 1) % rows * 2 + j % 2) for j in...  16.7 us
    unnamed x27, local copies, waits for them, and re-layouts  14.7 us
    dot_general x1, matrix products, local(): jnp.dot(gathered, qkv_weight, preferred_element_type=jnp.float32) + qkv_bias  12.5 us
    ppermute x8, starting transfers between devices, partner(): return lax.ppermute(x, 'tensor', [(j, j ^ 1) for j in range(tensor_count)])  8.88 us
    ppermute x3, waiting for transfers between devices, shifted(): return lax.ppermute(x, axis, [(j, (j + k) % n) for j in range(n)])  8.42 us
    dot_general x4, matrix products, send_decode(): jnp.einsum('gud,gohdtc->guothc', placement_index, per_head_rows, preferre...  5.79 us
    convert_element_type x3, other arithmetic, scatter_tokens(): arrived = ring(carried.astype(jnp.bfloat16)).astype(jnp.float32)  5.3 us
  transfers between devices with their start and end apart: 18, of which 11 were waited for; matrix products, arithmetic and copies ran while one was open for 37% of the time, Pallas kernels for 0%

profile of v4, /device:TPU:0, one launch (start us, length us, event | category | flops | bytes accessed | tf_op | source)
XLA Modules:
  0.0 153.8 jit_solution(17214208068375223227)
XLA Ops:
  0.6 1.2 convert_reduce_fusion
  1.8 1.2 fusion.53
  3.1 1.9 %constant_dynamic-update-slice_fusion.7 = (bf16[192,7168]{1,0:T(8,128)(2,1)}, bf16[24,7168]{1,0:T(8,128)(2,1)S(1)}) fusion(f32[7168]{0:T(1024)} %param.12, f32[7168]{0:T(1024)} %param.11, f32[24]{0:T(128)S(1)} %add_rsqrt_fusion, f32[24]{0:T(128)S(1)} %broadcast_multiply_fusion, bf16[24,7168]{1,0:T(8,128)(2,1)} %param.10), kind=kLoop, calls=%fused_computation.76 | loop fusion | flops 1032191 | bytes 1089728
  5.0 3.0 %collective-permute-start = (bf16[24,7168]{1,0:T(8,128)(2,1)S(1)}, bf16[24,7168]{1,0:T(8,128)(2,1)S(1)}, u32[]{:S(2)}, u32[]{:S(2)}) collective-permute-start(bf16[24,7168]{1,0:T(8,128)(2,1)S(1)} %get-tuple-element.13), channel_id=1, source_target_pairs={{0,2},{1,3},{2,4},{3,5},{4,6},{5,7},{6,0},{7,1},{8,10},{9,11},{10,... | collective-permute-start | bytes 1032200 | tf_op jit(solution)/shard_map/ppermute | solution.py:73
  8.0 1.5 collective-permute-start.3
  9.8 1.2 slice.62
  11.0 2.0 %gather_fusion = s32[192]{0:T(256)S(1)} fusion(s32[192]{0:T(256)} %param.17, s32[1024]{0:T(1024)S(1)} %pad_clamp_fusion), kind=kCustom, calls=%fused_computation | custom fusion | bytes 2304 | tf_op jit(solution)/shard_map/gather | solution.py:145
  14.0 3.1 %copy.50 = bf16[1,1,2,128,4096]{3,4,2,1,0:T(8,128)(2,1)S(1)} copy(bf16[1,1,2,128,4096]{4,3,2,1,0:T(8,128)(2,1)} %param.18) | data formatting | bytes 4194304 | tf_op args[8]
  20.4 8.8 %collective-permute-done.1 = bf16[24,7168]{1,0:T(8,128)(2,1)S(1)} collective-permute-done((bf16[24,7168]{1,0:T(8,128)(2,1)S(1)}, bf16[24,7168]{1,0:T(8,128)(2,1)S(1)}, u32[]{:S(2)}, u32[]{:S(2)}) %collective-permute-start.1) | collective-permute-done | bytes 344096 | tf_op jit(solution)/shard_map/ppermute | solution.py:73
  29.2 1.3 collective-permute-start.5
  31.2 2.6 %copy.51 = bf16[1,2,4,8,128,128]{5,4,2,1,0,3:T(8,128)(2,1)} copy(bf16[1,2,4,8,128,128]{4,5,2,3,1,0:T(8,128)(2,1)S(1)} %bitcast.138) | data formatting | bytes 4194304 | tf_op jit(solution)/shard_map/optimization_barrier | solution.py:87
  33.8 5.3 %all-to-all-start = ((bf16[1,2,4,8,128,128]{5,4,2,1,0,3:T(8,128)(2,1)}), bf16[1,2,4,8,128,128]{5,4,2,1,0,3:T(8,128)(2,1)S(1)}, u32[]{:S(2)}, u32[]{:S(2)}) async-start(bf16[1,2,4,8,128,128]{5,4,2,1,0,3:T(8,128)(2,1)} %copy.51), calls=%async_computation | async-start | bytes 4194304 | tf_op jit(solution)/shard_map/all_to_all | solution.py:137
  39.4 1.8 %collective-permute-start.6 = (bf16[24,7168]{1,0:T(8,128)(2,1)}, bf16[24,7168]{1,0:T(8,128)(2,1)S(1)}, u32[]{:S(2)}, u32[]{:S(2)}) collective-permute-start(bf16[24,7168]{1,0:T(8,128)(2,1)} %collective-permute-done.2), channel_id=1, source_target_pairs={{0,1},{1,0},{2,3},{3,2},{4,5},{5,4},{6,7},{7,6},{8,9},{9,8},{10,11... | collective-permute-start | bytes 1032200 | tf_op jit(solution)/shard_map/ppermute | solution.py:67
  41.2 1.8 %constant_dynamic-update-slice_fusion.4 = bf16[192,7168]{1,0:T(8,128)(2,1)} fusion(bf16[192,7168]{1,0:T(8,128)(2,1)} %constant_dynamic-update-slice_fusion.5, bf16[24,7168]{1,0:T(8,128)(2,1)} %collective-permute-done.2), kind=kLoop, calls=%fused_computation.73 | loop fusion | bytes 688128
  43.7 1.7 %constant_dynamic-update-slice_fusion.2 = bf16[192,7168]{1,0:T(8,128)(2,1)} fusion(bf16[192,7168]{1,0:T(8,128)(2,1)} %constant_dynamic-update-slice_fusion.3, bf16[24,7168]{1,0:T(8,128)(2,1)} %collective-permute-done.4), kind=kLoop, calls=%fused_computation.71 | loop fusion | bytes 688128
  45.4 1.7 %constant_dynamic-update-slice_fusion.1 = bf16[192,7168]{1,0:T(8,128)(2,1)} fusion(bf16[192,7168]{1,0:T(8,128)(2,1)} %constant_dynamic-update-slice_fusion.2, bf16[24,7168]{1,0:T(8,128)(2,1)} %collective-permute-done.5), kind=kLoop, calls=%fused_computation.70 | loop fusion | bytes 688128
  47.2 18.8 %collective-permute-done.6 = bf16[24,7168]{1,0:T(8,128)(2,1)S(1)} collective-permute-done((bf16[24,7168]{1,0:T(8,128)(2,1)}, bf16[24,7168]{1,0:T(8,128)(2,1)S(1)}, u32[]{:S(2)}, u32[]{:S(2)}) %collective-permute-start.6) | collective-permute-done | bytes 344096 | tf_op jit(solution)/shard_map/ppermute | solution.py:67
  66.8 12.5 %fusion.2 = bf16[192,1536]{1,0:T(8,128)(2,1)S(1)} fusion(bf16[192,7168]{1,0:T(8,128)(2,1)} %constant_dynamic-update-slice_fusion, bf16[7168,1536]{1,0:T(8,128)(2,1)} %param.13, f32[1536]{0:T(1024)S(1)} %copy-done.7), kind=kOutput, calls=%fused_computation.7 | convolution fusion | flops 4228448256 | bytes 25368576 | tf_op jit(solution)/shard_map/dot_general | solution.py:140
  81.8 3.7 %all-to-all-done = bf16[1,2,4,8,128,128]{5,4,2,1,0,3:T(8,128)(2,1)S(1)} async-done(((bf16[1,2,4,8,128,128]{5,4,2,1,0,3:T(8,128)(2,1)}), bf16[1,2,4,8,128,128]{5,4,2,1,0,3:T(8,128)(2,1)S(1)}, u32[]{:S(2)}, u32[]{:S(2)}) %all-to-all-start) | async-done | bytes 2097184 | tf_op jit(solution)/shard_map/all_to_all | solution.py:137
  90.6 4.0 %fusion.99 = (bf16[192,7168]{1,0:T(8,128)(2,1)S(1)}, f32[192,7168]{1,0:T(8,128)}) fusion(bf16[512,7168]{1,0:T(8,128)(2,1)S(1)} %bitcast.140, bf16[4,24,8,128]{3,2,1,0:T(8,128)(2,1)S(1)} %fusion.48), kind=kOutput, calls=%fused_computation.124 | convolution fusion | flops 1410662400 | bytes 15794176 | tf_op jit(solution)/shard_map/dot_general | solution.py:182
  94.6 1.1 fusion.94
  95.7 1.2 collective-permute-start.7
  96.9 1.4 fusion.31
  98.3 1.4 copy.61
  99.7 4.7 %collective-permute-done.7 = bf16[24,7168]{1,0:T(8,128)(2,1)S(1)} collective-permute-done((bf16[24,7168]{1,0:T(8,128)(2,1)}, bf16[24,7168]{1,0:T(8,128)(2,1)S(1)}, u32[]{:S(2)}, u32[]{:S(2)}) %collective-permute-start.7) | collective-permute-done | bytes 344096 | tf_op jit(solution)/shard_map/ppermute | solution.py:67
  104.4 1.7 %collective-permute-start.9 = (bf16[24,7168]{1,0:T(8,128)(2,1)}, bf16[24,7168]{1,0:T(8,128)(2,1)}, u32[]{:S(2)}, u32[]{:S(2)}) collective-permute-start(bf16[24,7168]{1,0:T(8,128)(2,1)} %get-tuple-element.9), channel_id=1, source_target_pairs={{0,1},{1,0},{2,3},{3,2},{4,5},{5,4},{6,7},{7,6},{8,9},{9,8},{10,11... | collective-permute-start | bytes 1032200 | tf_op jit(solution)/shard_map/ppermute | solution.py:67
  106.1 1.9 %fusion.68 = bf16[24,7168]{1,0:T(8,128)(2,1)} fusion(f32[2,4,24,7168]{3,2,1,0:T(8,128)} %bitcast.134, bf16[24,7168]{1,0:T(8,128)(2,1)S(1)} %collective-permute-done.7), kind=kLoop, calls=%fused_computation.59 | loop fusion | flops 516096 | bytes 1376256 | tf_op jit(solution)/shard_map/convert_element_type | solution.py:113
  108.0 1.4 fusion.28
  109.4 1.3 copy.63
  110.8 1.0 collective-permute-start.15
  111.8 1.4 fusion.25
  113.3 1.4 copy.65
  115.0 3.1 %collective-permute-done.8 = bf16[24,7168]{1,0:T(8,128)(2,1)} collective-permute-done((bf16[24,7168]{1,0:T(8,128)(2,1)}, bf16[24,7168]{1,0:T(8,128)(2,1)}, u32[]{:S(2)}, u32[]{:S(2)}) %collective-permute-start.8) | collective-permute-done | bytes 344096 | tf_op jit(solution)/shard_map/ppermute | solution.py:73
  118.0 2.1 %fusion.66 = bf16[24,7168]{1,0:T(8,128)(2,1)} fusion(f32[2,4,24,7168]{3,2,1,0:T(8,128)} %bitcast.135, bf16[24,7168]{1,0:T(8,128)(2,1)} %collective-permute-done.9, bf16[24,7168]{1,0:T(8,128)(2,1)} %collective-permute-done.8), kind=kLoop, calls=%fused_computation.56 | loop fusion | flops 860160 | bytes 1720320 | tf_op jit(solution)/shard_map/convert_element_type | solution.py:113
  120.1 1.4 fusion.34
  123.0 1.7 %copy-done.1 = bf16[1,12,2,128,512]{4,3,2,1,0:T(8,128)(2,1)} copy-done((bf16[1,12,2,128,512]{4,3,2,1,0:T(8,128)(2,1)}, bf16[1,12,2,128,512]{4,3,2,1,0:T(8,128)(2,1)S(1)}, u32[]{:S(2)}) %copy-start.1) | copy-done | bytes 3145752
  124.7 1.5 copy.62
  126.1 2.8 %collective-permute-done.15 = bf16[1,3,2,128,512]{3,4,2,1,0:T(8,128)(2,1)} collective-permute-done((bf16[1,3,2,128,512]{3,4,2,1,0:T(8,128)(2,1)}, bf16[1,3,2,128,512]{3,4,2,1,0:T(8,128)(2,1)}, u32[]{:S(2)}, u32[]{:S(2)}) %collective-permute-start.15) | collective-permute-done | bytes 786464 | tf_op jit(solution)/shard_map/ppermute | solution.py:19
  129.0 1.4 copy.64
  130.4 5.6 %collective-permute-done.16 = bf16[1,3,2,128,512]{3,4,2,1,0:T(8,128)(2,1)} collective-permute-done((bf16[1,3,2,128,512]{3,4,2,1,0:T(8,128)(2,1)}, bf16[1,3,2,128,512]{3,4,2,1,0:T(8,128)(2,1)}, u32[]{:S(2)}, u32[]{:S(2)}) %collective-permute-start.16) | collective-permute-done | bytes 786464 | tf_op jit(solution)/shard_map/ppermute | solution.py:19
  136.0 1.4 copy.66
  137.8 1.3 fusion.63
  139.4 0.9 constant_dynamic-update-slice_fusion.10
  140.3 0.9 constant_dynamic-update-slice_fusion.9
  141.3 0.9 constant_dynamic-update-slice_fusion.8
  142.2 5.9 %collective-permute-done.13 = bf16[24,7168]{1,0:T(8,128)(2,1)S(1)} collective-permute-done((bf16[24,7168]{1,0:T(8,128)(2,1)S(1)}, bf16[24,7168]{1,0:T(8,128)(2,1)S(1)}, u32[]{:S(2)}, u32[]{:S(2)}) %collective-permute-start.13) | collective-permute-done | bytes 344096 | tf_op jit(solution)/shard_map/ppermute | solution.py:67
  148.1 3.7 %collective-permute-done.12 = bf16[24,7168]{1,0:T(8,128)(2,1)S(1)} collective-permute-done((bf16[24,7168]{1,0:T(8,128)(2,1)S(1)}, bf16[24,7168]{1,0:T(8,128)(2,1)S(1)}, u32[]{:S(2)}, u32[]{:S(2)}) %collective-permute-start.12) | collective-permute-done | bytes 344096 | tf_op jit(solution)/shard_map/ppermute | solution.py:73
  151.8 2.0 %fusion.58 = bf16[24,7168]{1,0:T(8,128)(2,1)} fusion(bf16[24,7168]{1,0:T(8,128)(2,1)S(1)} %copy-done, f32[2,4,24,7168]{3,2,1,0:T(8,128)} %bitcast.137, bf16[24,7168]{1,0:T(8,128)(2,1)S(1)} %collective-permute-done.13, bf16[24,7168]{1,0:T(8,128)(2,1)S(1)} %collective-permute-done.12, f32[7168]{0:T(1024)S(1)} %copy-done.5), kind=kLoop, calls=%fused_computation.45 | loop fusion | flops 1376256 | bytes 2093056 | tf_op jit(solution)/shard_map/convert_element_type | solution.py:184
  (78 shorter events, 16.8 us)
Async XLA Ops:
  0.6 12.4 %copy-start.6 = (s32[1,8,1]{1,2,0:T(1,128)S(1)}, s32[1,8,1]{1,2,0:T(1,128)}, u32[]{:S(2)}) copy-start(s32[1,8,1]{1,2,0:T(1,128)} %param.19) | copy-start | bytes 100
  5.0 13.1 %collective-permute-start = (bf16[24,7168]{1,0:T(8,128)(2,1)S(1)}, bf16[24,7168]{1,0:T(8,128)(2,1)S(1)}, u32[]{:S(2)}, u32[]{:S(2)}) collective-permute-start(bf16[24,7168]{1,0:T(8,128)(2,1)S(1)} %get-tuple-element.13), channel_id=1, source_target_pairs={{0,2},{1,3},{2,4},{3,5},{4,6},{5,7},{6,0},{7,1},{8,10},{9,11},{10,... | collective-permute-start | bytes 1032200 | tf_op jit(solution)/shard_map/ppermute | solution.py:73
  8.0 34.9 %collective-permute-start.3 = (bf16[24,7168]{1,0:T(8,128)(2,1)S(1)}, bf16[24,7168]{1,0:T(8,128)(2,1)S(1)}, u32[]{:S(2)}, u32[]{:S(2)}) collective-permute-start(bf16[24,7168]{1,0:T(8,128)(2,1)S(1)} %get-tuple-element.13), channel_id=1, source_target_pairs={{0,1},{1,0},{2,3},{3,2},{4,5},{5,4},{6,7},{7,6},{8,9},{9,8},{10,11... | collective-permute-start | bytes 1032200 | tf_op jit(solution)/shard_map/ppermute | solution.py:67
  18.1 11.0 %collective-permute-start.1 = (bf16[24,7168]{1,0:T(8,128)(2,1)S(1)}, bf16[24,7168]{1,0:T(8,128)(2,1)S(1)}, u32[]{:S(2)}, u32[]{:S(2)}) collective-permute-start(bf16[24,7168]{1,0:T(8,128)(2,1)S(1)} %collective-permute-done), channel_id=1, source_target_pairs={{0,2},{1,3},{2,4},{3,5},{4,6},{5,7},{6,0},{7,1},{8,10},{9,11},{10,... | collective-permute-start | bytes 1032200 | tf_op jit(solution)/shard_map/ppermute | solution.py:73
  18.9 24.8 %collective-permute-start.4 = (bf16[24,7168]{1,0:T(8,128)(2,1)S(1)}, bf16[24,7168]{1,0:T(8,128)(2,1)}, u32[]{:S(2)}, u32[]{:S(2)}) collective-permute-start(bf16[24,7168]{1,0:T(8,128)(2,1)S(1)} %collective-permute-done), channel_id=1, source_target_pairs={{0,1},{1,0},{2,3},{3,2},{4,5},{5,4},{6,7},{7,6},{8,9},{9,8},{10,11... | collective-permute-start | bytes 1032200 | tf_op jit(solution)/shard_map/ppermute | solution.py:67
  29.2 10.2 %collective-permute-start.2 = (bf16[24,7168]{1,0:T(8,128)(2,1)S(1)}, bf16[24,7168]{1,0:T(8,128)(2,1)}, u32[]{:S(2)}, u32[]{:S(2)}) collective-permute-start(bf16[24,7168]{1,0:T(8,128)(2,1)S(1)} %collective-permute-done.1), channel_id=1, source_target_pairs={{0,2},{1,3},{2,4},{3,5},{4,6},{5,7},{6,0},{7,1},{8,10},{9,11},{10,... | collective-permute-start | bytes 1032200 | tf_op jit(solution)/shard_map/ppermute | solution.py:73
  29.2 16.3 %collective-permute-start.5 = (bf16[24,7168]{1,0:T(8,128)(2,1)S(1)}, bf16[24,7168]{1,0:T(8,128)(2,1)}, u32[]{:S(2)}, u32[]{:S(2)}) collective-permute-start(bf16[24,7168]{1,0:T(8,128)(2,1)S(1)} %collective-permute-done.1), channel_id=1, source_target_pairs={{0,1},{1,0},{2,3},{3,2},{4,5},{5,4},{6,7},{7,6},{8,9},{9,8},{10,11... | collective-permute-start | bytes 1032200 | tf_op jit(solution)/shard_map/ppermute | solution.py:67
  33.8 51.7 %all-to-all-start = ((bf16[1,2,4,8,128,128]{5,4,2,1,0,3:T(8,128)(2,1)}), bf16[1,2,4,8,128,128]{5,4,2,1,0,3:T(8,128)(2,1)S(1)}, u32[]{:S(2)}, u32[]{:S(2)}) async-start(bf16[1,2,4,8,128,128]{5,4,2,1,0,3:T(8,128)(2,1)} %copy.51), calls=%async_computation | async-start | bytes 4194304 | tf_op jit(solution)/shard_map/all_to_all | solution.py:137
  39.1 27.7 %copy-start.7 = (f32[1536]{0:T(1024)S(1)}, f32[1536]{0:T(1024)}, u32[]{:S(2)}) copy-start(f32[1536]{0:T(1024)} %param.14) | copy-start | bytes 18436
  39.4 26.6 %collective-permute-start.6 = (bf16[24,7168]{1,0:T(8,128)(2,1)}, bf16[24,7168]{1,0:T(8,128)(2,1)S(1)}, u32[]{:S(2)}, u32[]{:S(2)}) collective-permute-start(bf16[24,7168]{1,0:T(8,128)(2,1)} %collective-permute-done.2), channel_id=1, source_target_pairs={{0,1},{1,0},{2,3},{3,2},{4,5},{5,4},{6,7},{7,6},{8,9},{9,8},{10,11... | collective-permute-start | bytes 1032200 | tf_op jit(solution)/shard_map/ppermute | solution.py:67
  80.6 0.7 copy-start.2
  85.5 1.0 copy-start.3
  87.2 2.5 %slice-start = ((s8[7340032]{0:T(1024)(128)(4,1)}), s8[4194304]{0:T(1024)(128)(4,1)S(1)}, s32[]{:S(2)}) async-start(s8[7340032]{0:T(1024)(128)(4,1)} %bitcast.139), calls=%async_computation.1 | async-start | bytes 8388608
  87.9 2.6 %slice-start.1 = ((s8[7340032]{0:T(1024)(128)(4,1)}), s8[3145728]{0:T(1024)(128)(4,1)S(1)}, s32[]{:S(2)}) async-start(s8[7340032]{0:T(1024)(128)(4,1)} %bitcast.139), calls=%async_computation.2 | async-start | bytes 6291456
  95.7 8.7 %collective-permute-start.7 = (bf16[24,7168]{1,0:T(8,128)(2,1)}, bf16[24,7168]{1,0:T(8,128)(2,1)S(1)}, u32[]{:S(2)}, u32[]{:S(2)}) collective-permute-start(bf16[24,7168]{1,0:T(8,128)(2,1)} %get-tuple-element.14), channel_id=1, source_target_pairs={{0,1},{1,0},{2,3},{3,2},{4,5},{5,4},{6,7},{7,6},{8,9},{9,8},{10,11... | collective-permute-start | bytes 1032200 | tf_op jit(solution)/shard_map/ppermute | solution.py:67
  99.7 25.0 %collective-permute-start.14 = (bf16[1,3,2,128,512]{3,4,2,1,0:T(8,128)(2,1)}, bf16[1,3,2,128,512]{3,4,2,1,0:T(8,128)(2,1)}, u32[]{:S(2)}, u32[]{:S(2)}) collective-permute-start(bf16[1,3,2,128,512]{3,4,2,1,0:T(8,128)(2,1)} %bitcast.144), channel_id=1, source_target_pairs={{0,8},{8,16},{16,24},{24,0},{1,9},{9,17},{17,25},{25,1},{2,10},{10... | collective-permute-start | bytes 2359304 | tf_op jit(solution)/shard_map/ppermute | solution.py:19
  104.4 10.3 %collective-permute-start.9 = (bf16[24,7168]{1,0:T(8,128)(2,1)}, bf16[24,7168]{1,0:T(8,128)(2,1)}, u32[]{:S(2)}, u32[]{:S(2)}) collective-permute-start(bf16[24,7168]{1,0:T(8,128)(2,1)} %get-tuple-element.9), channel_id=1, source_target_pairs={{0,1},{1,0},{2,3},{3,2},{4,5},{5,4},{6,7},{7,6},{8,9},{9,8},{10,11... | collective-permute-start | bytes 1032200 | tf_op jit(solution)/shard_map/ppermute | solution.py:67
  108.0 10.0 %collective-permute-start.8 = (bf16[24,7168]{1,0:T(8,128)(2,1)}, bf16[24,7168]{1,0:T(8,128)(2,1)}, u32[]{:S(2)}, u32[]{:S(2)}) collective-permute-start(bf16[24,7168]{1,0:T(8,128)(2,1)} %fusion.68), channel_id=1, source_target_pairs={{0,2},{1,3},{2,4},{3,5},{4,6},{5,7},{6,0},{7,1},{8,10},{9,11},{10,... | collective-permute-start | bytes 1032200 | tf_op jit(solution)/shard_map/ppermute | solution.py:73
  110.8 18.2 %collective-permute-start.15 = (bf16[1,3,2,128,512]{3,4,2,1,0:T(8,128)(2,1)}, bf16[1,3,2,128,512]{3,4,2,1,0:T(8,128)(2,1)}, u32[]{:S(2)}, u32[]{:S(2)}) collective-permute-start(bf16[1,3,2,128,512]{3,4,2,1,0:T(8,128)(2,1)} %bitcast.145), channel_id=1, source_target_pairs={{0,16},{8,24},{16,0},{24,8},{1,17},{9,25},{17,1},{25,9},{2,18},{10... | collective-permute-start | bytes 2359304 | tf_op jit(solution)/shard_map/ppermute | solution.py:19
  114.7 21.3 %collective-permute-start.16 = (bf16[1,3,2,128,512]{3,4,2,1,0:T(8,128)(2,1)}, bf16[1,3,2,128,512]{3,4,2,1,0:T(8,128)(2,1)}, u32[]{:S(2)}, u32[]{:S(2)}) collective-permute-start(bf16[1,3,2,128,512]{3,4,2,1,0:T(8,128)(2,1)} %bitcast.146), channel_id=1, source_target_pairs={{0,24},{8,0},{16,8},{24,16},{1,25},{9,1},{17,9},{25,17},{2,26},{10... | collective-permute-start | bytes 2359304 | tf_op jit(solution)/shard_map/ppermute | solution.py:19
  114.7 22.7 %collective-permute-start.11 = (bf16[24,7168]{1,0:T(8,128)(2,1)}, bf16[24,7168]{1,0:T(8,128)(2,1)S(1)}, u32[]{:S(2)}, u32[]{:S(2)}) collective-permute-start(bf16[24,7168]{1,0:T(8,128)(2,1)} %get-tuple-element.10), channel_id=1, source_target_pairs={{0,1},{1,0},{2,3},{3,2},{4,5},{5,4},{6,7},{7,6},{8,9},{9,8},{10,11... | collective-permute-start | bytes 1032200 | tf_op jit(solution)/shard_map/ppermute | solution.py:67
  120.1 17.6 %collective-permute-start.10 = (bf16[24,7168]{1,0:T(8,128)(2,1)}, bf16[24,7168]{1,0:T(8,128)(2,1)}, u32[]{:S(2)}, u32[]{:S(2)}) collective-permute-start(bf16[24,7168]{1,0:T(8,128)(2,1)} %fusion.66), channel_id=1, source_target_pairs={{0,2},{1,3},{2,4},{3,5},{4,6},{5,7},{6,0},{7,1},{8,10},{9,11},{10,... | collective-permute-start | bytes 1032200 | tf_op jit(solution)/shard_map/ppermute | solution.py:73
  123.0 1.7 %copy-start.1 = (bf16[1,12,2,128,512]{4,3,2,1,0:T(8,128)(2,1)}, bf16[1,12,2,128,512]{4,3,2,1,0:T(8,128)(2,1)S(1)}, u32[]{:S(2)}) copy-start(bf16[1,12,2,128,512]{4,3,2,1,0:T(8,128)(2,1)S(1)} %constant_dynamic-update-slice_fusion.11) | copy-start | bytes 9437188
  124.7 12.7 %copy-start.4 = (bf16[24,7168]{1,0:T(8,128)(2,1)S(1)}, bf16[24,7168]{1,0:T(8,128)(2,1)}, u32[]{:S(2)}) copy-start(bf16[24,7168]{1,0:T(8,128)(2,1)} %get-tuple-element.11) | copy-start | bytes 1032196
  137.4 10.7 %collective-permute-start.13 = (bf16[24,7168]{1,0:T(8,128)(2,1)S(1)}, bf16[24,7168]{1,0:T(8,128)(2,1)S(1)}, u32[]{:S(2)}, u32[]{:S(2)}) collective-permute-start(bf16[24,7168]{1,0:T(8,128)(2,1)S(1)} %copy-done.4), channel_id=1, source_target_pairs={{0,1},{1,0},{2,3},{3,2},{4,5},{5,4},{6,7},{7,6},{8,9},{9,8},{10,11... | collective-permute-start | bytes 1032200 | tf_op jit(solution)/shard_map/ppermute | solution.py:67
  139.0 12.8 %copy-start = (bf16[24,7168]{1,0:T(8,128)(2,1)S(1)}, bf16[24,7168]{1,0:T(8,128)(2,1)}, u32[]{:S(2)}) copy-start(bf16[24,7168]{1,0:T(8,128)(2,1)} %param.10) | copy-start | bytes 1032196
  139.1 12.8 %copy-start.5 = (f32[7168]{0:T(1024)S(1)}, f32[7168]{0:T(1024)}, u32[]{:S(2)}) copy-start(f32[7168]{0:T(1024)} %param.16) | copy-start | bytes 86020
  139.1 12.8 %collective-permute-start.12 = (bf16[24,7168]{1,0:T(8,128)(2,1)S(1)}, bf16[24,7168]{1,0:T(8,128)(2,1)S(1)}, u32[]{:S(2)}, u32[]{:S(2)}) collective-permute-start(bf16[24,7168]{1,0:T(8,128)(2,1)S(1)} %fusion.63), channel_id=1, source_target_pairs={{0,2},{1,3},{2,4},{3,5},{4,6},{5,7},{6,0},{7,1},{8,10},{9,11},{10,... | collective-permute-start | bytes 1032200 | tf_op jit(solution)/shard_map/ppermute | solution.py:73

commit v5 on v4

--- a/solution.py
+++ b/solution.py
@@ -7,6 +7,7 @@
 RELAY_STEP = 0
 CACHE_STEP = 2
 CHAIN_PARTNER = True
+CHAIN_RELAY = True
 
 
 def normalize(x, gain, shift):
@@ -55,8 +56,14 @@
     i = lax.axis_index("pipe")
     layers, capacity = outgoing[0].shape[:2]
     arrived = jnp.zeros((layers, pipe_count * capacity) + outgoing[0].shape[2:], outgoing[0].dtype)
+    previous = None
     for k in range(pipe_count):
-        piece = outgoing[k] if k == 0 else shifted(outgoing[k], "pipe", k, pipe_count)
+        piece = outgoing[k]
+        if k > 0:
+            if previous is not None and CHAIN_RELAY:
+                piece, previous = lax.optimization_barrier((piece, previous))
+            piece = shifted(piece, "pipe", k, pipe_count)
+            previous = piece
         arrived = lax.dynamic_update_slice_in_dim(
             arrived, piece, ((i - k) % pipe_count) * capacity, axis=1
         )

time: 155 us -> 153 us (0.987)
  waiting for transfers between devices: 58.3 us -> 52.6 us
  matrix products: 24.3 us -> 26 us
    ppermute x3, waiting for transfers between devices: 8.42 us -> 5.47 us  [shifted(): return lax.ppermute(x, axis, [(j, (j + k) % n) for j in range(n)])]
    all_to_all x1, waiting for transfers between devices: 3.75 us -> 1.99 us  [local(): lax.all_to_all(split, 'tensor', split_axis=3, concat_axis=3, tiled=True)]
    broadcast_in_dim x1, local copies, waits for them, and re-layouts: 0.33 us -> 2 us  [receive_decode(): jnp.zeros((layers, pipe_count * capacity) + outgoing[0].shape[2:], outgoi...]
    ppermute x8, waiting for transfers between devices: 29.4 us -> 27.8 us  [partner(): return lax.ppermute(x, 'tensor', [(j, j ^ 1) for j in range(tensor_count)])]
    ppermute x8, starting transfers between devices: 8.88 us -> 10.5 us  [partner(): return lax.ppermute(x, 'tensor', [(j, j ^ 1) for j in range(tensor_count)])]
    unnamed x27 -> x25, local copies, waits for them, and re-layouts: 14.7 us -> 13.3 us
  transfers between devices with their start and end apart: 18 -> 18, of which waited for: 11 -> 11; matrix products, arithmetic and copies ran while one was open for 37% -> 40% of each run, Pallas kernels for 0% -> 0%
where the time goes in v5:
time: 153 us; the launch traced here: 151 us
  waiting for transfers between devices  52.6 us (34%)
  local copies, waits for them, and re-layouts  36.6 us (24%)
  matrix products  26 us (17%)
  starting transfers between devices  20.6 us (13%)
  other arithmetic  14.6 us (10%)
    ppermute x8, waiting for transfers between devices, partner(): return lax.ppermute(x, 'tensor', [(j, j ^ 1) for j in range(tensor_count)])  27.8 us
    ppermute x6, waiting for transfers between devices, ring(): lax.ppermute(x, 'tensor', [(j, (j // 2 + 1) % rows * 2 + j % 2) for j in...  17.3 us
    dot_general x1, matrix products, local(): jnp.dot(gathered, qkv_weight, preferred_element_type=jnp.float32) + qkv_bias  13.3 us
    unnamed x25, local copies, waits for them, and re-layouts  13.3 us
    ppermute x8, starting transfers between devices, partner(): return lax.ppermute(x, 'tensor', [(j, j ^ 1) for j in range(tensor_count)])  10.5 us
    dot_general x4, matrix products, send_decode(): jnp.einsum('gud,gohdtc->guothc', placement_index, per_head_rows, preferre...  6.77 us
    ppermute x3, waiting for transfers between devices, shifted(): return lax.ppermute(x, axis, [(j, (j + k) % n) for j in range(n)])  5.47 us
    convert_element_type x3, other arithmetic, scatter_tokens(): arrived = ring(carried.astype(jnp.bfloat16)).astype(jnp.float32)  5.33 us
  transfers between devices with their start and end apart: 18, of which 11 were waited for; matrix products, arithmetic and copies ran while one was open for 40% of the time, Pallas kernels for 0%

profile of v5, /device:TPU:0, one launch (start us, length us, event | category | flops | bytes accessed | tf_op | source)
XLA Modules:
  0.0 151.4 jit_solution(18293799910639144887)
XLA Ops:
  0.6 1.2 convert_reduce_fusion
  1.8 1.2 fusion.53
  3.1 1.9 %constant_dynamic-update-slice_fusion.7 = (bf16[192,7168]{1,0:T(8,128)(2,1)}, bf16[24,7168]{1,0:T(8,128)(2,1)S(1)}) fusion(f32[7168]{0:T(1024)} %param.12, f32[7168]{0:T(1024)} %param.11, f32[24]{0:T(128)S(1)} %add_rsqrt_fusion, f32[24]{0:T(128)S(1)} %broadcast_multiply_fusion, bf16[24,7168]{1,0:T(8,128)(2,1)} %param.10), kind=kLoop, calls=%fused_computation.76 | loop fusion | flops 1032191 | bytes 1089728
  5.0 3.0 %collective-permute-start = (bf16[24,7168]{1,0:T(8,128)(2,1)S(1)}, bf16[24,7168]{1,0:T(8,128)(2,1)S(1)}, u32[]{:S(2)}, u32[]{:S(2)}) collective-permute-start(bf16[24,7168]{1,0:T(8,128)(2,1)S(1)} %get-tuple-element.17), channel_id=1, source_target_pairs={{0,2},{1,3},{2,4},{3,5},{4,6},{5,7},{6,0},{7,1},{8,10},{9,11},{10,... | collective-permute-start | bytes 1032200 | tf_op jit(solution)/shard_map/ppermute | solution.py:80
  8.0 1.5 %collective-permute-start.3 = (bf16[24,7168]{1,0:T(8,128)(2,1)S(1)}, bf16[24,7168]{1,0:T(8,128)(2,1)S(1)}, u32[]{:S(2)}, u32[]{:S(2)}) collective-permute-start(bf16[24,7168]{1,0:T(8,128)(2,1)S(1)} %get-tuple-element.17), channel_id=1, source_target_pairs={{0,1},{1,0},{2,3},{3,2},{4,5},{5,4},{6,7},{7,6},{8,9},{9,8},{10,11... | collective-permute-start | bytes 1032200 | tf_op jit(solution)/shard_map/ppermute | solution.py:74
  9.8 1.2 slice.62
  11.0 2.0 %gather_fusion = s32[192]{0:T(256)S(1)} fusion(s32[192]{0:T(256)} %param.17, s32[1024]{0:T(1024)S(1)} %pad_clamp_fusion), kind=kCustom, calls=%fused_computation | custom fusion | bytes 2304 | tf_op jit(solution)/shard_map/gather | solution.py:152
  13.7 3.1 %copy.50 = bf16[1,1,2,128,4096]{3,4,2,1,0:T(8,128)(2,1)S(1)} copy(bf16[1,1,2,128,4096]{4,3,2,1,0:T(8,128)(2,1)} %param.18) | data formatting | bytes 4194304 | tf_op args[8]
  17.0 1.1 collective-permute-done
  18.7 1.0 collective-permute-start.4
  20.4 8.8 %collective-permute-done.1 = bf16[24,7168]{1,0:T(8,128)(2,1)S(1)} collective-permute-done((bf16[24,7168]{1,0:T(8,128)(2,1)S(1)}, bf16[24,7168]{1,0:T(8,128)(2,1)S(1)}, u32[]{:S(2)}, u32[]{:S(2)}) %collective-permute-start.1) | collective-permute-done | bytes 344096 | tf_op jit(solution)/shard_map/ppermute | solution.py:80
  29.2 1.3 collective-permute-start.5
  31.2 2.6 %copy.51 = bf16[1,2,4,8,128,128]{5,4,2,1,0,3:T(8,128)(2,1)} copy(bf16[1,2,4,8,128,128]{4,5,2,3,1,0:T(8,128)(2,1)S(1)} %bitcast.138) | data formatting | bytes 4194304 | tf_op jit(solution)/shard_map/optimization_barrier | solution.py:94
  33.8 5.3 %all-to-all-start = ((bf16[1,2,4,8,128,128]{5,4,2,1,0,3:T(8,128)(2,1)}), bf16[1,2,4,8,128,128]{5,4,2,1,0,3:T(8,128)(2,1)S(1)}, u32[]{:S(2)}, u32[]{:S(2)}) async-start(bf16[1,2,4,8,128,128]{5,4,2,1,0,3:T(8,128)(2,1)} %copy.51), calls=%async_computation | async-start | bytes 4194304 | tf_op jit(solution)/shard_map/all_to_all | solution.py:144
  39.4 1.8 %collective-permute-start.6 = (bf16[24,7168]{1,0:T(8,128)(2,1)}, bf16[24,7168]{1,0:T(8,128)(2,1)S(1)}, u32[]{:S(2)}, u32[]{:S(2)}) collective-permute-start(bf16[24,7168]{1,0:T(8,128)(2,1)} %collective-permute-done.2), channel_id=1, source_target_pairs={{0,1},{1,0},{2,3},{3,2},{4,5},{5,4},{6,7},{7,6},{8,9},{9,8},{10,11... | collective-permute-start | bytes 1032200 | tf_op jit(solution)/shard_map/ppermute | solution.py:74
  41.2 1.8 %constant_dynamic-update-slice_fusion.4 = bf16[192,7168]{1,0:T(8,128)(2,1)} fusion(bf16[192,7168]{1,0:T(8,128)(2,1)} %constant_dynamic-update-slice_fusion.5, bf16[24,7168]{1,0:T(8,128)(2,1)} %collective-permute-done.2), kind=kLoop, calls=%fused_computation.73 | loop fusion | bytes 688128
  43.7 1.7 %constant_dynamic-update-slice_fusion.2 = bf16[192,7168]{1,0:T(8,128)(2,1)} fusion(bf16[192,7168]{1,0:T(8,128)(2,1)} %constant_dynamic-update-slice_fusion.3, bf16[24,7168]{1,0:T(8,128)(2,1)} %collective-permute-done.4), kind=kLoop, calls=%fused_computation.71 | loop fusion | bytes 688128
  45.5 1.7 %constant_dynamic-update-slice_fusion.1 = bf16[192,7168]{1,0:T(8,128)(2,1)} fusion(bf16[192,7168]{1,0:T(8,128)(2,1)} %constant_dynamic-update-slice_fusion.2, bf16[24,7168]{1,0:T(8,128)(2,1)} %collective-permute-done.5), kind=kLoop, calls=%fused_computation.70 | loop fusion | bytes 688128
  47.2 18.8 %collective-permute-done.6 = bf16[24,7168]{1,0:T(8,128)(2,1)S(1)} collective-permute-done((bf16[24,7168]{1,0:T(8,128)(2,1)}, bf16[24,7168]{1,0:T(8,128)(2,1)S(1)}, u32[]{:S(2)}, u32[]{:S(2)}) %collective-permute-start.6) | collective-permute-done | bytes 344096 | tf_op jit(solution)/shard_map/ppermute | solution.py:74
  66.8 13.3 %fusion.2 = bf16[192,1536]{1,0:T(8,128)(2,1)} fusion(bf16[192,7168]{1,0:T(8,128)(2,1)} %constant_dynamic-update-slice_fusion, bf16[7168,1536]{1,0:T(8,128)(2,1)} %param.13, f32[1536]{0:T(1024)S(1)} %copy-done.6), kind=kOutput, calls=%fused_computation.7 | convolution fusion | flops 4228448256 | bytes 25368576 | tf_op jit(solution)/shard_map/dot_general | solution.py:147
  80.1 1.4 reshape.413
  83.5 2.0 %all-to-all-done = bf16[1,2,4,8,128,128]{5,4,2,1,0,3:T(8,128)(2,1)S(1)} async-done(((bf16[1,2,4,8,128,128]{5,4,2,1,0,3:T(8,128)(2,1)}), bf16[1,2,4,8,128,128]{5,4,2,1,0,3:T(8,128)(2,1)S(1)}, u32[]{:S(2)}, u32[]{:S(2)}) %all-to-all-start) | async-done | bytes 2097184 | tf_op jit(solution)/shard_map/all_to_all | solution.py:144
  90.6 4.0 %fusion.99 = (bf16[192,7168]{1,0:T(8,128)(2,1)S(1)}, f32[192,7168]{1,0:T(8,128)}) fusion(bf16[512,7168]{1,0:T(8,128)(2,1)S(1)} %bitcast.140, bf16[4,24,8,128]{3,2,1,0:T(8,128)(2,1)S(1)} %fusion.48), kind=kOutput, calls=%fused_computation.124 | convolution fusion | flops 1410662400 | bytes 15794176 | tf_op jit(solution)/shard_map/dot_general | solution.py:189
  94.6 1.0 fusion.94
  95.6 1.2 collective-permute-start.7
  97.0 7.1 %collective-permute-done.7 = bf16[24,7168]{1,0:T(8,128)(2,1)S(1)} collective-permute-done((bf16[24,7168]{1,0:T(8,128)(2,1)S(1)}, bf16[24,7168]{1,0:T(8,128)(2,1)S(1)}, u32[]{:S(2)}, u32[]{:S(2)}) %collective-permute-start.7) | collective-permute-done | bytes 344096 | tf_op jit(solution)/shard_map/ppermute | solution.py:74
  104.0 1.7 %collective-permute-start.9 = (bf16[24,7168]{1,0:T(8,128)(2,1)}, bf16[24,7168]{1,0:T(8,128)(2,1)S(1)}, u32[]{:S(2)}, u32[]{:S(2)}) collective-permute-start(bf16[24,7168]{1,0:T(8,128)(2,1)} %get-tuple-element.11), channel_id=1, source_target_pairs={{0,1},{1,0},{2,3},{3,2},{4,5},{5,4},{6,7},{7,6},{8,9},{9,8},{10,11... | collective-permute-start | bytes 1032200 | tf_op jit(solution)/shard_map/ppermute | solution.py:74
  105.8 1.9 %fusion.68 = bf16[24,7168]{1,0:T(8,128)(2,1)} fusion(f32[2,4,24,7168]{3,2,1,0:T(8,128)} %bitcast.134, bf16[24,7168]{1,0:T(8,128)(2,1)S(1)} %collective-permute-done.7), kind=kLoop, calls=%fused_computation.59 | loop fusion | flops 516096 | bytes 1376256 | tf_op jit(solution)/shard_map/convert_element_type | solution.py:120
  107.7 1.4 fusion.31
  109.1 1.3 copy.61
  110.5 1.9 %collective-permute-done.9 = bf16[24,7168]{1,0:T(8,128)(2,1)S(1)} collective-permute-done((bf16[24,7168]{1,0:T(8,128)(2,1)}, bf16[24,7168]{1,0:T(8,128)(2,1)S(1)}, u32[]{:S(2)}, u32[]{:S(2)}) %collective-permute-start.9) | collective-permute-done | bytes 344096 | tf_op jit(solution)/shard_map/ppermute | solution.py:74
  112.3 1.7 %collective-permute-start.11 = (bf16[24,7168]{1,0:T(8,128)(2,1)}, bf16[24,7168]{1,0:T(8,128)(2,1)}, u32[]{:S(2)}, u32[]{:S(2)}) collective-permute-start(bf16[24,7168]{1,0:T(8,128)(2,1)} %get-tuple-element.12), channel_id=1, source_target_pairs={{0,1},{1,0},{2,3},{3,2},{4,5},{5,4},{6,7},{7,6},{8,9},{9,8},{10,11... | collective-permute-start | bytes 1032200 | tf_op jit(solution)/shard_map/ppermute | solution.py:74
  114.1 3.5 %collective-permute-done.8 = bf16[24,7168]{1,0:T(8,128)(2,1)} collective-permute-done((bf16[24,7168]{1,0:T(8,128)(2,1)}, bf16[24,7168]{1,0:T(8,128)(2,1)}, u32[]{:S(2)}, u32[]{:S(2)}) %collective-permute-start.8) | collective-permute-done | bytes 344096 | tf_op jit(solution)/shard_map/ppermute | solution.py:80
  117.6 2.0 %fusion.66 = bf16[24,7168]{1,0:T(8,128)(2,1)} fusion(f32[2,4,24,7168]{3,2,1,0:T(8,128)} %bitcast.135, bf16[24,7168]{1,0:T(8,128)(2,1)S(1)} %collective-permute-done.9, bf16[24,7168]{1,0:T(8,128)(2,1)} %collective-permute-done.8), kind=kLoop, calls=%fused_computation.56 | loop fusion | flops 860160 | bytes 1720320 | tf_op jit(solution)/shard_map/convert_element_type | solution.py:120
  119.7 1.4 fusion.28
  121.1 1.3 copy.63
  122.5 1.4 fusion.34
  123.9 1.1 collective-permute-start.15
  125.3 3.7 %collective-permute-done.10 = bf16[24,7168]{1,0:T(8,128)(2,1)} collective-permute-done((bf16[24,7168]{1,0:T(8,128)(2,1)}, bf16[24,7168]{1,0:T(8,128)(2,1)}, u32[]{:S(2)}, u32[]{:S(2)}) %collective-permute-start.10) | collective-permute-done | bytes 344096 | tf_op jit(solution)/shard_map/ppermute | solution.py:80
  129.0 1.4 fusion.63
  130.5 2.4 %fusion.25 = bf16[1,3,2,128,4,128]{5,1,3,4,2,0:T(4,128)(2,1)} fusion(bf16[1,2,4,8,128,128]{5,4,2,1,0,3:T(8,128)(2,1)S(1)} %all-to-all-done, s32[8]{0:T(128)S(1)} %multiply_add_fusion, s32[3]{0:T(128)S(1)} %iota_add_fusion.1), kind=kOutput, calls=%fused_computation.22 | convolution fusion | flops 6684696 | bytes 2883628 | tf_op jit(solution)/shard_map/gud,gohdtc->guothc/dot_general | solution.py:47
  134.8 2.0 %broadcast_in_dim.22 = bf16[1,12,2,128,512]{4,3,2,1,0:T(8,128)(2,1)} broadcast(bf16[]{:T(256)} %constant.111.clone.1), dimensions={} | broadcast | bytes 3145730 | tf_op jit(solution)/shard_map/broadcast_in_dim | solution.py:58
  137.8 1.4 copy.62
  139.2 1.0 constant_dynamic-update-slice_fusion.10
  140.7 2.2 %fusion.58 = bf16[24,7168]{1,0:T(8,128)(2,1)} fusion(bf16[24,7168]{1,0:T(8,128)(2,1)S(1)} %copy-done, f32[2,4,24,7168]{3,2,1,0:T(8,128)} %bitcast.137, bf16[24,7168]{1,0:T(8,128)(2,1)} %collective-permute-done.13, bf16[24,7168]{1,0:T(8,128)(2,1)} %collective-permute-done.12, f32[7168]{0:T(1024)S(1)} %copy-done.4), kind=kLoop, calls=%fused_computation.45 | loop fusion | flops 1376256 | bytes 2093056 | tf_op jit(solution)/shard_map/convert_element_type | solution.py:191
  142.9 1.4 copy.64
  145.2 4.9 %collective-permute-done.16 = bf16[1,3,2,128,512]{3,4,2,1,0:T(8,128)(2,1)S(1)} collective-permute-done((bf16[1,3,2,128,512]{3,4,2,1,0:T(8,128)(2,1)S(1)}, bf16[1,3,2,128,512]{3,4,2,1,0:T(8,128)(2,1)S(1)}, u32[]{:S(2)}, u32[]{:S(2)}) %collective-permute-start.16) | collective-permute-done | bytes 786464 | tf_op jit(solution)/shard_map/ppermute | solution.py:20
  150.5 0.9 constant_dynamic-update-slice_fusion.8
  (76 shorter events, 17.1 us)
Async XLA Ops:
  0.6 12.4 %copy-start.5 = (s32[1,8,1]{1,2,0:T(1,128)S(1)}, s32[1,8,1]{1,2,0:T(1,128)}, u32[]{:S(2)}) copy-start(s32[1,8,1]{1,2,0:T(1,128)} %param.19) | copy-start | bytes 100
  5.0 13.1 %collective-permute-start = (bf16[24,7168]{1,0:T(8,128)(2,1)S(1)}, bf16[24,7168]{1,0:T(8,128)(2,1)S(1)}, u32[]{:S(2)}, u32[]{:S(2)}) collective-permute-start(bf16[24,7168]{1,0:T(8,128)(2,1)S(1)} %get-tuple-element.17), channel_id=1, source_target_pairs={{0,2},{1,3},{2,4},{3,5},{4,6},{5,7},{6,0},{7,1},{8,10},{9,11},{10,... | collective-permute-start | bytes 1032200 | tf_op jit(solution)/shard_map/ppermute | solution.py:80
  8.0 34.9 %collective-permute-start.3 = (bf16[24,7168]{1,0:T(8,128)(2,1)S(1)}, bf16[24,7168]{1,0:T(8,128)(2,1)S(1)}, u32[]{:S(2)}, u32[]{:S(2)}) collective-permute-start(bf16[24,7168]{1,0:T(8,128)(2,1)S(1)} %get-tuple-element.17), channel_id=1, source_target_pairs={{0,1},{1,0},{2,3},{3,2},{4,5},{5,4},{6,7},{7,6},{8,9},{9,8},{10,11... | collective-permute-start | bytes 1032200 | tf_op jit(solution)/shard_map/ppermute | solution.py:74
  18.1 11.0 %collective-permute-start.1 = (bf16[24,7168]{1,0:T(8,128)(2,1)S(1)}, bf16[24,7168]{1,0:T(8,128)(2,1)S(1)}, u32[]{:S(2)}, u32[]{:S(2)}) collective-permute-start(bf16[24,7168]{1,0:T(8,128)(2,1)S(1)} %collective-permute-done), channel_id=1, source_target_pairs={{0,2},{1,3},{2,4},{3,5},{4,6},{5,7},{6,0},{7,1},{8,10},{9,11},{10,... | collective-permute-start | bytes 1032200 | tf_op jit(solution)/shard_map/ppermute | solution.py:80
  18.7 25.0 %collective-permute-start.4 = (bf16[24,7168]{1,0:T(8,128)(2,1)S(1)}, bf16[24,7168]{1,0:T(8,128)(2,1)}, u32[]{:S(2)}, u32[]{:S(2)}) collective-permute-start(bf16[24,7168]{1,0:T(8,128)(2,1)S(1)} %collective-permute-done), channel_id=1, source_target_pairs={{0,1},{1,0},{2,3},{3,2},{4,5},{5,4},{6,7},{7,6},{8,9},{9,8},{10,11... | collective-permute-start | bytes 1032200 | tf_op jit(solution)/shard_map/ppermute | solution.py:74
  29.2 10.2 %collective-permute-start.2 = (bf16[24,7168]{1,0:T(8,128)(2,1)S(1)}, bf16[24,7168]{1,0:T(8,128)(2,1)}, u32[]{:S(2)}, u32[]{:S(2)}) collective-permute-start(bf16[24,7168]{1,0:T(8,128)(2,1)S(1)} %collective-permute-done.1), channel_id=1, source_target_pairs={{0,2},{1,3},{2,4},{3,5},{4,6},{5,7},{6,0},{7,1},{8,10},{9,11},{10,... | collective-permute-start | bytes 1032200 | tf_op jit(solution)/shard_map/ppermute | solution.py:80
  29.2 16.3 %collective-permute-start.5 = (bf16[24,7168]{1,0:T(8,128)(2,1)S(1)}, bf16[24,7168]{1,0:T(8,128)(2,1)}, u32[]{:S(2)}, u32[]{:S(2)}) collective-permute-start(bf16[24,7168]{1,0:T(8,128)(2,1)S(1)} %collective-permute-done.1), channel_id=1, source_target_pairs={{0,1},{1,0},{2,3},{3,2},{4,5},{5,4},{6,7},{7,6},{8,9},{9,8},{10,11... | collective-permute-start | bytes 1032200 | tf_op jit(solution)/shard_map/ppermute | solution.py:74
  33.8 51.7 %all-to-all-start = ((bf16[1,2,4,8,128,128]{5,4,2,1,0,3:T(8,128)(2,1)}), bf16[1,2,4,8,128,128]{5,4,2,1,0,3:T(8,128)(2,1)S(1)}, u32[]{:S(2)}, u32[]{:S(2)}) async-start(bf16[1,2,4,8,128,128]{5,4,2,1,0,3:T(8,128)(2,1)} %copy.51), calls=%async_computation | async-start | bytes 4194304 | tf_op jit(solution)/shard_map/all_to_all | solution.py:144
  39.1 27.7 %copy-start.6 = (f32[1536]{0:T(1024)S(1)}, f32[1536]{0:T(1024)}, u32[]{:S(2)}) copy-start(f32[1536]{0:T(1024)} %param.14) | copy-start | bytes 18436
  39.4 26.6 %collective-permute-start.6 = (bf16[24,7168]{1,0:T(8,128)(2,1)}, bf16[24,7168]{1,0:T(8,128)(2,1)S(1)}, u32[]{:S(2)}, u32[]{:S(2)}) collective-permute-start(bf16[24,7168]{1,0:T(8,128)(2,1)} %collective-permute-done.2), channel_id=1, source_target_pairs={{0,1},{1,0},{2,3},{3,2},{4,5},{5,4},{6,7},{7,6},{8,9},{9,8},{10,11... | collective-permute-start | bytes 1032200 | tf_op jit(solution)/shard_map/ppermute | solution.py:74
  82.4 0.7 copy-start.2
  85.5 1.0 copy-start.3
  87.2 2.5 %slice-start = ((s8[7340032]{0:T(1024)(128)(4,1)}), s8[4194304]{0:T(1024)(128)(4,1)S(1)}, s32[]{:S(2)}) async-start(s8[7340032]{0:T(1024)(128)(4,1)} %bitcast.139), calls=%async_computation.1 | async-start | bytes 8388608
  87.9 2.6 %slice-start.1 = ((s8[7340032]{0:T(1024)(128)(4,1)}), s8[3145728]{0:T(1024)(128)(4,1)S(1)}, s32[]{:S(2)}) async-start(s8[7340032]{0:T(1024)(128)(4,1)} %bitcast.139), calls=%async_computation.2 | async-start | bytes 6291456
  95.6 8.5 %collective-permute-start.7 = (bf16[24,7168]{1,0:T(8,128)(2,1)S(1)}, bf16[24,7168]{1,0:T(8,128)(2,1)S(1)}, u32[]{:S(2)}, u32[]{:S(2)}) collective-permute-start(bf16[24,7168]{1,0:T(8,128)(2,1)S(1)} %get-tuple-element.18), channel_id=1, source_target_pairs={{0,1},{1,0},{2,3},{3,2},{4,5},{5,4},{6,7},{7,6},{8,9},{9,8},{10,11... | collective-permute-start | bytes 1032200 | tf_op jit(solution)/shard_map/ppermute | solution.py:74
  104.0 8.3 %collective-permute-start.9 = (bf16[24,7168]{1,0:T(8,128)(2,1)}, bf16[24,7168]{1,0:T(8,128)(2,1)S(1)}, u32[]{:S(2)}, u32[]{:S(2)}) collective-permute-start(bf16[24,7168]{1,0:T(8,128)(2,1)} %get-tuple-element.11), channel_id=1, source_target_pairs={{0,1},{1,0},{2,3},{3,2},{4,5},{5,4},{6,7},{7,6},{8,9},{9,8},{10,11... | collective-permute-start | bytes 1032200 | tf_op jit(solution)/shard_map/ppermute | solution.py:74
  107.7 9.9 %collective-permute-start.8 = (bf16[24,7168]{1,0:T(8,128)(2,1)}, bf16[24,7168]{1,0:T(8,128)(2,1)}, u32[]{:S(2)}, u32[]{:S(2)}) collective-permute-start(bf16[24,7168]{1,0:T(8,128)(2,1)} %fusion.68), channel_id=1, source_target_pairs={{0,2},{1,3},{2,4},{3,5},{4,6},{5,7},{6,0},{7,1},{8,10},{9,11},{10,... | collective-permute-start | bytes 1032200 | tf_op jit(solution)/shard_map/ppermute | solution.py:80
  110.5 13.4 %collective-permute-start.14 = (bf16[1,3,2,128,512]{3,4,2,1,0:T(8,128)(2,1)}, bf16[1,3,2,128,512]{3,4,2,1,0:T(8,128)(2,1)}, u32[]{:S(2)}, u32[]{:S(2)}) collective-permute-start(bf16[1,3,2,128,512]{3,4,2,1,0:T(8,128)(2,1)} %bitcast.145), channel_id=1, source_target_pairs={{0,8},{8,16},{16,24},{24,0},{1,9},{9,17},{17,25},{25,1},{2,10},{10... | collective-permute-start | bytes 2359304 | tf_op jit(solution)/shard_map/ppermute | solution.py:20
  112.3 12.7 %collective-permute-start.11 = (bf16[24,7168]{1,0:T(8,128)(2,1)}, bf16[24,7168]{1,0:T(8,128)(2,1)}, u32[]{:S(2)}, u32[]{:S(2)}) collective-permute-start(bf16[24,7168]{1,0:T(8,128)(2,1)} %get-tuple-element.12), channel_id=1, source_target_pairs={{0,1},{1,0},{2,3},{3,2},{4,5},{5,4},{6,7},{7,6},{8,9},{9,8},{10,11... | collective-permute-start | bytes 1032200 | tf_op jit(solution)/shard_map/ppermute | solution.py:74
  119.7 9.4 %collective-permute-start.10 = (bf16[24,7168]{1,0:T(8,128)(2,1)}, bf16[24,7168]{1,0:T(8,128)(2,1)}, u32[]{:S(2)}, u32[]{:S(2)}) collective-permute-start(bf16[24,7168]{1,0:T(8,128)(2,1)} %fusion.66), channel_id=1, source_target_pairs={{0,2},{1,3},{2,4},{3,5},{4,6},{5,7},{6,0},{7,1},{8,10},{9,11},{10,... | collective-permute-start | bytes 1032200 | tf_op jit(solution)/shard_map/ppermute | solution.py:80
  123.9 16.8 %collective-permute-start.15 = (bf16[1,3,2,128,512]{3,4,2,1,0:T(8,128)(2,1)}, bf16[1,3,2,128,512]{3,4,2,1,0:T(8,128)(2,1)}, u32[]{:S(2)}, u32[]{:S(2)}) collective-permute-start(bf16[1,3,2,128,512]{3,4,2,1,0:T(8,128)(2,1)} %bitcast.31), channel_id=1, source_target_pairs={{0,16},{8,24},{16,0},{24,8},{1,17},{9,25},{17,1},{25,9},{2,18},{10... | collective-permute-start | bytes 2359304 | tf_op jit(solution)/shard_map/ppermute | solution.py:20
  125.0 15.7 %collective-permute-start.13 = (bf16[24,7168]{1,0:T(8,128)(2,1)}, bf16[24,7168]{1,0:T(8,128)(2,1)}, u32[]{:S(2)}, u32[]{:S(2)}) collective-permute-start(bf16[24,7168]{1,0:T(8,128)(2,1)} %get-tuple-element.13), channel_id=1, source_target_pairs={{0,1},{1,0},{2,3},{3,2},{4,5},{5,4},{6,7},{7,6},{8,9},{9,8},{10,11... | collective-permute-start | bytes 1032200 | tf_op jit(solution)/shard_map/ppermute | solution.py:74
  130.4 10.3 %collective-permute-start.12 = (bf16[24,7168]{1,0:T(8,128)(2,1)S(1)}, bf16[24,7168]{1,0:T(8,128)(2,1)}, u32[]{:S(2)}, u32[]{:S(2)}) collective-permute-start(bf16[24,7168]{1,0:T(8,128)(2,1)S(1)} %fusion.63), channel_id=1, source_target_pairs={{0,2},{1,3},{2,4},{3,5},{4,6},{5,7},{6,0},{7,1},{8,10},{9,11},{10,... | collective-permute-start | bytes 1032200 | tf_op jit(solution)/shard_map/ppermute | solution.py:80
  132.9 1.2 copy-start.1
  136.8 3.9 %copy-start = (bf16[24,7168]{1,0:T(8,128)(2,1)S(1)}, bf16[24,7168]{1,0:T(8,128)(2,1)}, u32[]{:S(2)}) copy-start(bf16[24,7168]{1,0:T(8,128)(2,1)} %param.10) | copy-start | bytes 1032196
  136.8 3.9 %copy-start.4 = (f32[7168]{0:T(1024)S(1)}, f32[7168]{0:T(1024)}, u32[]{:S(2)}) copy-start(f32[7168]{0:T(1024)} %param.16) | copy-start | bytes 86020
  140.7 9.5 %collective-permute-start.16 = (bf16[1,3,2,128,512]{3,4,2,1,0:T(8,128)(2,1)S(1)}, bf16[1,3,2,128,512]{3,4,2,1,0:T(8,128)(2,1)S(1)}, u32[]{:S(2)}, u32[]{:S(2)}) collective-permute-start(bf16[1,3,2,128,512]{3,4,2,1,0:T(8,128)(2,1)S(1)} %bitcast.144), channel_id=1, source_target_pairs={{0,24},{8,0},{16,8},{24,16},{1,25},{9,1},{17,9},{25,17},{2,26},{10... | collective-permute-start | bytes 2359304 | tf_op jit(solution)/shard_map/ppermute | solution.py:20

commit v6 on v5

--- a/solution.py
+++ b/solution.py
@@ -103,8 +103,8 @@
 def scatter_tokens(partial, rider):
     tensor_count = lax.axis_size("tensor")
     rows = tensor_count // 2
-    blocks = partial.reshape((2, rows, -1) + partial.shape[1:])
-    sent = blocks[1].astype(jnp.bfloat16)
+    kept = partial[0].reshape((rows, -1) + partial[0].shape[1:])
+    sent = partial[1].astype(jnp.bfloat16).reshape((rows, -1) + partial[1].shape[1:])
     mine = [None] * rows
     previous = None
     for s in [(s + 1) % rows for s in range(rows)]:
@@ -112,7 +112,7 @@
         if previous is not None and CHAIN_PARTNER:
             piece, previous = lax.optimization_barrier((piece, previous))
         previous = partner(piece)
-        mine[s] = blocks[0, s] + previous.astype(jnp.float32)
+        mine[s] = kept[s] + previous.astype(jnp.float32)
     carried = mine[1 % rows]
     for k in range(1, rows):
         if k == RELAY_STEP:
@@ -185,8 +185,13 @@
     )
     context = context.astype(jnp.bfloat16).reshape(group_tokens, head_count * HD)
     decode_side_cache = receive_decode(outgoing)
+    half = context.shape[0] // 2
     summed, decode_side_cache = scatter_tokens(
-        jnp.dot(context, out_weight, preferred_element_type=jnp.float32), decode_side_cache
+        [
+            jnp.dot(context[:half], out_weight, preferred_element_type=jnp.float32),
+            jnp.dot(context[half:], out_weight, preferred_element_type=jnp.bfloat16),
+        ],
+        decode_side_cache,
     )
     mixed = (hidden + summed + out_bias).astype(jnp.bfloat16)
     return (mixed, decode_side_cache)

time: 153 us -> 149 us (0.974)
    dot_general x1 -> x2, matrix products: 4.01 us -> 2.72 us  [the longest x1 1.36 us: local(): jnp.dot(context[half:], out_weight, preferred_element_type=jnp.bfloat16)]
    unnamed x25 -> x28, local copies, waits for them, and re-layouts: 13.3 us -> 13.1 us
  transfers between devices with their start and end apart: 18 -> 18, of which waited for: 11 -> 11; matrix products, arithmetic and copies ran while one was open for 40% -> 41% of each run, Pallas kernels for 0% -> 0%
where the time goes in v6:
time: 149 us; the launch traced here: 148 us
  waiting for transfers between devices  51.2 us (34%)
  local copies, waits for them, and re-layouts  36.6 us (25%)
  matrix products  24.8 us (17%)
  starting transfers between devices  20.6 us (14%)
  other arithmetic  13.5 us (9%)
    ppermute x8, waiting for transfers between devices, partner(): return lax.ppermute(x, 'tensor', [(j, j ^ 1) for j in range(tensor_count)])  27.7 us
    ppermute x6, waiting for transfers between devices, ring(): lax.ppermute(x, 'tensor', [(j, (j // 2 + 1) % rows * 2 + j % 2) for j in...  16 us
    dot_general x1, matrix products, local(): jnp.dot(gathered, qkv_weight, preferred_element_type=jnp.float32) + qkv_bias  13.3 us
    unnamed x28, local copies, waits for them, and re-layouts  13.1 us
    ppermute x8, starting transfers between devices, partner(): return lax.ppermute(x, 'tensor', [(j, j ^ 1) for j in range(tensor_count)])  10.3 us
    dot_general x4, matrix products, send_decode(): jnp.einsum('gud,gohdtc->guothc', placement_index, per_head_rows, preferre...  6.77 us
    ppermute x3, waiting for transfers between devices, shifted(): return lax.ppermute(x, axis, [(j, (j + k) % n) for j in range(n)])  5.49 us
    all_to_all x1, starting transfers between devices, local(): lax.all_to_all(split, 'tensor', split_axis=3, concat_axis=3, tiled=True)  5.29 us
  transfers between devices with their start and end apart: 18, of which 11 were waited for; matrix products, arithmetic and copies ran while one was open for 41% of the time, Pallas kernels for 0%

profile of v6, /device:TPU:0, one launch (start us, length us, event | category | flops | bytes accessed | tf_op | source)
XLA Modules:
  0.0 147.7 jit_solution(5265712922754977024)
XLA Ops:
  0.6 1.2 convert_reduce_fusion
  1.8 1.2 fusion.53
  3.1 1.9 %constant_dynamic-update-slice_fusion.7 = (bf16[192,7168]{1,0:T(8,128)(2,1)}, bf16[24,7168]{1,0:T(8,128)(2,1)S(1)}) fusion(f32[7168]{0:T(1024)} %param.12, f32[7168]{0:T(1024)} %param.11, f32[24]{0:T(128)S(1)} %add_rsqrt_fusion, f32[24]{0:T(128)S(1)} %broadcast_multiply_fusion, bf16[24,7168]{1,0:T(8,128)(2,1)} %param.10), kind=kLoop, calls=%fused_computation.77 | loop fusion | flops 1032191 | bytes 1089728
  5.0 3.0 %collective-permute-start = (bf16[24,7168]{1,0:T(8,128)(2,1)S(1)}, bf16[24,7168]{1,0:T(8,128)(2,1)S(1)}, u32[]{:S(2)}, u32[]{:S(2)}) collective-permute-start(bf16[24,7168]{1,0:T(8,128)(2,1)S(1)} %get-tuple-element.17), channel_id=1, source_target_pairs={{0,2},{1,3},{2,4},{3,5},{4,6},{5,7},{6,0},{7,1},{8,10},{9,11},{10,... | collective-permute-start | bytes 1032200 | tf_op jit(solution)/shard_map/ppermute | solution.py:80
  8.0 1.5 %collective-permute-start.3 = (bf16[24,7168]{1,0:T(8,128)(2,1)S(1)}, bf16[24,7168]{1,0:T(8,128)(2,1)S(1)}, u32[]{:S(2)}, u32[]{:S(2)}) collective-permute-start(bf16[24,7168]{1,0:T(8,128)(2,1)S(1)} %get-tuple-element.17), channel_id=1, source_target_pairs={{0,1},{1,0},{2,3},{3,2},{4,5},{5,4},{6,7},{7,6},{8,9},{9,8},{10,11... | collective-permute-start | bytes 1032200 | tf_op jit(solution)/shard_map/ppermute | solution.py:74
  9.8 1.2 slice.71
  11.0 2.0 %gather_fusion = s32[192]{0:T(256)S(1)} fusion(s32[192]{0:T(256)} %param.17, s32[1024]{0:T(1024)S(1)} %pad_clamp_fusion), kind=kCustom, calls=%fused_computation | custom fusion | bytes 2304 | tf_op jit(solution)/shard_map/gather | solution.py:152
  14.0 3.1 %copy.52 = bf16[1,1,2,128,4096]{3,4,2,1,0:T(8,128)(2,1)S(1)} copy(bf16[1,1,2,128,4096]{4,3,2,1,0:T(8,128)(2,1)} %param.18) | data formatting | bytes 4194304 | tf_op args[8]
  20.4 8.8 %collective-permute-done.1 = bf16[24,7168]{1,0:T(8,128)(2,1)S(1)} collective-permute-done((bf16[24,7168]{1,0:T(8,128)(2,1)S(1)}, bf16[24,7168]{1,0:T(8,128)(2,1)S(1)}, u32[]{:S(2)}, u32[]{:S(2)}) %collective-permute-start.1) | collective-permute-done | bytes 344096 | tf_op jit(solution)/shard_map/ppermute | solution.py:80
  29.2 1.3 collective-permute-start.5
  31.2 2.6 %copy.53 = bf16[1,2,4,8,128,128]{5,4,2,1,0,3:T(8,128)(2,1)} copy(bf16[1,2,4,8,128,128]{4,5,2,3,1,0:T(8,128)(2,1)S(1)} %bitcast.110) | data formatting | bytes 4194304 | tf_op jit(solution)/shard_map/optimization_barrier | solution.py:94
  33.8 5.3 %all-to-all-start = ((bf16[1,2,4,8,128,128]{5,4,2,1,0,3:T(8,128)(2,1)}), bf16[1,2,4,8,128,128]{5,4,2,1,0,3:T(8,128)(2,1)S(1)}, u32[]{:S(2)}, u32[]{:S(2)}) async-start(bf16[1,2,4,8,128,128]{5,4,2,1,0,3:T(8,128)(2,1)} %copy.53), calls=%async_computation | async-start | bytes 4194304 | tf_op jit(solution)/shard_map/all_to_all | solution.py:144
  39.4 1.8 %collective-permute-start.6 = (bf16[24,7168]{1,0:T(8,128)(2,1)}, bf16[24,7168]{1,0:T(8,128)(2,1)S(1)}, u32[]{:S(2)}, u32[]{:S(2)}) collective-permute-start(bf16[24,7168]{1,0:T(8,128)(2,1)} %collective-permute-done.2), channel_id=1, source_target_pairs={{0,1},{1,0},{2,3},{3,2},{4,5},{5,4},{6,7},{7,6},{8,9},{9,8},{10,11... | collective-permute-start | bytes 1032200 | tf_op jit(solution)/shard_map/ppermute | solution.py:74
  41.2 1.8 %constant_dynamic-update-slice_fusion.4 = bf16[192,7168]{1,0:T(8,128)(2,1)} fusion(bf16[192,7168]{1,0:T(8,128)(2,1)} %constant_dynamic-update-slice_fusion.5, bf16[24,7168]{1,0:T(8,128)(2,1)} %collective-permute-done.2), kind=kLoop, calls=%fused_computation.74 | loop fusion | bytes 688128
  43.7 1.7 %constant_dynamic-update-slice_fusion.2 = bf16[192,7168]{1,0:T(8,128)(2,1)} fusion(bf16[192,7168]{1,0:T(8,128)(2,1)} %constant_dynamic-update-slice_fusion.3, bf16[24,7168]{1,0:T(8,128)(2,1)} %collective-permute-done.4), kind=kLoop, calls=%fused_computation.72 | loop fusion | bytes 688128
  45.4 1.7 %constant_dynamic-update-slice_fusion.1 = bf16[192,7168]{1,0:T(8,128)(2,1)} fusion(bf16[192,7168]{1,0:T(8,128)(2,1)} %constant_dynamic-update-slice_fusion.2, bf16[24,7168]{1,0:T(8,128)(2,1)} %collective-permute-done.5), kind=kLoop, calls=%fused_computation.71 | loop fusion | bytes 688128
  47.2 18.8 %collective-permute-done.6 = bf16[24,7168]{1,0:T(8,128)(2,1)S(1)} collective-permute-done((bf16[24,7168]{1,0:T(8,128)(2,1)}, bf16[24,7168]{1,0:T(8,128)(2,1)S(1)}, u32[]{:S(2)}, u32[]{:S(2)}) %collective-permute-start.6) | collective-permute-done | bytes 344096 | tf_op jit(solution)/shard_map/ppermute | solution.py:74
  66.8 13.3 %fusion.2 = bf16[192,1536]{1,0:T(8,128)(2,1)} fusion(bf16[192,7168]{1,0:T(8,128)(2,1)} %constant_dynamic-update-slice_fusion, bf16[7168,1536]{1,0:T(8,128)(2,1)} %param.13, f32[1536]{0:T(1024)S(1)} %copy-done.7), kind=kOutput, calls=%fused_computation.7 | convolution fusion | flops 4228448256 | bytes 25368576 | tf_op jit(solution)/shard_map/dot_general | solution.py:147
  80.1 1.4 reshape.417
  83.5 2.0 %all-to-all-done = bf16[1,2,4,8,128,128]{5,4,2,1,0,3:T(8,128)(2,1)S(1)} async-done(((bf16[1,2,4,8,128,128]{5,4,2,1,0,3:T(8,128)(2,1)}), bf16[1,2,4,8,128,128]{5,4,2,1,0,3:T(8,128)(2,1)S(1)}, u32[]{:S(2)}, u32[]{:S(2)}) %all-to-all-start) | async-done | bytes 2097184 | tf_op jit(solution)/shard_map/all_to_all | solution.py:144
  90.5 1.4 fusion.67
  91.9 1.0 fusion.94
  92.9 1.2 collective-permute-start.7
  94.1 1.4 fusion.70
  95.5 5.9 %collective-permute-done.7 = bf16[24,7168]{1,0:T(8,128)(2,1)S(1)} collective-permute-done((bf16[24,7168]{1,0:T(8,128)(2,1)S(1)}, bf16[24,7168]{1,0:T(8,128)(2,1)S(1)}, u32[]{:S(2)}, u32[]{:S(2)}) %collective-permute-start.7) | collective-permute-done | bytes 344096 | tf_op jit(solution)/shard_map/ppermute | solution.py:74
  101.4 1.7 %collective-permute-start.9 = (bf16[24,7168]{1,0:T(8,128)(2,1)}, bf16[24,7168]{1,0:T(8,128)(2,1)S(1)}, u32[]{:S(2)}, u32[]{:S(2)}) collective-permute-start(bf16[24,7168]{1,0:T(8,128)(2,1)} %get-tuple-element.11), channel_id=1, source_target_pairs={{0,1},{1,0},{2,3},{3,2},{4,5},{5,4},{6,7},{7,6},{8,9},{9,8},{10,11... | collective-permute-start | bytes 1032200 | tf_op jit(solution)/shard_map/ppermute | solution.py:74
  104.0 1.5 fusion.31
  105.4 1.3 copy.64
  106.8 2.9 %collective-permute-done.9 = bf16[24,7168]{1,0:T(8,128)(2,1)S(1)} collective-permute-done((bf16[24,7168]{1,0:T(8,128)(2,1)}, bf16[24,7168]{1,0:T(8,128)(2,1)S(1)}, u32[]{:S(2)}, u32[]{:S(2)}) %collective-permute-start.9) | collective-permute-done | bytes 344096 | tf_op jit(solution)/shard_map/ppermute | solution.py:74
  109.7 1.7 %collective-permute-start.11 = (bf16[24,7168]{1,0:T(8,128)(2,1)}, bf16[24,7168]{1,0:T(8,128)(2,1)}, u32[]{:S(2)}, u32[]{:S(2)}) collective-permute-start(bf16[24,7168]{1,0:T(8,128)(2,1)} %get-tuple-element.12), channel_id=1, source_target_pairs={{0,1},{1,0},{2,3},{3,2},{4,5},{5,4},{6,7},{7,6},{8,9},{9,8},{10,11... | collective-permute-start | bytes 1032200 | tf_op jit(solution)/shard_map/ppermute | solution.py:74
  111.4 2.5 %collective-permute-done.8 = bf16[24,7168]{1,0:T(8,128)(2,1)} collective-permute-done((bf16[24,7168]{1,0:T(8,128)(2,1)}, bf16[24,7168]{1,0:T(8,128)(2,1)}, u32[]{:S(2)}, u32[]{:S(2)}) %collective-permute-start.8) | collective-permute-done | bytes 344096 | tf_op jit(solution)/shard_map/ppermute | solution.py:80
  113.9 2.0 %fusion.63 = bf16[24,7168]{1,0:T(8,128)(2,1)} fusion(f32[96,7168]{1,0:T(8,128)} %copy-done, bf16[24,7168]{1,0:T(8,128)(2,1)S(1)} %collective-permute-done.9, bf16[24,7168]{1,0:T(8,128)(2,1)} %collective-permute-done.8), kind=kLoop, calls=%fused_computation.53 | loop fusion | flops 860160 | bytes 1720320 | tf_op jit(solution)/shard_map/convert_element_type | solution.py:120
  115.9 1.4 fusion.28
  117.3 1.4 copy.66
  118.7 1.4 fusion.34
  120.2 1.1 collective-permute-start.15
  121.6 3.7 %collective-permute-done.10 = bf16[24,7168]{1,0:T(8,128)(2,1)} collective-permute-done((bf16[24,7168]{1,0:T(8,128)(2,1)}, bf16[24,7168]{1,0:T(8,128)(2,1)}, u32[]{:S(2)}, u32[]{:S(2)}) %collective-permute-start.10) | collective-permute-done | bytes 344096 | tf_op jit(solution)/shard_map/ppermute | solution.py:80
  125.3 1.4 fusion.61
  126.7 2.4 %fusion.25 = bf16[1,3,2,128,4,128]{5,1,3,4,2,0:T(4,128)(2,1)} fusion(bf16[1,2,4,8,128,128]{5,4,2,1,0,3:T(8,128)(2,1)S(1)} %all-to-all-done, s32[8]{0:T(128)S(1)} %multiply_add_fusion, s32[3]{0:T(128)S(1)} %iota_add_fusion.1), kind=kOutput, calls=%fused_computation.22 | convolution fusion | flops 6684696 | bytes 2883628 | tf_op jit(solution)/shard_map/gud,gohdtc->guothc/dot_general | solution.py:47
  131.1 2.0 %broadcast_in_dim.22 = bf16[1,12,2,128,512]{4,3,2,1,0:T(8,128)(2,1)} broadcast(bf16[]{:T(256)} %constant.111.clone.1), dimensions={} | broadcast | bytes 3145730 | tf_op jit(solution)/shard_map/broadcast_in_dim | solution.py:58
  133.1 0.9 constant_dynamic-update-slice_fusion.11
  134.0 1.4 copy.65
  135.4 1.0 constant_dynamic-update-slice_fusion.10
  137.0 2.2 %fusion.58 = bf16[24,7168]{1,0:T(8,128)(2,1)} fusion(bf16[24,7168]{1,0:T(8,128)(2,1)S(1)} %copy-done.1, f32[96,7168]{1,0:T(8,128)} %copy-done, bf16[24,7168]{1,0:T(8,128)(2,1)} %collective-permute-done.13, bf16[24,7168]{1,0:T(8,128)(2,1)} %collective-permute-done.12, f32[7168]{0:T(1024)S(1)} %copy-done.5), kind=kLoop, calls=%fused_computation.45 | loop fusion | flops 1376256 | bytes 2093056 | tf_op jit(solution)/shard_map/convert_element_type | solution.py:196
  139.2 1.4 copy.67
  140.6 0.9 constant_dynamic-update-slice_fusion.9
  141.5 4.9 %collective-permute-done.16 = bf16[1,3,2,128,512]{3,4,2,1,0:T(8,128)(2,1)S(1)} collective-permute-done((bf16[1,3,2,128,512]{3,4,2,1,0:T(8,128)(2,1)S(1)}, bf16[1,3,2,128,512]{3,4,2,1,0:T(8,128)(2,1)S(1)}, u32[]{:S(2)}, u32[]{:S(2)}) %collective-permute-start.16) | collective-permute-done | bytes 786464 | tf_op jit(solution)/shard_map/ppermute | solution.py:20
  146.7 0.9 constant_dynamic-update-slice_fusion.8
  (80 shorter events, 17.9 us)
Async XLA Ops:
  0.6 12.4 %copy-start.6 = (s32[1,8,1]{1,2,0:T(1,128)S(1)}, s32[1,8,1]{1,2,0:T(1,128)}, u32[]{:S(2)}) copy-start(s32[1,8,1]{1,2,0:T(1,128)} %param.19) | copy-start | bytes 100
  5.0 13.1 %collective-permute-start = (bf16[24,7168]{1,0:T(8,128)(2,1)S(1)}, bf16[24,7168]{1,0:T(8,128)(2,1)S(1)}, u32[]{:S(2)}, u32[]{:S(2)}) collective-permute-start(bf16[24,7168]{1,0:T(8,128)(2,1)S(1)} %get-tuple-element.17), channel_id=1, source_target_pairs={{0,2},{1,3},{2,4},{3,5},{4,6},{5,7},{6,0},{7,1},{8,10},{9,11},{10,... | collective-permute-start | bytes 1032200 | tf_op jit(solution)/shard_map/ppermute | solution.py:80
  8.0 34.9 %collective-permute-start.3 = (bf16[24,7168]{1,0:T(8,128)(2,1)S(1)}, bf16[24,7168]{1,0:T(8,128)(2,1)S(1)}, u32[]{:S(2)}, u32[]{:S(2)}) collective-permute-start(bf16[24,7168]{1,0:T(8,128)(2,1)S(1)} %get-tuple-element.17), channel_id=1, source_target_pairs={{0,1},{1,0},{2,3},{3,2},{4,5},{5,4},{6,7},{7,6},{8,9},{9,8},{10,11... | collective-permute-start | bytes 1032200 | tf_op jit(solution)/shard_map/ppermute | solution.py:74
  18.1 11.0 %collective-permute-start.1 = (bf16[24,7168]{1,0:T(8,128)(2,1)S(1)}, bf16[24,7168]{1,0:T(8,128)(2,1)S(1)}, u32[]{:S(2)}, u32[]{:S(2)}) collective-permute-start(bf16[24,7168]{1,0:T(8,128)(2,1)S(1)} %collective-permute-done), channel_id=1, source_target_pairs={{0,2},{1,3},{2,4},{3,5},{4,6},{5,7},{6,0},{7,1},{8,10},{9,11},{10,... | collective-permute-start | bytes 1032200 | tf_op jit(solution)/shard_map/ppermute | solution.py:80
  18.9 24.8 %collective-permute-start.4 = (bf16[24,7168]{1,0:T(8,128)(2,1)S(1)}, bf16[24,7168]{1,0:T(8,128)(2,1)}, u32[]{:S(2)}, u32[]{:S(2)}) collective-permute-start(bf16[24,7168]{1,0:T(8,128)(2,1)S(1)} %collective-permute-done), channel_id=1, source_target_pairs={{0,1},{1,0},{2,3},{3,2},{4,5},{5,4},{6,7},{7,6},{8,9},{9,8},{10,11... | collective-permute-start | bytes 1032200 | tf_op jit(solution)/shard_map/ppermute | solution.py:74
  29.2 10.2 %collective-permute-start.2 = (bf16[24,7168]{1,0:T(8,128)(2,1)S(1)}, bf16[24,7168]{1,0:T(8,128)(2,1)}, u32[]{:S(2)}, u32[]{:S(2)}) collective-permute-start(bf16[24,7168]{1,0:T(8,128)(2,1)S(1)} %collective-permute-done.1), channel_id=1, source_target_pairs={{0,2},{1,3},{2,4},{3,5},{4,6},{5,7},{6,0},{7,1},{8,10},{9,11},{10,... | collective-permute-start | bytes 1032200 | tf_op jit(solution)/shard_map/ppermute | solution.py:80
  29.2 16.3 %collective-permute-start.5 = (bf16[24,7168]{1,0:T(8,128)(2,1)S(1)}, bf16[24,7168]{1,0:T(8,128)(2,1)}, u32[]{:S(2)}, u32[]{:S(2)}) collective-permute-start(bf16[24,7168]{1,0:T(8,128)(2,1)S(1)} %collective-permute-done.1), channel_id=1, source_target_pairs={{0,1},{1,0},{2,3},{3,2},{4,5},{5,4},{6,7},{7,6},{8,9},{9,8},{10,11... | collective-permute-start | bytes 1032200 | tf_op jit(solution)/shard_map/ppermute | solution.py:74
  33.8 51.7 %all-to-all-start = ((bf16[1,2,4,8,128,128]{5,4,2,1,0,3:T(8,128)(2,1)}), bf16[1,2,4,8,128,128]{5,4,2,1,0,3:T(8,128)(2,1)S(1)}, u32[]{:S(2)}, u32[]{:S(2)}) async-start(bf16[1,2,4,8,128,128]{5,4,2,1,0,3:T(8,128)(2,1)} %copy.53), calls=%async_computation | async-start | bytes 4194304 | tf_op jit(solution)/shard_map/all_to_all | solution.py:144
  39.1 27.7 %copy-start.7 = (f32[1536]{0:T(1024)S(1)}, f32[1536]{0:T(1024)}, u32[]{:S(2)}) copy-start(f32[1536]{0:T(1024)} %param.14) | copy-start | bytes 18436
  39.4 26.6 %collective-permute-start.6 = (bf16[24,7168]{1,0:T(8,128)(2,1)}, bf16[24,7168]{1,0:T(8,128)(2,1)S(1)}, u32[]{:S(2)}, u32[]{:S(2)}) collective-permute-start(bf16[24,7168]{1,0:T(8,128)(2,1)} %collective-permute-done.2), channel_id=1, source_target_pairs={{0,1},{1,0},{2,3},{3,2},{4,5},{5,4},{6,7},{7,6},{8,9},{9,8},{10,11... | collective-permute-start | bytes 1032200 | tf_op jit(solution)/shard_map/ppermute | solution.py:74
  82.3 0.7 copy-start.3
  85.5 1.0 copy-start.4
  87.2 2.6 %slice-start = ((s8[7340032]{0:T(1024)(128)(4,1)}), s8[3145728]{0:T(1024)(128)(4,1)S(1)}, s32[]{:S(2)}) async-start(s8[7340032]{0:T(1024)(128)(4,1)} %bitcast.108), calls=%async_computation.1 | async-start | bytes 6291456
  87.9 2.6 %slice-start.1 = ((s8[7340032]{0:T(1024)(128)(4,1)}), s8[4194304]{0:T(1024)(128)(4,1)S(1)}, s32[]{:S(2)}) async-start(s8[7340032]{0:T(1024)(128)(4,1)} %bitcast.108), calls=%async_computation.2 | async-start | bytes 8388608
  92.9 8.5 %collective-permute-start.7 = (bf16[24,7168]{1,0:T(8,128)(2,1)S(1)}, bf16[24,7168]{1,0:T(8,128)(2,1)S(1)}, u32[]{:S(2)}, u32[]{:S(2)}) collective-permute-start(bf16[24,7168]{1,0:T(8,128)(2,1)S(1)} %get-tuple-element.20), channel_id=1, source_target_pairs={{0,1},{1,0},{2,3},{3,2},{4,5},{5,4},{6,7},{7,6},{8,9},{9,8},{10,11... | collective-permute-start | bytes 1032200 | tf_op jit(solution)/shard_map/ppermute | solution.py:74
  95.5 7.7 %copy-start = (f32[96,7168]{1,0:T(8,128)}, f32[96,7168]{1,0:T(8,128)S(1)}, u32[]{:S(2)}) copy-start(f32[96,7168]{1,0:T(8,128)S(1)} %fusion.70) | copy-start | bytes 8257540
  101.4 8.3 %collective-permute-start.9 = (bf16[24,7168]{1,0:T(8,128)(2,1)}, bf16[24,7168]{1,0:T(8,128)(2,1)S(1)}, u32[]{:S(2)}, u32[]{:S(2)}) collective-permute-start(bf16[24,7168]{1,0:T(8,128)(2,1)} %get-tuple-element.11), channel_id=1, source_target_pairs={{0,1},{1,0},{2,3},{3,2},{4,5},{5,4},{6,7},{7,6},{8,9},{9,8},{10,11... | collective-permute-start | bytes 1032200 | tf_op jit(solution)/shard_map/ppermute | solution.py:74
  103.9 9.9 %collective-permute-start.8 = (bf16[24,7168]{1,0:T(8,128)(2,1)}, bf16[24,7168]{1,0:T(8,128)(2,1)}, u32[]{:S(2)}, u32[]{:S(2)}) collective-permute-start(bf16[24,7168]{1,0:T(8,128)(2,1)} %fusion.64), channel_id=1, source_target_pairs={{0,2},{1,3},{2,4},{3,5},{4,6},{5,7},{6,0},{7,1},{8,10},{9,11},{10,... | collective-permute-start | bytes 1032200 | tf_op jit(solution)/shard_map/ppermute | solution.py:80
  106.8 13.4 %collective-permute-start.14 = (bf16[1,3,2,128,512]{3,4,2,1,0:T(8,128)(2,1)}, bf16[1,3,2,128,512]{3,4,2,1,0:T(8,128)(2,1)}, u32[]{:S(2)}, u32[]{:S(2)}) collective-permute-start(bf16[1,3,2,128,512]{3,4,2,1,0:T(8,128)(2,1)} %bitcast.115), channel_id=1, source_target_pairs={{0,8},{8,16},{16,24},{24,0},{1,9},{9,17},{17,25},{25,1},{2,10},{10... | collective-permute-start | bytes 2359304 | tf_op jit(solution)/shard_map/ppermute | solution.py:20
  109.7 11.6 %collective-permute-start.11 = (bf16[24,7168]{1,0:T(8,128)(2,1)}, bf16[24,7168]{1,0:T(8,128)(2,1)}, u32[]{:S(2)}, u32[]{:S(2)}) collective-permute-start(bf16[24,7168]{1,0:T(8,128)(2,1)} %get-tuple-element.12), channel_id=1, source_target_pairs={{0,1},{1,0},{2,3},{3,2},{4,5},{5,4},{6,7},{7,6},{8,9},{9,8},{10,11... | collective-permute-start | bytes 1032200 | tf_op jit(solution)/shard_map/ppermute | solution.py:74
  115.9 9.4 %collective-permute-start.10 = (bf16[24,7168]{1,0:T(8,128)(2,1)}, bf16[24,7168]{1,0:T(8,128)(2,1)}, u32[]{:S(2)}, u32[]{:S(2)}) collective-permute-start(bf16[24,7168]{1,0:T(8,128)(2,1)} %fusion.63), channel_id=1, source_target_pairs={{0,2},{1,3},{2,4},{3,5},{4,6},{5,7},{6,0},{7,1},{8,10},{9,11},{10,... | collective-permute-start | bytes 1032200 | tf_op jit(solution)/shard_map/ppermute | solution.py:80
  120.2 16.8 %collective-permute-start.15 = (bf16[1,3,2,128,512]{3,4,2,1,0:T(8,128)(2,1)}, bf16[1,3,2,128,512]{3,4,2,1,0:T(8,128)(2,1)}, u32[]{:S(2)}, u32[]{:S(2)}) collective-permute-start(bf16[1,3,2,128,512]{3,4,2,1,0:T(8,128)(2,1)} %bitcast.26), channel_id=1, source_target_pairs={{0,16},{8,24},{16,0},{24,8},{1,17},{9,25},{17,1},{25,9},{2,18},{10... | collective-permute-start | bytes 2359304 | tf_op jit(solution)/shard_map/ppermute | solution.py:20
  121.3 15.7 %collective-permute-start.13 = (bf16[24,7168]{1,0:T(8,128)(2,1)}, bf16[24,7168]{1,0:T(8,128)(2,1)}, u32[]{:S(2)}, u32[]{:S(2)}) collective-permute-start(bf16[24,7168]{1,0:T(8,128)(2,1)} %get-tuple-element.13), channel_id=1, source_target_pairs={{0,1},{1,0},{2,3},{3,2},{4,5},{5,4},{6,7},{7,6},{8,9},{9,8},{10,11... | collective-permute-start | bytes 1032200 | tf_op jit(solution)/shard_map/ppermute | solution.py:74
  126.6 10.3 %collective-permute-start.12 = (bf16[24,7168]{1,0:T(8,128)(2,1)S(1)}, bf16[24,7168]{1,0:T(8,128)(2,1)}, u32[]{:S(2)}, u32[]{:S(2)}) collective-permute-start(bf16[24,7168]{1,0:T(8,128)(2,1)S(1)} %fusion.61), channel_id=1, source_target_pairs={{0,2},{1,3},{2,4},{3,5},{4,6},{5,7},{6,0},{7,1},{8,10},{9,11},{10,... | collective-permute-start | bytes 1032200 | tf_op jit(solution)/shard_map/ppermute | solution.py:80
  129.1 1.2 copy-start.2
  133.1 3.9 %copy-start.1 = (bf16[24,7168]{1,0:T(8,128)(2,1)S(1)}, bf16[24,7168]{1,0:T(8,128)(2,1)}, u32[]{:S(2)}) copy-start(bf16[24,7168]{1,0:T(8,128)(2,1)} %param.10) | copy-start | bytes 1032196
  133.1 3.9 %copy-start.5 = (f32[7168]{0:T(1024)S(1)}, f32[7168]{0:T(1024)}, u32[]{:S(2)}) copy-start(f32[7168]{0:T(1024)} %param.16) | copy-start | bytes 86020
  136.9 9.5 %collective-permute-start.16 = (bf16[1,3,2,128,512]{3,4,2,1,0:T(8,128)(2,1)S(1)}, bf16[1,3,2,128,512]{3,4,2,1,0:T(8,128)(2,1)S(1)}, u32[]{:S(2)}, u32[]{:S(2)}) collective-permute-start(bf16[1,3,2,128,512]{3,4,2,1,0:T(8,128)(2,1)S(1)} %bitcast.114), channel_id=1, source_target_pairs={{0,24},{8,0},{16,8},{24,16},{1,25},{9,1},{17,9},{25,17},{2,26},{10... | collective-permute-start | bytes 2359304 | tf_op jit(solution)/shard_map/ppermute | solution.py:20
